TPU v7x, 512 devices: a whole 4x8x8 slice. The times are simulated.
512 devices in a mesh: owner: 16 (over x, y_hi), beam: 32 (over y_lo, z, core).
Axes of the slice: x: 4, y: 8 (y_hi: 4, y_lo: 2; y = y_hi * 2 + y_lo), z: 8, core: 2. Of those that a mesh axis runs over, the one named last changes fastest.
Arguments:
- hidden: bfloat16 [4096, 8192], P('owner'), may hold values from -6 to 6
- norm_gain: bfloat16 [8192], replicated, may hold values from 0.099609375 to 1.8984375
- w_qkv: bfloat16 [8192, 10240], P('owner', 'beam'), may hold values from -0.0625 to 0.0625
- w_out: bfloat16 [8192, 8192], P('beam', 'owner'), may hold values from -0.125 to 0.125
- kv_cache: bfloat16 [16384, 2, 8, 1024], P(('owner', 'beam')), may hold values from -384 to 384
- lengths: int32 [4096], P('owner'), may hold values from 1 to 32, 98304 in all
- kept_parent_device: int32 [16384, 1], P('owner'), may hold values from 0 to 31; in each aligned block of 32 rows (0 to 31, 32 to 63, ...) at most 2 rows name the same one
- keep_block: int32 [16384], P('owner'), may hold values from 0 to 31
Outputs:
- mixed: bfloat16 [4096, 8192], P('owner', 'beam')
Inputs may be any that keep to these rules, and one draw needn't show every extreme that they name: `kept_parent_device`: in each aligned block of 32 entries (the new blocks of one device) no value appears more than 2 times, and some value appears exactly 2 times in some block. `lengths`: each entry is at least 1; the largest is exactly 32.
All inputs are finite; a program needn't handle non-finite values. No bound on the sum of `lengths` on one device may be relied on, other than what follows from the above.
Results may differ from a plain program's by a relative error of at most 0.024.
Values may be sent and summed in bfloat16 or wider, within the bound.
No kernel may reach another device: no remote copies, remote signals or barrier semaphores. Data moves between devices by JAX's collectives and lax.ppermute only.
A program may use at most 64 MiB of HBM per device.

v0:
```python
import jax
import jax.numpy as jnp
from jax import lax
from jax.sharding import PartitionSpec as P

QH = 64
KVH = 8
HD = 128
CACHE = 32
PAGE = 8
QKV = 10240


def rotary_embed(values, positions):
    half = values.shape[-1] // 2
    freqs = 500000.0 ** (-(jnp.arange(half, dtype=jnp.float32) * 2.0) / values.shape[-1])
    angles = positions.astype(jnp.float32)[:, None] * freqs[None, :]
    cosine = jnp.cos(angles)[:, None, :]
    sine = jnp.sin(angles)[:, None, :]
    first = values[..., :half]
    second = values[..., half:]
    return jnp.concatenate(
        [first * cosine - second * sine, second * cosine + first * sine], axis=-1
    )


def regroup(blocks):
    return lax.all_to_all(blocks, "beam", split_axis=1, concat_axis=1, tiled=True)


def attend(queries, fresh_key, value_new, keys, values, positions):
    beams = queries.shape[0]
    grouped_heads = queries.reshape(beams, KVH, QH // KVH, HD)
    scale_factor = HD ** (-0.5)
    scores = (
        jnp.einsum("bkgd,btkd->bkgt", grouped_heads, keys, preferred_element_type=jnp.float32)
        * scale_factor
    )
    local_beam_score = (
        jnp.einsum("rhap,rhp->rha", grouped_heads, fresh_key, preferred_element_type=jnp.float32)
        * scale_factor
    )
    valid = (jnp.arange(keys.shape[1], dtype=jnp.int32)[None, :] < positions[:, None])[
        :, None, None, :
    ]
    scores = jnp.where(valid, scores, -1e30)
    highest = jnp.maximum(jnp.max(scores, axis=-1), local_beam_score)
    weights = jnp.where(valid, jnp.exp(scores - highest[..., None]), 0.0)
    own_weight = jnp.exp(local_beam_score - highest)
    totals = jnp.sum(weights, axis=-1) + own_weight
    probs = (weights / totals[..., None]).astype(jnp.bfloat16)
    own_prob = (own_weight / totals).astype(jnp.bfloat16)
    output = jnp.einsum("bkgt,btkd->bkgd", probs, values, preferred_element_type=jnp.float32)
    output = (
        output
        + own_prob.astype(jnp.float32)[..., None] * value_new.astype(jnp.float32)[:, :, None, :]
    )
    return output.reshape(beams, QH * HD).astype(jnp.bfloat16)


def shards(hidden, norm_gain, w_qkv, w_out, kv_cache, lengths, kept_parent_device, keep_block):
    columns = lax.axis_size("beam")
    my_column = lax.axis_index("beam")
    grouped_row_block = hidden.shape[0]
    own_beams = grouped_row_block // columns
    floats = hidden.astype(jnp.float32)
    scale_rms = lax.rsqrt(jnp.mean(floats * floats, axis=-1, keepdims=True) + 1e-05)
    normed = (floats * scale_rms * norm_gain.astype(jnp.float32)).astype(jnp.bfloat16)
    normed_split = normed.reshape(columns, own_beams, normed.shape[1])
    projected = jnp.einsum(
        "jbd,dc->bjc",
        normed_split,
        lax.all_gather(w_qkv, "owner", axis=0, tiled=True),
        preferred_element_type=jnp.float32,
    )
    own_qkv = regroup(projected.astype(jnp.bfloat16)).reshape(own_beams, QKV)
    blk_dev = kv_cache.shape[0]
    most_slots = max(2, 2 * blk_dev // columns)
    sources = kept_parent_device.reshape(columns, blk_dev)
    picked = keep_block.reshape(columns, blk_dev)
    is_mine = (sources == my_column).astype(jnp.int32)
    ranks = jnp.cumsum(is_mine, axis=1) - 1
    slot_ids = jnp.arange(most_slots, dtype=jnp.int32)
    chosen = is_mine[:, :, None] * (ranks[:, :, None] == slot_ids[None, None, :]).astype(jnp.int32)
    send_table = jnp.sum(chosen * picked[:, :, None], axis=1)
    outgoing = kv_cache[send_table.reshape(-1)].reshape((columns, most_slots) + kv_cache.shape[1:])
    incoming_blocks = lax.all_to_all(outgoing, "beam", split_axis=0, concat_axis=0, tiled=True)
    own_sources = lax.dynamic_index_in_dim(sources, my_column, 0, keepdims=False)
    one_hot = (own_sources[:, None] == jnp.arange(columns, dtype=jnp.int32)[None, :]).astype(
        jnp.int32
    )
    earlier = jnp.cumsum(one_hot, axis=0) - one_hot
    arrival = jnp.sum(earlier * one_hot, axis=1)
    flat_blocks = incoming_blocks.reshape((columns * most_slots,) + kv_cache.shape[1:])
    moved = flat_blocks[own_sources * most_slots + arrival]
    moved = moved.reshape(own_beams, CACHE // PAGE, 2, PAGE, KVH, HD)
    keys = moved[:, :, 0].reshape(own_beams, CACHE, KVH, HD)
    values = moved[:, :, 1].reshape(own_beams, CACHE, KVH, HD)
    positions = lax.dynamic_slice_in_dim(lengths, my_column * own_beams, own_beams)
    query_cols = own_qkv[:, : QH * HD].reshape(own_beams, QH, HD).astype(jnp.float32)
    key_cols = own_qkv[:, QH * HD : (QH + KVH) * HD].reshape(own_beams, KVH, HD).astype(jnp.float32)
    value_new = own_qkv[:, (QH + KVH) * HD :].reshape(own_beams, KVH, HD)
    queries = rotary_embed(query_cols, positions).astype(jnp.bfloat16)
    fresh_key = rotary_embed(key_cols, positions).astype(jnp.bfloat16)
    attn = attend(queries, fresh_key, value_new, keys, values, positions)
    head_rows = regroup(attn.reshape(own_beams, columns, attn.shape[1] // columns))
    w_piece = lax.all_gather(w_out, "owner", axis=1, tiled=True)
    terms = jnp.einsum(
        "bjh,hc->jbc", head_rows, w_piece, preferred_element_type=jnp.float32
    ).reshape(grouped_row_block, w_piece.shape[1])
    return lax.psum_scatter(terms.astype(jnp.bfloat16), "beam", scatter_dimension=1, tiled=True)


def solution(mesh):
    return jax.shard_map(
        shards,
        mesh=mesh,
        in_specs=(
            P("owner", None),
            P(),
            P("owner", "beam"),
            P("beam", "owner"),
            P(("owner", "beam"), None, None, None),
            P("owner"),
            P("owner", None),
            P("owner"),
        ),
        out_specs=P("owner", "beam"),
        check_vma=False,
    )
```

profile of v0, /device:TPU:56, one launch (start us, length us, event | category | flops | bytes accessed | tf_op | source)
XLA Modules:
  0.0 347.2 jit_solution(10896632046652622338)
XLA Ops:
  6.5 0.0 copy-start
  6.5 0.0 all-gather.3.cloned.1.call-start
  6.5 0.7 all-gather.3.cloned.1.call-update
  7.3 0.0 all-gather.5.cloned.1.call-start
  7.3 0.7 all-gather.5.cloned.1.call-update
  8.0 0.5 broadcast.155
  8.5 1.3 reduce.3
  9.9 0.1 reshape.206
  10.0 0.2 reduce_window_sum.22
  10.1 0.8 mul.193
  10.9 0.1 multiply_reduce_fusion
  11.0 0.1 copy.28
  11.1 0.1 reshape.207
  11.3 0.0 copy-done
  11.3 0.0 copy-start.1
  11.3 0.0 copy-start.2
  11.3 2.0 gather_fusion
  13.3 11.9 %all-to-all-start.1 = ((bf16[32,2,2,8,1024]{4,3,2,1,0:T(8,128)(2,1)}), bf16[32,2,2,8,1024]{4,3,2,1,0:T(8,128)(2,1)S(1)}, u32[]{:S(2)}, u32[]{:S(2)}) async-start(bf16[32,2,2,8,1024]{4,3,2,1,0:T(8,128)(2,1)} %bitcast.8), calls=%async_computation.1 | async-start | bytes 4194304 | tf_op jit(solution)/shard_map/all_to_all | solution.py:87
  25.2 0.0 copy-done.1
  25.3 0.1 fusion.41
  25.4 0.1 reduce_window_sum.23
  25.4 0.0 copy-done.2
  25.4 0.1 fusion.49
  25.5 0.2 select_reduce_fusion
  25.7 0.1 iota_compare_fusion.2
  25.8 3.1 fusion.1
  28.9 0.1 multiply_cosine_fusion
  29.0 87.4 %all-gather.3.cloned.1.call-done = bf16[8192,320]{0,1:T(8,128)(2,1)} async-done(((bf16[512,320]{0,1:T(8,128)(2,1)}), bf16[8192,320]{0,1:T(8,128)(2,1)}) %all-gather.3.cloned.1.call-update) | async-done | bytes 5242896 | tf_op jit(solution)/shard_map/all_gather | solution.py:73
  116.4 6.8 %fusion.18 = bf16[8,32,320]{2,0,1:T(8,128)(2,1)} fusion(bf16[8192,320]{0,1:T(8,128)(2,1)} %all-gather.3.cloned.1.call-done, bf16[256,8192]{1,0:T(8,128)(2,1)} %param.8, f32[8192]{0:T(1024)S(1)} %convert_element_type.85, f32[256]{0:T(256)S(1)} %add_rsqrt_fusion), kind=kOutput, calls=%fused_computation.21 | convolution fusion | flops 1350647808 | bytes 9634816 | tf_op jit(solution)/shard_map/jbd,dc->bjc/dot_general | solution.py:70
  123.2 0.0 all-to-all-done.1
  123.2 9.8 %all-to-all-start = ((bf16[8,32,320]{2,0,1:T(8,128)(2,1)}), bf16[8,32,320]{2,0,1:T(8,128)(2,1)S(1)}, u32[]{:S(2)}, u32[]{:S(2)}) async-start(bf16[8,32,320]{2,0,1:T(8,128)(2,1)} %fusion.18), calls=%async_computation | async-start | bytes 393216 | tf_op jit(solution)/shard_map/all_to_all | solution.py:28
  133.0 1.6 gather_fusion.1
  134.6 1.5 copy.39
  136.2 0.1 fusion.50
  136.3 6.7 %all-to-all-done = bf16[8,32,320]{2,0,1:T(8,128)(2,1)S(1)} async-done(((bf16[8,32,320]{2,0,1:T(8,128)(2,1)}), bf16[8,32,320]{2,0,1:T(8,128)(2,1)S(1)}, u32[]{:S(2)}, u32[]{:S(2)}) %all-to-all-start) | async-done | bytes 163872 | tf_op jit(solution)/shard_map/all_to_all | solution.py:28
  143.0 0.2 reshape.205
  143.3 0.1 subtract_convert_fusion.1
  143.4 0.1 maximum_bitcast_fusion
  143.5 0.1 fusion.51
  143.6 0.1 fusion.28
  143.7 0.3 fusion.36
  144.0 0.5 fusion.52
  144.5 0.3 fusion.27
  144.9 0.3 fusion.17
  145.2 0.7 copy.32
  146.0 4.2 %all-to-all-start.2 = ((bf16[8,32,256]{2,0,1:T(8,128)(2,1)}), bf16[8,32,256]{2,0,1:T(8,128)(2,1)S(1)}, u32[]{:S(2)}, u32[]{:S(2)}) async-start(bf16[8,32,256]{2,0,1:T(8,128)(2,1)} %copy.32), calls=%async_computation.2 | async-start | bytes 262144 | tf_op jit(solution)/shard_map/all_to_all | solution.py:28
  150.1 0.0 reduce-scatter.2.cloned.1.call-start
  150.2 54.7 %all-gather.5.cloned.1.call-done = bf16[256,8192]{1,0:T(8,128)(2,1)} async-done(((bf16[256,512]{1,0:T(8,128)(2,1)}), bf16[256,8192]{1,0:T(8,128)(2,1)}) %all-gather.5.cloned.1.call-update) | async-done | bytes 4194320 | tf_op jit(solution)/shard_map/all_gather | solution.py:107
  204.9 0.0 all-to-all-done.2
  204.9 3.4 fusion
  208.3 4.2 %copy.67 = bf16[32,8,8192]{2,1,0:T(8,128)(2,1)} copy(bf16[32,8,8192]{2,0,1:T(8,128)(2,1)S(1)} %fusion) | data formatting | bytes 8388608 | tf_op jit(solution)/shard_map/convert_element_type | solution.py:111
  212.6 0.0 reduce-scatter.2.cloned.1.call-update
  212.6 128.1 %reduce-scatter.2.cloned.1.call-done = bf16[256,256]{1,0:T(8,128)(2,1)} async-done(((bf16[256,8192]{1,0:T(8,128)(2,1)}), bf16[256,256]{1,0:T(8,128)(2,1)}) %reduce-scatter.2.cloned.1.call-update) | async-done | bytes 131088 | tf_op jit(solution)/shard_map/reduce_scatter | solution.py:111
  (17 shorter events, 0.2 us)
Async XLA Ops:
  6.5 4.7 %copy-start = (bf16[32,2,8,1024]{3,2,1,0:T(8,128)(2,1)S(1)}, bf16[32,2,8,1024]{3,2,1,0:T(8,128)(2,1)}, u32[]{:S(2)}) copy-start(bf16[32,2,8,1024]{3,2,1,0:T(8,128)(2,1)} %param.12) | copy-start | bytes 3145732
  6.5 109.9 %all-gather.3.cloned.1.call-start = ((), (), s32[]{:S(2)}) async-start(), calls=%async_computation.4 | async-start | bytes 5570560 | tf_op jit(solution)/shard_map/all_gather | solution.py:73
  7.3 197.6 %all-gather.5.cloned.1.call-start = ((), (), s32[]{:S(2)}) async-start(), calls=%async_computation.5 | async-start | bytes 4456448 | tf_op jit(solution)/shard_map/all_gather | solution.py:107
  11.3 14.0 %copy-start.1 = (bf16[8192]{0:T(1024)(128)(2,1)S(1)}, bf16[8192]{0:T(1024)(128)(2,1)}, u32[]{:S(2)}) copy-start(bf16[8192]{0:T(1024)(128)(2,1)} %param.9) | copy-start | bytes 49156
  11.3 14.2 %copy-start.2 = (s32[256]{0:T(256)S(1)}, s32[256]{0:T(256)}, u32[]{:S(2)}) copy-start(s32[256]{0:T(256)} %param.13) | copy-start | bytes 3076
  13.3 109.9 %all-to-all-start.1 = ((bf16[32,2,2,8,1024]{4,3,2,1,0:T(8,128)(2,1)}), bf16[32,2,2,8,1024]{4,3,2,1,0:T(8,128)(2,1)S(1)}, u32[]{:S(2)}, u32[]{:S(2)}) async-start(bf16[32,2,2,8,1024]{4,3,2,1,0:T(8,128)(2,1)} %bitcast.8), calls=%async_computation.1 | async-start | bytes 4194304 | tf_op jit(solution)/shard_map/all_to_all | solution.py:87
  123.2 19.8 %all-to-all-start = ((bf16[8,32,320]{2,0,1:T(8,128)(2,1)}), bf16[8,32,320]{2,0,1:T(8,128)(2,1)S(1)}, u32[]{:S(2)}, u32[]{:S(2)}) async-start(bf16[8,32,320]{2,0,1:T(8,128)(2,1)} %fusion.18), calls=%async_computation | async-start | bytes 393216 | tf_op jit(solution)/shard_map/all_to_all | solution.py:28
  146.0 58.9 %all-to-all-start.2 = ((bf16[8,32,256]{2,0,1:T(8,128)(2,1)}), bf16[8,32,256]{2,0,1:T(8,128)(2,1)S(1)}, u32[]{:S(2)}, u32[]{:S(2)}) async-start(bf16[8,32,256]{2,0,1:T(8,128)(2,1)} %copy.32), calls=%async_computation.2 | async-start | bytes 262144 | tf_op jit(solution)/shard_map/all_to_all | solution.py:28
  150.1 190.6 %reduce-scatter.2.cloned.1.call-start = ((), (), s32[]{:S(2)}) async-start(), calls=%async_computation.6 | async-start | bytes 4325376 | tf_op jit(solution)/shard_map/reduce_scatter | solution.py:111
Sparse Core Ops, SparseCore 0:
  10.3 106.0 all-gather.2
  119.4 85.4 all-gather.4
  212.7 127.9 reduce-scatter.1
where the time goes:
time: 348 us; the launch traced here: 347 us
  waiting for transfers between devices  278 us (80%)
  starting transfers between devices  26 us (7%)
  between operations  13.3 us (4%)
  local copies, waits for them, and re-layouts  12.2 us (4%)
  matrix products  11.4 us (3%)
  other arithmetic  5.99 us (2%)
    reduce_scatter x1, waiting for transfers between devices, shards(): lax.psum_scatter(terms.astype(jnp.bfloat16), 'beam', scatter_dimension=1,...  128 us
    all_gather x1, waiting for transfers between devices, shards(): lax.all_gather(w_qkv, 'owner', axis=0, tiled=True)  87.4 us
    all_gather x1, waiting for transfers between devices, shards(): w_piece = lax.all_gather(w_out, 'owner', axis=1, tiled=True)  54.7 us
    all_to_all x2, starting transfers between devices, regroup(): lax.all_to_all(blocks, 'beam', split_axis=1, concat_axis=1, tiled=True)  14 us
    all_to_all x1, starting transfers between devices, shards(): lax.all_to_all(outgoing, 'beam', split_axis=0, concat_axis=0, tiled=True)  11.9 us
  transfers between devices with their start and end apart: 6, of which 4 were waited for; matrix products, arithmetic and copies ran while one was open for 6% of the time, Pallas kernels for 0%

commit v1 on v0

--- a/solution.py
+++ b/solution.py
@@ -1,6 +1,7 @@
 import jax
 import jax.numpy as jnp
 from jax import lax
+from jax.sharding import Mesh
 from jax.sharding import PartitionSpec as P
 
 QH = 64
@@ -9,6 +10,10 @@
 CACHE = 32
 PAGE = 8
 QKV = 10240
+
+OWNER = ("x", "yh")
+BEAM = ("yl", "z", "c")
+PAIR = ("yl", "z")
 
 
 def rotary_embed(values, positions):
@@ -25,7 +30,12 @@
 
 
 def regroup(blocks):
-    return lax.all_to_all(blocks, "beam", split_axis=1, concat_axis=1, tiled=True)
+    return lax.all_to_all(blocks, BEAM, split_axis=1, concat_axis=1, tiled=True)
+
+
+def gather_rows(tile, axis, count):
+    copies = jnp.broadcast_to(tile[None], (count,) + tile.shape)
+    return lax.all_to_all(copies, axis, 0, 0, tiled=True).reshape((-1,) + tile.shape[1:])
 
 
 def attend(queries, fresh_key, value_new, keys, values, positions):
@@ -59,19 +69,18 @@
 
 
 def shards(hidden, norm_gain, w_qkv, w_out, kv_cache, lengths, kept_parent_device, keep_block):
-    columns = lax.axis_size("beam")
-    my_column = lax.axis_index("beam")
+    columns = lax.axis_size(BEAM)
+    my_column = lax.axis_index(BEAM)
     grouped_row_block = hidden.shape[0]
     own_beams = grouped_row_block // columns
+    w_piece = lax.all_gather(w_out, OWNER, axis=1, tiled=True)
+    full_w = gather_rows(gather_rows(w_qkv, "yh", lax.axis_size("yh")), "x", lax.axis_size("x"))
     floats = hidden.astype(jnp.float32)
     scale_rms = lax.rsqrt(jnp.mean(floats * floats, axis=-1, keepdims=True) + 1e-05)
     normed = (floats * scale_rms * norm_gain.astype(jnp.float32)).astype(jnp.bfloat16)
     normed_split = normed.reshape(columns, own_beams, normed.shape[1])
     projected = jnp.einsum(
-        "jbd,dc->bjc",
-        normed_split,
-        lax.all_gather(w_qkv, "owner", axis=0, tiled=True),
-        preferred_element_type=jnp.float32,
+        "jbd,dc->bjc", normed_split, full_w, preferred_element_type=jnp.float32
     )
     own_qkv = regroup(projected.astype(jnp.bfloat16)).reshape(own_beams, QKV)
     blk_dev = kv_cache.shape[0]
@@ -84,7 +93,7 @@
     chosen = is_mine[:, :, None] * (ranks[:, :, None] == slot_ids[None, None, :]).astype(jnp.int32)
     send_table = jnp.sum(chosen * picked[:, :, None], axis=1)
     outgoing = kv_cache[send_table.reshape(-1)].reshape((columns, most_slots) + kv_cache.shape[1:])
-    incoming_blocks = lax.all_to_all(outgoing, "beam", split_axis=0, concat_axis=0, tiled=True)
+    incoming_blocks = lax.all_to_all(outgoing, BEAM, split_axis=0, concat_axis=0, tiled=True)
     own_sources = lax.dynamic_index_in_dim(sources, my_column, 0, keepdims=False)
     one_hot = (own_sources[:, None] == jnp.arange(columns, dtype=jnp.int32)[None, :]).astype(
         jnp.int32
@@ -104,27 +113,38 @@
     fresh_key = rotary_embed(key_cols, positions).astype(jnp.bfloat16)
     attn = attend(queries, fresh_key, value_new, keys, values, positions)
     head_rows = regroup(attn.reshape(own_beams, columns, attn.shape[1] // columns))
-    w_piece = lax.all_gather(w_out, "owner", axis=1, tiled=True)
     terms = jnp.einsum(
         "bjh,hc->jbc", head_rows, w_piece, preferred_element_type=jnp.float32
-    ).reshape(grouped_row_block, w_piece.shape[1])
-    return lax.psum_scatter(terms.astype(jnp.bfloat16), "beam", scatter_dimension=1, tiled=True)
+    ).reshape(grouped_row_block, w_piece.shape[1]).astype(jnp.bfloat16)
+    cores = lax.axis_size("c")
+    core = lax.axis_index("c")
+    width = terms.shape[1] // columns
+    split = terms.reshape(grouped_row_block, columns // cores, cores, width)
+    kept = jnp.take(split, core, axis=2)
+    sent = jnp.take(split, 1 - core, axis=2)
+    got = lax.ppermute(sent, "c", [(0, 1), (1, 0)])
+    pair = (kept.astype(jnp.float32) + got.astype(jnp.float32)).astype(jnp.bfloat16)
+    spread = lax.all_to_all(pair.transpose(1, 0, 2), PAIR, 0, 0, tiled=True)
+    return jnp.sum(spread.astype(jnp.float32), axis=0).astype(jnp.bfloat16)
 
 
 def solution(mesh):
+    sizes = dict(mesh.shape)
+    parts = mesh.devices.reshape(4, sizes["owner"] // 4, 2, sizes["beam"] // 4, 2)
+    view = Mesh(parts, OWNER + BEAM)
     return jax.shard_map(
         shards,
-        mesh=mesh,
+        mesh=view,
         in_specs=(
-            P("owner", None),
+            P(OWNER, None),
             P(),
-            P("owner", "beam"),
-            P("beam", "owner"),
-            P(("owner", "beam"), None, None, None),
-            P("owner"),
-            P("owner", None),
-            P("owner"),
+            P(OWNER, BEAM),
+            P(BEAM, OWNER),
+            P(OWNER + BEAM, None, None, None),
+            P(OWNER),
+            P(OWNER, None),
+            P(OWNER),
         ),
-        out_specs=P("owner", "beam"),
+        out_specs=P(OWNER, BEAM),
         check_vma=False,
     )

time: 348 us -> 321 us (0.922)
  waiting for transfers between devices: 278 us -> 101 us
  blocking collectives: 0 us -> 87.5 us
  local copies, waits for them, and re-layouts: 12.2 us -> 41.1 us
  starting transfers between devices: 26 us -> 42.7 us
  other arithmetic: 5.99 us -> 19.6 us
    all_gather x2 -> x1, waiting for transfers between devices: 142 us -> 0.01 us  [shards(): w_piece = lax.all_gather(w_out, OWNER, axis=1, tiled=True)]
    reduce_scatter x1 -> x0, waiting for transfers between devices: 128 us -> none  [shards(): lax.psum_scatter(terms.astype(jnp.bfloat16), 'beam', scatter_dimension=1,...]
    all_to_all x3 -> x4, waiting for transfers between devices: 6.75 us -> 96.3 us  [the longest x1 51.4 us: gather_rows(): lax.all_to_all(copies, axis, 0, 0, tiled=True)]
    all_to_all x0 -> x2, blocking collectives: none -> 87.5 us  [the longest x1 52.9 us: shards(): spread = lax.all_to_all(pair.transpose(1, 0, 2), PAIR, 0, 0, tiled=True)]
    all_to_all x3 -> x4, starting transfers between devices: 25.9 us -> 40.7 us  [the longest x1 19.8 us: shards(): lax.all_to_all(outgoing, BEAM, split_axis=0, concat_axis=0, tiled=True)]
    select_n x0 -> x1, other arithmetic: none -> 12.4 us  [shards(): kept = jnp.take(split, core, axis=2)]
    reshape x0 -> x1, local copies, waits for them, and re-layouts: none -> 9.39 us  [gather_rows(): lax.all_to_all(copies, axis, 0, 0, tiled=True)]
    all_to_all x1 -> x2, local copies, waits for them, and re-layouts: 0.02 us -> 9.06 us  [the longest x1 9.03 us: gather_rows(): lax.all_to_all(copies, axis, 0, 0, tiled=True)]
  transfers between devices with their start and end apart: 6 -> 6, of which waited for: 4 -> 5; matrix products, arithmetic and copies ran while one was open for 6% -> 12% of each run, Pallas kernels for 0% -> 0%
where the time goes in v1:
time: 321 us; the launch traced here: 317 us
  waiting for transfers between devices  101 us (31%)
  blocking collectives  87.5 us (27%)
  starting transfers between devices  42.7 us (13%)
  local copies, waits for them, and re-layouts  41.1 us (13%)
  other arithmetic  19.6 us (6%)
  between operations  13.7 us (4%)
  matrix products  11.7 us (4%)
    all_to_all x1, blocking collectives, shards(): spread = lax.all_to_all(pair.transpose(1, 0, 2), PAIR, 0, 0, tiled=True)  52.9 us
    all_to_all x1, waiting for transfers between devices, gather_rows(): lax.all_to_all(copies, axis, 0, 0, tiled=True)  51.4 us
    all_to_all x1, blocking collectives, gather_rows(): lax.all_to_all(copies, axis, 0, 0, tiled=True)  34.6 us
    all_to_all x1, waiting for transfers between devices, shards(): lax.all_to_all(outgoing, BEAM, split_axis=0, concat_axis=0, tiled=True)  27.2 us
    all_to_all x1, starting transfers between devices, shards(): lax.all_to_all(outgoing, BEAM, split_axis=0, concat_axis=0, tiled=True)  19.8 us
    all_to_all x2, waiting for transfers between devices, regroup(): return lax.all_to_all(blocks, BEAM, split_axis=1, concat_axis=1, tiled=True)  17.7 us
    all_to_all x2, starting transfers between devices, regroup(): return lax.all_to_all(blocks, BEAM, split_axis=1, concat_axis=1, tiled=True)  13.5 us
    select_n x1, other arithmetic, shards(): kept = jnp.take(split, core, axis=2)  12.4 us
  transfers between devices with their start and end apart: 6, of which 5 were waited for; matrix products, arithmetic and copies ran while one was open for 12% of the time, Pallas kernels for 0%

profile of v1, /device:TPU:56, one launch (start us, length us, event | category | flops | bytes accessed | tf_op | source)
XLA Modules:
  0.0 317.3 jit_solution(14353957520964871685)
XLA Ops:
  6.5 0.0 copy-start
  6.5 1.2 broadcast_in_dim.27
  7.7 34.6 %all_to_all.30 = bf16[4,512,320]{1,2,0:T(8,128)(2,1)S(1)} all-to-all(bf16[4,512,320]{1,2,0:T(8,128)(2,1)S(1)} %broadcast_in_dim.27), channel_id=1, replica_groups=mesh['x'=4,'yh'=4,'yl'=2,'z'=8,'c'=2] {'yh'}, dimensions={0} | all-to-all | bytes 2621440 | tf_op jit(solution)/shard_map/all_to_all | solution.py:38
  42.3 0.2 copy.66
  42.5 3.0 broadcast_in_dim.29
  45.5 7.4 %all-to-all-start.1 = ((bf16[4,2048,320]{1,2,0:T(8,128)(2,1)}), bf16[4,2048,320]{1,2,0:T(8,128)(2,1)}, u32[]{:S(2)}, u32[]{:S(2)}) async-start(bf16[4,2048,320]{1,2,0:T(8,128)(2,1)} %broadcast_in_dim.29), calls=%async_computation.1 | async-start | bytes 10485760 | tf_op jit(solution)/shard_map/all_to_all | solution.py:38
  52.9 0.0 all-gather.2.cloned.1.call-start
  52.9 0.7 all-gather.2.cloned.1.call-update
  53.6 0.5 broadcast.197
  54.1 0.7 reduce.4
  54.8 0.1 reshape.215
  54.9 0.2 reduce_window_sum.22
  55.0 0.1 mul.201
  55.1 0.1 multiply_reduce_fusion
  55.2 0.1 copy.52
  55.3 0.1 reshape.216
  55.5 0.0 copy-start.2
  55.5 0.0 copy-start.5
  55.5 2.0 gather_fusion
  57.5 51.4 %all-to-all-done.1 = bf16[4,2048,320]{1,2,0:T(8,128)(2,1)} async-done(((bf16[4,2048,320]{1,2,0:T(8,128)(2,1)}), bf16[4,2048,320]{1,2,0:T(8,128)(2,1)}, u32[]{:S(2)}, u32[]{:S(2)}) %all-to-all-start.1) | async-done | bytes 5242912 | tf_op jit(solution)/shard_map/all_to_all | solution.py:38
  108.9 19.8 %all-to-all-start.3 = ((bf16[32,2,2,8,1024]{4,3,2,1,0:T(8,128)(2,1)}), bf16[32,2,2,8,1024]{4,3,2,1,0:T(8,128)(2,1)S(1)}, u32[]{:S(2)}, u32[]{:S(2)}) async-start(bf16[32,2,2,8,1024]{4,3,2,1,0:T(8,128)(2,1)} %bitcast.7), calls=%async_computation.3 | async-start | bytes 4194304 | tf_op jit(solution)/shard_map/all_to_all | solution.py:96
  128.7 0.0 copy-done.2
  128.8 0.1 fusion.37
  128.8 0.1 reduce_window_sum.23
  128.9 0.0 copy-done.5
  128.9 0.1 fusion.45
  129.0 0.2 select_reduce_fusion
  129.2 0.1 iota_compare_fusion.2
  129.2 3.1 fusion.1
  132.4 0.1 multiply_cosine_fusion
  132.5 9.0 %copy.48 = bf16[4,2048,320]{1,0,2:T(4,128)(2,1)} copy(bf16[4,2048,320]{1,2,0:T(8,128)(2,1)} %all-to-all-done.1) | data formatting | bytes 10485760 | tf_op jit(solution)/shard_map/all_to_all | solution.py:38
  141.5 9.4 %reshape.298 = bf16[8192,320,1]{0,1,2:T(8,128)(2,1)} reshape(bf16[4,2048,320]{1,0,2:T(4,128)(2,1)} %copy.48) | data formatting | bytes 10485760 | tf_op jit(solution)/shard_map/reshape | solution.py:38
  150.9 7.1 %fusion.16 = bf16[8,32,320]{2,0,1:T(8,128)(2,1)} fusion(bf16[8192,320,1]{0,1,2:T(8,128)(2,1)} %reshape.298, bf16[256,8192]{1,0:T(8,128)(2,1)} %param.10, f32[8192]{0:T(1024)S(1)} %convert_element_type.97, f32[256]{0:T(256)S(1)} %add_rsqrt_fusion), kind=kOutput, calls=%fused_computation.24 | convolution fusion | flops 1350647808 | bytes 9634816 | tf_op jit(solution)/shard_map/jbd,dc->bjc/dot_general | solution.py:82
  158.0 27.2 %all-to-all-done.3 = bf16[32,2,2,8,1024]{4,3,2,1,0:T(8,128)(2,1)S(1)} async-done(((bf16[32,2,2,8,1024]{4,3,2,1,0:T(8,128)(2,1)}), bf16[32,2,2,8,1024]{4,3,2,1,0:T(8,128)(2,1)S(1)}, u32[]{:S(2)}, u32[]{:S(2)}) %all-to-all-start.3) | async-done | bytes 2097184 | tf_op jit(solution)/shard_map/all_to_all | solution.py:96
  185.2 9.4 %all-to-all-start.2 = ((bf16[8,32,320]{2,0,1:T(8,128)(2,1)}), bf16[8,32,320]{2,0,1:T(8,128)(2,1)S(1)}, u32[]{:S(2)}, u32[]{:S(2)}) async-start(bf16[8,32,320]{2,0,1:T(8,128)(2,1)} %fusion.16), calls=%async_computation.2 | async-start | bytes 393216 | tf_op jit(solution)/shard_map/all_to_all | solution.py:33
  194.6 0.6 gather_fusion.1
  195.2 0.3 copy.67
  195.5 0.1 fusion.46
  195.6 9.0 %all-to-all-done.2 = bf16[8,32,320]{2,0,1:T(8,128)(2,1)S(1)} async-done(((bf16[8,32,320]{2,0,1:T(8,128)(2,1)}), bf16[8,32,320]{2,0,1:T(8,128)(2,1)S(1)}, u32[]{:S(2)}, u32[]{:S(2)}) %all-to-all-start.2) | async-done | bytes 163872 | tf_op jit(solution)/shard_map/all_to_all | solution.py:33
  204.6 0.2 reshape.214
  204.8 0.1 subtract_convert_fusion.1
  204.9 0.1 maximum_bitcast_fusion
  205.0 0.1 fusion.47
  205.2 0.1 fusion.24
  205.3 0.3 fusion.32
  205.6 0.5 fusion.48
  206.1 0.3 fusion.23
  206.4 0.3 fusion.15
  206.8 0.7 copy.56
  207.5 4.1 %all-to-all-start.4 = ((bf16[8,32,256]{2,0,1:T(8,128)(2,1)}), bf16[8,32,256]{2,0,1:T(8,128)(2,1)S(1)}, u32[]{:S(2)}, u32[]{:S(2)}) async-start(bf16[8,32,256]{2,0,1:T(8,128)(2,1)} %copy.56), calls=%async_computation.4 | async-start | bytes 262144 | tf_op jit(solution)/shard_map/all_to_all | solution.py:33
  211.7 8.7 %all-to-all-done.4 = bf16[8,32,256]{2,0,1:T(8,128)(2,1)S(1)} async-done(((bf16[8,32,256]{2,0,1:T(8,128)(2,1)}), bf16[8,32,256]{2,0,1:T(8,128)(2,1)S(1)}, u32[]{:S(2)}, u32[]{:S(2)}) %all-to-all-start.4) | async-done | bytes 131104 | tf_op jit(solution)/shard_map/all_to_all | solution.py:33
  220.4 3.4 %fusion = bf16[32,8,8192]{2,0,1:T(8,128)(2,1)S(1)} fusion(bf16[256,8192]{1,0:T(8,128)(2,1)} %all-gather.2.cloned.1.call-done, bf16[8,32,256]{2,0,1:T(8,128)(2,1)S(1)} %all-to-all-done.4), kind=kOutput, calls=%fused_computation.5 | convolution fusion | flops 1075838976 | bytes 8519680 | tf_op jit(solution)/shard_map/bjh,hc->jbc/dot_general | solution.py:116
  223.8 4.2 %copy.58 = bf16[32,8,8192]{2,1,0:T(8,128)(2,1)} copy(bf16[32,8,8192]{2,0,1:T(8,128)(2,1)S(1)} %fusion) | data formatting | bytes 8388608 | tf_op jit(solution)/shard_map/convert_element_type | solution.py:118
  228.1 7.8 %convert_element_type.117 = bf16[256,16,2,256]{3,2,1,0:T(2,128)(2,1)} reshape(bf16[32,8,8192]{2,1,0:T(8,128)(2,1)} %copy.58) | data formatting | bytes 8388608 | tf_op jit(solution)/shard_map/convert_element_type | solution.py:118
  235.9 12.4 %broadcast_select_fusion.1 = (bf16[256,16,1,256]{3,2,1,0:T(2,128)(2,1)S(1)}, bf16[256,16,1,256]{3,2,1,0:T(2,128)(2,1)S(1)}) fusion(pred[]{:T(512)S(6)} %and.9, bf16[256,16,2,256]{3,2,1,0:T(2,128)(2,1)} %convert_element_type.117, s32[]{:T(128)S(6)} %select_n.53, s32[]{:T(128)S(6)} %select_n.55, pred[]{:T(512)S(6)} %and.10), kind=kLoop, calls=%fused_computation.10 | loop fusion | flops 2097152 | bytes 8388618 | tf_op jit(solution)/shard_map/jit(_take)/select_n | solution.py:123
  248.3 0.6 copy.96
  248.9 2.0 collective-permute-start
  250.9 4.0 %collective-permute-done = bf16[256,16,256]{2,1,0:T(8,128)(2,1)S(1)} collective-permute-done((bf16[256,16,256]{2,1,0:T(8,128)(2,1)S(1)}, bf16[256,16,256]{2,1,0:T(8,128)(2,1)S(1)}, u32[]{:S(2)}, u32[]{:S(2)}) %collective-permute-start) | collective-permute-done | bytes 2097184 | tf_op jit(solution)/shard_map/ppermute | solution.py:125
  254.9 1.0 fusion.10
  255.9 0.0 copy-start.1
  255.9 0.8 copy.59
  256.6 52.9 %all_to_all.31 = bf16[16,256,256]{2,1,0:T(8,128)(2,1)S(1)} all-to-all(bf16[16,256,256]{2,1,0:T(8,128)(2,1)S(1)} %copy.59), channel_id=1, replica_groups=mesh['x'=4,'yh'=4,'yl'=2,'z'=8,'c'=2] {'yl','z'}, dimensions={0} | all-to-all | bytes 4194304 | tf_op jit(solution)/shard_map/all_to_all | solution.py:127
  309.5 1.0 reduce_sum.55
  310.5 0.0 copy-done.1
  (23 shorter events, 0.2 us)
Async XLA Ops:
  6.5 48.9 %copy-start = (bf16[32,2,8,1024]{3,2,1,0:T(8,128)(2,1)S(1)}, bf16[32,2,8,1024]{3,2,1,0:T(8,128)(2,1)}, u32[]{:S(2)}) copy-start(bf16[32,2,8,1024]{3,2,1,0:T(8,128)(2,1)} %param.14) | copy-start | bytes 3145732
  45.5 8.6 %copy-start.4 = (s32[1024,1]{0,1:T(1,128)S(1)}, s32[1024,1]{0,1:T(1,128)}, u32[]{:S(2)}) copy-start(s32[1024,1]{0,1:T(1,128)} %param.16) | copy-start | bytes 12292
  45.5 9.6 %copy-start.3 = (s32[1024]{0:T(1024)S(1)}, s32[1024]{0:T(1024)}, u32[]{:S(2)}) copy-start(s32[1024]{0:T(1024)} %param.17) | copy-start | bytes 12292
  45.5 63.4 %all-to-all-start.1 = ((bf16[4,2048,320]{1,2,0:T(8,128)(2,1)}), bf16[4,2048,320]{1,2,0:T(8,128)(2,1)}, u32[]{:S(2)}, u32[]{:S(2)}) async-start(bf16[4,2048,320]{1,2,0:T(8,128)(2,1)} %broadcast_in_dim.29), calls=%async_computation.1 | async-start | bytes 10485760 | tf_op jit(solution)/shard_map/all_to_all | solution.py:38
  52.9 167.5 %all-gather.2.cloned.1.call-start = ((), (), s32[]{:S(2)}) async-start(), calls=%async_computation.6 | async-start | bytes 4456448 | tf_op jit(solution)/shard_map/all_gather | solution.py:76
  55.5 73.2 %copy-start.2 = (bf16[8192]{0:T(1024)(128)(2,1)S(1)}, bf16[8192]{0:T(1024)(128)(2,1)}, u32[]{:S(2)}) copy-start(bf16[8192]{0:T(1024)(128)(2,1)} %param.11) | copy-start | bytes 49156
  55.5 73.4 %copy-start.5 = (s32[256]{0:T(256)S(1)}, s32[256]{0:T(256)}, u32[]{:S(2)}) copy-start(s32[256]{0:T(256)} %param.15) | copy-start | bytes 3076
  108.9 76.3 %all-to-all-start.3 = ((bf16[32,2,2,8,1024]{4,3,2,1,0:T(8,128)(2,1)}), bf16[32,2,2,8,1024]{4,3,2,1,0:T(8,128)(2,1)S(1)}, u32[]{:S(2)}, u32[]{:S(2)}) async-start(bf16[32,2,2,8,1024]{4,3,2,1,0:T(8,128)(2,1)} %bitcast.7), calls=%async_computation.3 | async-start | bytes 4194304 | tf_op jit(solution)/shard_map/all_to_all | solution.py:96
  185.2 19.4 %all-to-all-start.2 = ((bf16[8,32,320]{2,0,1:T(8,128)(2,1)}), bf16[8,32,320]{2,0,1:T(8,128)(2,1)S(1)}, u32[]{:S(2)}, u32[]{:S(2)}) async-start(bf16[8,32,320]{2,0,1:T(8,128)(2,1)} %fusion.16), calls=%async_computation.2 | async-start | bytes 393216 | tf_op jit(solution)/shard_map/all_to_all | solution.py:33
  207.5 12.8 %all-to-all-start.4 = ((bf16[8,32,256]{2,0,1:T(8,128)(2,1)}), bf16[8,32,256]{2,0,1:T(8,128)(2,1)S(1)}, u32[]{:S(2)}, u32[]{:S(2)}) async-start(bf16[8,32,256]{2,0,1:T(8,128)(2,1)} %copy.56), calls=%async_computation.4 | async-start | bytes 262144 | tf_op jit(solution)/shard_map/all_to_all | solution.py:33
  248.9 6.1 %collective-permute-start = (bf16[256,16,256]{2,1,0:T(8,128)(2,1)S(1)}, bf16[256,16,256]{2,1,0:T(8,128)(2,1)S(1)}, u32[]{:S(2)}, u32[]{:S(2)}) collective-permute-start(bf16[256,16,256]{2,1,0:T(8,128)(2,1)S(1)} %bitcast.84), channel_id=1, source_target_pairs={{0,1},{1,0},{2,3},{3,2},{4,5},{5,4},{6,7},{7,6},{8,9},{9,8},{10,11... | collective-permute-start | bytes 6291464 | tf_op jit(solution)/shard_map/ppermute | solution.py:125
  255.9 54.6 %copy-start.1 = (bf16[32,2,8,1024]{3,2,1,0:T(8,128)(2,1)S(1)}, bf16[32,2,8,1024]{3,2,1,0:T(8,128)(2,1)}, u32[]{:S(2)}) copy-start(bf16[32,2,8,1024]{3,2,1,0:T(8,128)(2,1)} %param.14) | copy-start | bytes 3145732
Sparse Core Ops, SparseCore 0:
  56.7 132.3 all-gather.1

commit v2 on v1

--- a/solution.py
+++ b/solution.py
@@ -73,14 +73,20 @@
     my_column = lax.axis_index(BEAM)
     grouped_row_block = hidden.shape[0]
     own_beams = grouped_row_block // columns
-    w_piece = lax.all_gather(w_out, OWNER, axis=1, tiled=True)
-    full_w = gather_rows(gather_rows(w_qkv, "yh", lax.axis_size("yh")), "x", lax.axis_size("x"))
+    halves = w_out.reshape(w_out.shape[0], lax.axis_size("c"), w_out.shape[1] // lax.axis_size("c"))
+    w_local = lax.all_to_all(halves, "c", 1, 0, tiled=True).reshape(-1, halves.shape[2])
+    w_pair = lax.all_gather(w_local, OWNER, axis=1, tiled=False)
+    xs = lax.axis_size("x")
+    full_w = lax.all_to_all(
+        jnp.broadcast_to(gather_rows(w_qkv, "yh", lax.axis_size("yh"))[None], (xs, w_qkv.shape[0] * lax.axis_size("yh"), w_qkv.shape[1])),
+        "x", 0, 0, tiled=True,
+    )
     floats = hidden.astype(jnp.float32)
     scale_rms = lax.rsqrt(jnp.mean(floats * floats, axis=-1, keepdims=True) + 1e-05)
     normed = (floats * scale_rms * norm_gain.astype(jnp.float32)).astype(jnp.bfloat16)
-    normed_split = normed.reshape(columns, own_beams, normed.shape[1])
+    normed_split = normed.reshape(columns, own_beams, full_w.shape[0], full_w.shape[1])
     projected = jnp.einsum(
-        "jbd,dc->bjc", normed_split, full_w, preferred_element_type=jnp.float32
+        "jbxd,xdc->bjc", normed_split, full_w, preferred_element_type=jnp.float32
     )
     own_qkv = regroup(projected.astype(jnp.bfloat16)).reshape(own_beams, QKV)
     blk_dev = kv_cache.shape[0]
@@ -112,19 +118,25 @@
     queries = rotary_embed(query_cols, positions).astype(jnp.bfloat16)
     fresh_key = rotary_embed(key_cols, positions).astype(jnp.bfloat16)
     attn = attend(queries, fresh_key, value_new, keys, values, positions)
-    head_rows = regroup(attn.reshape(own_beams, columns, attn.shape[1] // columns))
-    terms = jnp.einsum(
-        "bjh,hc->jbc", head_rows, w_piece, preferred_element_type=jnp.float32
-    ).reshape(grouped_row_block, w_piece.shape[1]).astype(jnp.bfloat16)
     cores = lax.axis_size("c")
-    core = lax.axis_index("c")
-    width = terms.shape[1] // columns
-    split = terms.reshape(grouped_row_block, columns // cores, cores, width)
-    kept = jnp.take(split, core, axis=2)
-    sent = jnp.take(split, 1 - core, axis=2)
-    got = lax.ppermute(sent, "c", [(0, 1), (1, 0)])
-    pair = (kept.astype(jnp.float32) + got.astype(jnp.float32)).astype(jnp.bfloat16)
-    spread = lax.all_to_all(pair.transpose(1, 0, 2), PAIR, 0, 0, tiled=True)
+    pairs = columns // cores
+    pair_feats = attn.reshape(own_beams, pairs, 1, cores * attn.shape[1] // columns)
+    doubled = jnp.broadcast_to(pair_feats, (own_beams, pairs, cores, pair_feats.shape[3]))
+    head_rows = lax.all_to_all(
+        doubled.reshape(own_beams, columns, pair_feats.shape[3]), BEAM, 1, 1, tiled=True
+    )
+    block = attn.shape[1] // columns
+    partial = None
+    for half in range(cores):
+        term = jnp.einsum(
+            "bjh,hpc->jbpc",
+            head_rows[:, :, half * block : (half + 1) * block],
+            w_pair[half * block : (half + 1) * block],
+            preferred_element_type=jnp.float32,
+        ).astype(jnp.bfloat16).astype(jnp.float32)
+        partial = term if partial is None else partial + term
+    partial = partial.astype(jnp.bfloat16).reshape(grouped_row_block, pairs, block)
+    spread = lax.all_to_all(partial.transpose(1, 0, 2), PAIR, 0, 0, tiled=True)
     return jnp.sum(spread.astype(jnp.float32), axis=0).astype(jnp.bfloat16)
 
 

time: 321 us -> 299 us (0.931)
  waiting for transfers between devices: 101 us -> 146 us
  local copies, waits for them, and re-layouts: 41.1 us -> 17.5 us
  blocking collectives: 87.5 us -> 68.3 us
  other arithmetic: 19.6 us -> 7.61 us
  starting transfers between devices: 42.7 us -> 34.5 us
    all_to_all x0 -> x2, waiting for transfers between devices: none -> 60.3 us  [the longest x1 60 us: shards(): lax.all_to_all(jnp.broadcast_to(gather_rows(w_qkv, 'yh', lax.axis_size('y...]
    all_to_all x1, waiting for transfers between devices: 51.4 us -> 27.2 us  [gather_rows(): lax.all_to_all(copies, axis, 0, 0, tiled=True)]
    all_to_all x1, waiting for transfers between devices: 27.2 us -> 51.4 us  [shards(): lax.all_to_all(outgoing, BEAM, split_axis=0, concat_axis=0, tiled=True)]
    all_to_all x2, blocking collectives: 87.5 us -> 68.3 us  [the longest x1 53.2 us: shards(): spread = lax.all_to_all(partial.transpose(1, 0, 2), PAIR, 0, 0, tiled=True)]
    select_n x1 -> x0, other arithmetic: 12.4 us -> none  [shards(): kept = jnp.take(split, core, axis=2)]
    all_to_all x2 -> x1, waiting for transfers between devices: 17.7 us -> 6.79 us  [regroup(): return lax.all_to_all(blocks, BEAM, split_axis=1, concat_axis=1, tiled=True)]
    convert_element_type x2 -> x1, local copies, waits for them, and re-layouts: 12 us -> 1.19 us  [shards(): partial.astype(jnp.bfloat16).reshape(grouped_row_block, pairs, block)]
    all_to_all x1 -> x0, local copies, waits for them, and re-layouts: 9.03 us -> none  [gather_rows(): lax.all_to_all(copies, axis, 0, 0, tiled=True)]
  transfers between devices with their start and end apart: 6 -> 6, of which waited for: 5 -> 5; matrix products, arithmetic and copies ran while one was open for 12% -> 7% of each run, Pallas kernels for 0% -> 0%
where the time goes in v2:
time: 299 us; the launch traced here: 298 us
  waiting for transfers between devices  146 us (49%)
  blocking collectives  68.3 us (23%)
  starting transfers between devices  34.5 us (12%)
  local copies, waits for them, and re-layouts  17.5 us (6%)
  between operations  13.7 us (5%)
  matrix products  9.97 us (3%)
  other arithmetic  7.61 us (3%)
    all_to_all x1, waiting for transfers between devices, shards(): lax.all_to_all(jnp.broadcast_to(gather_rows(w_qkv, 'yh', lax.axis_size('y...  60 us
    all_to_all x1, blocking collectives, shards(): spread = lax.all_to_all(partial.transpose(1, 0, 2), PAIR, 0, 0, tiled=True)  53.2 us
    all_to_all x1, waiting for transfers between devices, shards(): lax.all_to_all(outgoing, BEAM, split_axis=0, concat_axis=0, tiled=True)  51.4 us
    all_to_all x1, waiting for transfers between devices, gather_rows(): lax.all_to_all(copies, axis, 0, 0, tiled=True)  27.2 us
    all_to_all x1, blocking collectives, shards(): lax.all_to_all(doubled.reshape(own_beams, columns, pair_feats.shape[3]),...  15.1 us
    all_to_all x1, starting transfers between devices, shards(): lax.all_to_all(outgoing, BEAM, split_axis=0, concat_axis=0, tiled=True)  13.9 us
    all_to_all x1, starting transfers between devices, gather_rows(): lax.all_to_all(copies, axis, 0, 0, tiled=True)  6.97 us
    all_to_all x1, waiting for transfers between devices, regroup(): return lax.all_to_all(blocks, BEAM, split_axis=1, concat_axis=1, tiled=True)  6.79 us
  transfers between devices with their start and end apart: 6, of which 5 were waited for; matrix products, arithmetic and copies ran while one was open for 7% of the time, Pallas kernels for 0%

profile of v2, /device:TPU:56, one launch (start us, length us, event | category | flops | bytes accessed | tf_op | source)
XLA Modules:
  0.0 298.0 jit_solution(6359367847757346687)
XLA Ops:
  6.5 0.0 copy-start
  6.5 2.2 broadcast_in_dim.23
  8.8 7.0 %all-to-all-start = ((bf16[4,512,320]{1,2,0:T(8,128)(2,1)}), bf16[4,512,320]{1,2,0:T(8,128)(2,1)S(1)}, u32[]{:S(2)}, u32[]{:S(2)}) async-start(bf16[4,512,320]{1,2,0:T(8,128)(2,1)} %broadcast_in_dim.23), calls=%async_computation | async-start | bytes 2621440 | tf_op jit(solution)/shard_map/all_to_all | solution.py:38
  15.8 0.7 copy.98
  16.5 27.2 %all-to-all-done = bf16[4,512,320]{1,2,0:T(8,128)(2,1)S(1)} async-done(((bf16[4,512,320]{1,2,0:T(8,128)(2,1)}), bf16[4,512,320]{1,2,0:T(8,128)(2,1)S(1)}, u32[]{:S(2)}, u32[]{:S(2)}) %all-to-all-start) | async-done | bytes 1310752 | tf_op jit(solution)/shard_map/all_to_all | solution.py:38
  43.7 3.4 %all-to-all-start.5 = ((bf16[256,2,256]{2,0,1:T(8,128)(2,1)}), bf16[256,2,256]{2,0,1:T(8,128)(2,1)S(1)}, u32[]{:S(2)}, u32[]{:S(2)}) async-start(bf16[256,2,256]{2,0,1:T(8,128)(2,1)} %bitcast.107), calls=%async_computation.5 | async-start | bytes 524288 | tf_op jit(solution)/shard_map/all_to_all | solution.py:77
  47.1 1.2 copy.67
  48.4 0.3 all-to-all-done.5
  48.7 4.4 %broadcast_in_dim.25 = bf16[4,2048,320]{1,2,0:T(8,128)(2,1)} broadcast(bf16[2048,320]{0,1:T(8,128)(2,1)} %bitcast.110), dimensions={1,2} | broadcast | bytes 6553600 | tf_op jit(solution)/shard_map/broadcast_in_dim | solution.py:81
  53.1 0.0 copy-done.3
  53.1 5.2 %all-to-all-start.1 = ((bf16[4,2048,320]{1,2,0:T(8,128)(2,1)}), bf16[4,2048,320]{1,2,0:T(8,128)(2,1)}, u32[]{:S(2)}, u32[]{:S(2)}) async-start(bf16[4,2048,320]{1,2,0:T(8,128)(2,1)} %broadcast_in_dim.25), calls=%async_computation.1 | async-start | bytes 10485760 | tf_op jit(solution)/shard_map/all_to_all | solution.py:80
  58.3 0.0 all-gather.2.cloned.1.call-start
  58.3 0.7 all-gather.2.cloned.1.call-update
  59.0 0.5 broadcast.156
  59.6 0.7 reduce.4
  60.2 0.1 reshape.219
  60.3 0.1 fusion.36
  60.4 0.1 reduce_window_sum.23
  60.4 0.2 reduce_window_sum.22
  60.6 0.1 mul.201
  60.7 0.1 multiply_reduce_fusion
  60.8 0.1 copy.47
  60.9 0.1 reshape.220
  61.1 0.0 copy-start.5
  61.1 0.0 copy-start.8
  61.1 2.0 gather_fusion
  63.1 0.2 select_reduce_fusion
  63.3 60.0 %all-to-all-done.1 = bf16[4,2048,320]{1,2,0:T(8,128)(2,1)} async-done(((bf16[4,2048,320]{1,2,0:T(8,128)(2,1)}), bf16[4,2048,320]{1,2,0:T(8,128)(2,1)}, u32[]{:S(2)}, u32[]{:S(2)}) %all-to-all-start.1) | async-done | bytes 5242912 | tf_op jit(solution)/shard_map/all_to_all | solution.py:80
  123.3 13.9 %all-to-all-start.3 = ((bf16[32,2,2,8,1024]{4,3,2,1,0:T(8,128)(2,1)}), bf16[32,2,2,8,1024]{4,3,2,1,0:T(8,128)(2,1)S(1)}, u32[]{:S(2)}, u32[]{:S(2)}) async-start(bf16[32,2,2,8,1024]{4,3,2,1,0:T(8,128)(2,1)} %bitcast.10), calls=%async_computation.3 | async-start | bytes 4194304 | tf_op jit(solution)/shard_map/all_to_all | solution.py:102
  137.1 0.0 copy-done.5
  137.2 0.0 copy-done.8
  137.2 0.0 copy-start.1
  137.2 0.1 fusion.44
  137.3 0.1 iota_compare_fusion.2
  137.3 3.3 %fusion = f32[256]{0:T(256)S(1)} fusion(bf16[256,8192]{1,0:T(8,128)(2,1)} %param.8), kind=kLoop, calls=%fused_computation.4 | loop fusion | flops 6291200 | bytes 4195328 | tf_op jit(solution)/shard_map/reduce_sum | solution.py:85
  140.6 0.1 multiply_cosine_fusion
  140.7 1.2 fusion.2
  141.9 5.7 %fusion.16 = bf16[8,32,320]{2,0,1:T(8,128)(2,1)} fusion(bf16[32,8,4,2048]{3,1,2,0:T(8,128)(2,1)S(1)} %bitcast.113, bf16[4,2048,320]{1,2,0:T(8,128)(2,1)} %all-to-all-done.1), kind=kOutput, calls=%fused_computation.21 | convolution fusion | flops 1342259200 | bytes 9601024 | tf_op jit(solution)/shard_map/jbxd,xdc->bjc/dot_general | solution.py:88
  147.6 51.4 %all-to-all-done.3 = bf16[32,2,2,8,1024]{4,3,2,1,0:T(8,128)(2,1)S(1)} async-done(((bf16[32,2,2,8,1024]{4,3,2,1,0:T(8,128)(2,1)}), bf16[32,2,2,8,1024]{4,3,2,1,0:T(8,128)(2,1)S(1)}, u32[]{:S(2)}, u32[]{:S(2)}) %all-to-all-start.3) | async-done | bytes 2097184 | tf_op jit(solution)/shard_map/all_to_all | solution.py:102
  198.9 5.0 %all-to-all-start.2 = ((bf16[8,32,320]{2,0,1:T(8,128)(2,1)}), bf16[8,32,320]{2,0,1:T(8,128)(2,1)S(1)}, u32[]{:S(2)}, u32[]{:S(2)}) async-start(bf16[8,32,320]{2,0,1:T(8,128)(2,1)} %fusion.16), calls=%async_computation.2 | async-start | bytes 393216 | tf_op jit(solution)/shard_map/all_to_all | solution.py:33
  203.9 1.6 gather_fusion.1
  205.5 1.5 copy.68
  207.0 0.1 fusion.45
  207.1 6.8 %all-to-all-done.2 = bf16[8,32,320]{2,0,1:T(8,128)(2,1)S(1)} async-done(((bf16[8,32,320]{2,0,1:T(8,128)(2,1)}), bf16[8,32,320]{2,0,1:T(8,128)(2,1)S(1)}, u32[]{:S(2)}, u32[]{:S(2)}) %all-to-all-start.2) | async-done | bytes 163872 | tf_op jit(solution)/shard_map/all_to_all | solution.py:33
  213.9 0.2 reshape.218
  214.2 0.1 subtract_convert_fusion.1
  214.3 0.1 maximum_bitcast_fusion
  214.4 0.1 fusion.47
  214.5 0.1 fusion.24
  214.6 0.3 fusion.31
  214.9 0.5 fusion.48
  215.5 0.3 fusion.23
  215.8 0.3 fusion.15
  216.1 0.1 convert_element_type.120
  216.2 0.1 copy.51
  216.3 15.1 %all_to_all.48 = bf16[8,32,512]{2,0,1:T(8,128)(2,1)S(1)} all-to-all(bf16[8,32,512]{2,0,1:T(8,128)(2,1)S(1)} %bitcast.116), channel_id=1, replica_groups=mesh['x'=4,'yh'=4,'yl'=2,'z'=8,'c'=2] {'yl','z','c'}, dimensions={1} | all-to-all | bytes 524288 | tf_op jit(solution)/shard_map/all_to_all | solution.py:125
  231.5 0.0 all-gather.2.cloned.1.call-done
  231.5 2.5 fusion.6
  234.0 0.3 copy-done.2
  234.3 0.7 fusion.5
  235.0 1.2 copy.55
  236.2 0.7 copy.56
  236.9 53.2 %all_to_all.49 = bf16[16,256,256]{2,1,0:T(8,128)(2,1)S(1)} all-to-all(bf16[16,256,256]{2,1,0:T(8,128)(2,1)S(1)} %copy.56), channel_id=1, replica_groups=mesh['x'=4,'yh'=4,'yl'=2,'z'=8,'c'=2] {'yl','z'}, dimensions={0} | all-to-all | bytes 4194304 | tf_op jit(solution)/shard_map/all_to_all | solution.py:139
  290.2 1.0 reduce_sum.55
  (28 shorter events, 0.2 us)
Async XLA Ops:
  6.5 54.5 %copy-start = (bf16[32,2,8,1024]{3,2,1,0:T(8,128)(2,1)S(1)}, bf16[32,2,8,1024]{3,2,1,0:T(8,128)(2,1)}, u32[]{:S(2)}) copy-start(bf16[32,2,8,1024]{3,2,1,0:T(8,128)(2,1)} %param.12) | copy-start | bytes 3145732
  6.5 9.2 %copy-start.4 = (bf16[256,512]{1,0:T(8,128)(2,1)S(1)}, bf16[256,512]{1,0:T(8,128)(2,1)}, u32[]{:S(2)}) copy-start(bf16[256,512]{1,0:T(8,128)(2,1)} %param.11) | copy-start | bytes 786436
  8.8 34.9 %all-to-all-start = ((bf16[4,512,320]{1,2,0:T(8,128)(2,1)}), bf16[4,512,320]{1,2,0:T(8,128)(2,1)S(1)}, u32[]{:S(2)}, u32[]{:S(2)}) async-start(bf16[4,512,320]{1,2,0:T(8,128)(2,1)} %broadcast_in_dim.23), calls=%async_computation | async-start | bytes 2621440 | tf_op jit(solution)/shard_map/all_to_all | solution.py:38
  43.7 5.0 %all-to-all-start.5 = ((bf16[256,2,256]{2,0,1:T(8,128)(2,1)}), bf16[256,2,256]{2,0,1:T(8,128)(2,1)S(1)}, u32[]{:S(2)}, u32[]{:S(2)}) async-start(bf16[256,2,256]{2,0,1:T(8,128)(2,1)} %bitcast.107), calls=%async_computation.5 | async-start | bytes 524288 | tf_op jit(solution)/shard_map/all_to_all | solution.py:77
  48.7 4.4 %copy-start.3 = (bf16[256,2,256]{2,0,1:T(8,128)(2,1)}, bf16[256,2,256]{2,0,1:T(8,128)(2,1)S(1)}, u32[]{:S(2)}) copy-start(bf16[256,2,256]{2,0,1:T(8,128)(2,1)S(1)} %all-to-all-done.5) | copy-start | bytes 786436
  53.1 6.5 %copy-start.7 = (s32[1024,1]{0,1:T(1,128)S(1)}, s32[1024,1]{0,1:T(1,128)}, u32[]{:S(2)}) copy-start(s32[1024,1]{0,1:T(1,128)} %param.14) | copy-start | bytes 12292
  53.1 7.5 %copy-start.6 = (s32[1024]{0:T(1024)S(1)}, s32[1024]{0:T(1024)}, u32[]{:S(2)}) copy-start(s32[1024]{0:T(1024)} %param.15) | copy-start | bytes 12292
  53.1 70.1 %all-to-all-start.1 = ((bf16[4,2048,320]{1,2,0:T(8,128)(2,1)}), bf16[4,2048,320]{1,2,0:T(8,128)(2,1)}, u32[]{:S(2)}, u32[]{:S(2)}) async-start(bf16[4,2048,320]{1,2,0:T(8,128)(2,1)} %broadcast_in_dim.25), calls=%async_computation.1 | async-start | bytes 10485760 | tf_op jit(solution)/shard_map/all_to_all | solution.py:80
  58.3 173.2 %all-gather.2.cloned.1.call-start = ((), (), s32[]{:S(2)}) async-start(), calls=%async_computation.7 | async-start | bytes 4456448 | tf_op jit(solution)/shard_map/all_gather | solution.py:78
  61.1 76.1 %copy-start.5 = (bf16[8192]{0:T(1024)(128)(2,1)S(1)}, bf16[8192]{0:T(1024)(128)(2,1)}, u32[]{:S(2)}) copy-start(bf16[8192]{0:T(1024)(128)(2,1)} %param.9) | copy-start | bytes 49156
  61.1 76.1 %copy-start.8 = (s32[256]{0:T(256)S(1)}, s32[256]{0:T(256)}, u32[]{:S(2)}) copy-start(s32[256]{0:T(256)} %param.13) | copy-start | bytes 3076
  123.3 75.7 %all-to-all-start.3 = ((bf16[32,2,2,8,1024]{4,3,2,1,0:T(8,128)(2,1)}), bf16[32,2,2,8,1024]{4,3,2,1,0:T(8,128)(2,1)S(1)}, u32[]{:S(2)}, u32[]{:S(2)}) async-start(bf16[32,2,2,8,1024]{4,3,2,1,0:T(8,128)(2,1)} %bitcast.10), calls=%async_computation.3 | async-start | bytes 4194304 | tf_op jit(solution)/shard_map/all_to_all | solution.py:102
  137.2 3.5 %copy-start.1 = (bf16[256,8192]{1,0:T(8,128)(2,1)S(1)}, bf16[256,8192]{1,0:T(8,128)(2,1)}, u32[]{:S(2)}) copy-start(bf16[256,8192]{1,0:T(8,128)(2,1)} %param.8) | copy-start | bytes 12582916
  198.9 15.0 %all-to-all-start.2 = ((bf16[8,32,320]{2,0,1:T(8,128)(2,1)}), bf16[8,32,320]{2,0,1:T(8,128)(2,1)S(1)}, u32[]{:S(2)}, u32[]{:S(2)}) async-start(bf16[8,32,320]{2,0,1:T(8,128)(2,1)} %fusion.16), calls=%async_computation.2 | async-start | bytes 393216 | tf_op jit(solution)/shard_map/all_to_all | solution.py:33
  231.5 2.8 copy-start.2
Sparse Core Ops, SparseCore 0:
  62.1 124.6 all-gather.1

commit v3 on v2

--- a/solution.py
+++ b/solution.py
@@ -76,18 +76,34 @@
     halves = w_out.reshape(w_out.shape[0], lax.axis_size("c"), w_out.shape[1] // lax.axis_size("c"))
     w_local = lax.all_to_all(halves, "c", 1, 0, tiled=True).reshape(-1, halves.shape[2])
     w_pair = lax.all_gather(w_local, OWNER, axis=1, tiled=False)
-    xs = lax.axis_size("x")
-    full_w = lax.all_to_all(
-        jnp.broadcast_to(gather_rows(w_qkv, "yh", lax.axis_size("yh"))[None], (xs, w_qkv.shape[0] * lax.axis_size("yh"), w_qkv.shape[1])),
-        "x", 0, 0, tiled=True,
-    )
     floats = hidden.astype(jnp.float32)
     scale_rms = lax.rsqrt(jnp.mean(floats * floats, axis=-1, keepdims=True) + 1e-05)
     normed = (floats * scale_rms * norm_gain.astype(jnp.float32)).astype(jnp.bfloat16)
-    normed_split = normed.reshape(columns, own_beams, full_w.shape[0], full_w.shape[1])
-    projected = jnp.einsum(
-        "jbxd,xdc->bjc", normed_split, full_w, preferred_element_type=jnp.float32
+    stack = gather_rows(w_qkv, "yh", lax.axis_size("yh"))
+    xs = lax.axis_size("x")
+    assert xs == 4
+    me = lax.axis_index("x")
+    ahead = [(i, (i + 1) % xs) for i in range(xs)]
+    behind = [(i, (i - 1) % xs) for i in range(xs)]
+    from_left = lax.ppermute(stack, "x", ahead)
+    from_right = lax.ppermute(stack, "x", behind)
+    cut = stack.shape[0] // 2
+    far = jnp.concatenate(
+        [lax.ppermute(from_left[:cut], "x", ahead), lax.ppermute(from_right[cut:], "x", behind)],
+        axis=0,
     )
+    rows = stack.shape[0]
+    projected = None
+    for step, piece in ((0, stack), (1, from_right), (3, from_left), (2, far)):
+        start = ((me + step) % xs) * rows
+        block = lax.dynamic_slice_in_dim(normed, start, rows, axis=1)
+        term = jnp.einsum(
+            "jbd,dc->bjc",
+            block.reshape(columns, own_beams, rows),
+            piece,
+            preferred_element_type=jnp.float32,
+        )
+        projected = term if projected is None else projected + term
     own_qkv = regroup(projected.astype(jnp.bfloat16)).reshape(own_beams, QKV)
     blk_dev = kv_cache.shape[0]
     most_slots = max(2, 2 * blk_dev // columns)

time: 299 us -> 268 us (0.90)
  the two profiles are of different devices: /device:TPU:56 before, /device:TPU:30 now
where the time goes in v3:
time: 268 us; the launch traced here: 267 us
  waiting for transfers between devices  79.5 us (30%)
  blocking collectives  73.1 us (27%)
  starting transfers between devices  49.9 us (19%)
  local copies, waits for them, and re-layouts  23.2 us (9%)
  matrix products  14 us (5%)
  between operations  13.8 us (5%)
  other arithmetic  13.2 us (5%)
    all_to_all x1, blocking collectives, shards(): spread = lax.all_to_all(partial.transpose(1, 0, 2), PAIR, 0, 0, tiled=True)  53.3 us
    ppermute x1, waiting for transfers between devices, shards(): from_left = lax.ppermute(stack, 'x', ahead)  40.6 us
    all_to_all x1, waiting for transfers between devices, gather_rows(): lax.all_to_all(copies, axis, 0, 0, tiled=True)  22.6 us
    all_to_all x1, starting transfers between devices, shards(): lax.all_to_all(outgoing, BEAM, split_axis=0, concat_axis=0, tiled=True)  22.2 us
    all_to_all x1, blocking collectives, shards(): lax.all_to_all(doubled.reshape(own_beams, columns, pair_feats.shape[3]),...  15.1 us
    dot_general x4, matrix products, shards(): jnp.einsum('jbd,dc->bjc', block.reshape(columns, own_beams, rows), piece,...  9.68 us
    all_to_all x1, starting transfers between devices, regroup(): return lax.all_to_all(blocks, BEAM, split_axis=1, concat_axis=1, tiled=True)  9.22 us
    all_to_all x1, waiting for transfers between devices, regroup(): return lax.all_to_all(blocks, BEAM, split_axis=1, concat_axis=1, tiled=True)  7.4 us
  transfers between devices with their start and end apart: 8, of which 5 were waited for; matrix products, arithmetic and copies ran while one was open for 15% of the time, Pallas kernels for 0%

profile of v3, /device:TPU:30, one launch (start us, length us, event | category | flops | bytes accessed | tf_op | source)
XLA Modules:
  0.0 266.8 jit_solution(15529965986637563992)
XLA Ops:
  6.5 1.1 copy.95
  7.6 4.7 %all_to_all.43 = bf16[256,2,256]{2,0,1:T(8,128)(2,1)} all-to-all(bf16[256,2,256]{2,0,1:T(8,128)(2,1)S(1)} %bitcast.136), channel_id=1, replica_groups=mesh['x'=4,'yh'=4,'yl'=2,'z'=8,'c'=2] {'c'}, dimensions={1} | all-to-all | bytes 524288 | tf_op jit(solution)/shard_map/all_to_all | solution.py:77
  12.3 2.2 broadcast_in_dim.19
  14.4 6.5 %all-to-all-start = ((bf16[4,512,320]{1,2,0:T(8,128)(2,1)}), bf16[4,512,320]{1,2,0:T(8,128)(2,1)S(1)}, u32[]{:S(2)}, u32[]{:S(2)}) async-start(bf16[4,512,320]{1,2,0:T(8,128)(2,1)} %broadcast_in_dim.19), calls=%async_computation | async-start | bytes 2621440 | tf_op jit(solution)/shard_map/all_to_all | solution.py:38
  21.0 0.7 all-gather.2.cloned.1.call-update
  21.7 0.5 broadcast.160
  22.2 0.7 reduce.4
  22.9 0.1 reshape.234
  23.0 0.2 reduce_window_sum.22
  23.2 0.1 mul.217
  23.3 0.1 multiply_reduce_fusion
  23.4 0.1 copy.42
  23.5 0.1 reshape.235
  23.6 2.1 gather_fusion
  25.7 3.1 %fusion = f32[256]{0:T(256)S(1)} fusion(bf16[256,8192]{1,0:T(8,128)(2,1)} %param.8), kind=kLoop, calls=%fused_computation.4 | loop fusion | flops 6291200 | bytes 4195328 | tf_op jit(solution)/shard_map/reduce_sum | solution.py:80
  28.8 22.6 %all-to-all-done = bf16[4,512,320]{1,2,0:T(8,128)(2,1)S(1)} async-done(((bf16[4,512,320]{1,2,0:T(8,128)(2,1)}), bf16[4,512,320]{1,2,0:T(8,128)(2,1)S(1)}, u32[]{:S(2)}, u32[]{:S(2)}) %all-to-all-start) | async-done | bytes 1310752 | tf_op jit(solution)/shard_map/all_to_all | solution.py:38
  51.4 22.2 %all-to-all-start.2 = ((bf16[32,2,2,8,1024]{4,3,2,1,0:T(8,128)(2,1)}), bf16[32,2,2,8,1024]{4,3,2,1,0:T(8,128)(2,1)}, u32[]{:S(2)}, u32[]{:S(2)}) async-start(bf16[32,2,2,8,1024]{4,3,2,1,0:T(8,128)(2,1)} %bitcast.130), calls=%async_computation.2 | async-start | bytes 4194304 | tf_op jit(solution)/shard_map/all_to_all | solution.py:118
  73.6 5.3 %fusion.2 = bf16[256,8192]{1,0:T(8,128)(2,1)} fusion(bf16[256,8192]{1,0:T(8,128)(2,1)} %param.8, f32[8192]{0:T(1024)S(1)} %convert_element_type.100, f32[256]{0:T(256)S(1)} %add_rsqrt_fusion), kind=kLoop, calls=%fused_computation.6 | loop fusion | flops 8388608 | bytes 8422400 | tf_op jit(solution)/shard_map/convert_element_type | solution.py:81
  78.9 1.3 copy.61
  80.2 2.4 collective-permute-start.1
  82.6 3.5 %collective-permute-start = (bf16[2048,320]{0,1:T(8,128)(2,1)}, bf16[2048,320]{0,1:T(8,128)(2,1)}, u32[]{:S(2)}, u32[]{:S(2)}) collective-permute-start(bf16[2048,320]{0,1:T(8,128)(2,1)} %bitcast.50), channel_id=1, source_target_pairs={{0,384},{128,0},{256,128},{384,256},{1,385},{129,1},{257,129},{385... | collective-permute-start | bytes 3932168 | tf_op jit(solution)/shard_map/ppermute | solution.py:89
  86.1 0.1 fusion.55
  86.3 0.1 fusion.67
  86.4 0.2 select_reduce_fusion
  86.5 0.1 iota_compare_fusion.2
  86.6 0.1 multiply_cosine_fusion
  86.7 1.3 dynamic-slice_bitcast_fusion
  88.0 40.6 %collective-permute-done.1 = bf16[2048,320]{0,1:T(8,128)(2,1)} collective-permute-done((bf16[2048,320]{0,1:T(8,128)(2,1)}, bf16[2048,320]{0,1:T(8,128)(2,1)}, u32[]{:S(2)}, u32[]{:S(2)}) %collective-permute-start.1) | collective-permute-done | bytes 1310752 | tf_op jit(solution)/shard_map/ppermute | solution.py:88
  128.7 2.0 slice.64
  130.6 4.3 %collective-permute-start.2 = (bf16[1024,320]{0,1:T(8,128)(2,1)}, bf16[1024,320]{0,1:T(8,128)(2,1)}, u32[]{:S(2)}, u32[]{:S(2)}) collective-permute-start(bf16[1024,320]{0,1:T(8,128)(2,1)} %slice.64), channel_id=1, source_target_pairs={{0,128},{128,256},{256,384},{384,0},{1,129},{129,257},{257,385},{3... | collective-permute-start | bytes 1966088 | tf_op jit(solution)/shard_map/ppermute | solution.py:92
  134.9 2.0 slice.65
  136.9 1.9 collective-permute-start.3
  138.9 2.1 copy.36
  141.0 3.0 %reshape.261 = bf16[2048,320,1]{0,1,2:T(8,128)(2,1)S(1)} reshape(bf16[4,512,320]{1,0,2:T(4,128)(2,1)} %copy.36) | data formatting | bytes 2621440 | tf_op jit(solution)/shard_map/reshape | solution.py:38
  144.0 2.0 fusion.32
  146.0 2.4 fusion.9
  148.3 0.9 collective-permute-done.2
  149.3 7.2 %collective-permute-done.3 = bf16[1024,320]{0,1:T(8,128)(2,1)} collective-permute-done((bf16[1024,320]{0,1:T(8,128)(2,1)}, bf16[1024,320]{0,1:T(8,128)(2,1)}, u32[]{:S(2)}, u32[]{:S(2)}) %collective-permute-start.3) | collective-permute-done | bytes 655392 | tf_op jit(solution)/shard_map/ppermute | solution.py:92
  156.5 2.2 fusion.6
  158.7 3.2 %fusion.25 = bf16[8,32,320]{2,0,1:T(8,128)(2,1)} fusion(f32[32,8,320]{2,1,0:T(8,128)S(1)} %fusion.9, f32[32,8,320]{2,1,0:T(8,128)S(1)} %fusion.32, bf16[2048,320]{0,1:T(8,128)(2,1)} %collective-permute-done, bf16[256,8192]{1,0:T(8,128)(2,1)} %fusion.2, s32[]{:T(128)S(6)} %select_n.69, f32[320,32,8]{0,1,2:T(8,128)S(1)} %fusion.6), kind=kOutput, calls=%fused_computation.25 | convolution fusion | flops 335872000 | bytes 3506180 | tf_op jit(solution)/shard_map/jbd,dc->bjc/dot_general | solution.py:100
  161.8 9.2 %all-to-all-start.1 = ((bf16[8,32,320]{2,0,1:T(8,128)(2,1)}), bf16[8,32,320]{2,0,1:T(8,128)(2,1)S(1)}, u32[]{:S(2)}, u32[]{:S(2)}) async-start(bf16[8,32,320]{2,0,1:T(8,128)(2,1)} %fusion.25), calls=%async_computation.1 | async-start | bytes 393216 | tf_op jit(solution)/shard_map/all_to_all | solution.py:33
  171.1 2.2 gather_fusion.1
  173.3 0.3 copy.62
  173.6 0.1 fusion.68
  173.6 7.4 %all-to-all-done.1 = bf16[8,32,320]{2,0,1:T(8,128)(2,1)S(1)} async-done(((bf16[8,32,320]{2,0,1:T(8,128)(2,1)}), bf16[8,32,320]{2,0,1:T(8,128)(2,1)S(1)}, u32[]{:S(2)}, u32[]{:S(2)}) %all-to-all-start.1) | async-done | bytes 163872 | tf_op jit(solution)/shard_map/all_to_all | solution.py:33
  181.1 0.2 reshape.233
  181.3 0.1 subtract_convert_fusion.1
  181.4 0.1 maximum_bitcast_fusion.2
  181.5 0.1 fusion.70
  181.6 0.1 fusion.43
  181.8 0.3 fusion.50
  182.0 0.5 fusion.71
  182.6 0.3 fusion.42
  182.9 0.3 fusion.29
  183.2 0.1 convert_element_type.116
  183.3 0.1 copy.46
  183.4 15.1 %all_to_all.44 = bf16[8,32,512]{2,0,1:T(8,128)(2,1)S(1)} all-to-all(bf16[8,32,512]{2,0,1:T(8,128)(2,1)S(1)} %bitcast.135), channel_id=1, replica_groups=mesh['x'=4,'yh'=4,'yl'=2,'z'=8,'c'=2] {'yl','z','c'}, dimensions={1} | all-to-all | bytes 524288 | tf_op jit(solution)/shard_map/all_to_all | solution.py:141
  198.6 2.5 fusion.4
  201.1 0.3 copy-done.1
  201.4 0.7 fusion.3
  202.1 1.2 copy.50
  203.3 0.7 copy.51
  204.0 53.3 %all_to_all.45 = bf16[16,256,256]{2,1,0:T(8,128)(2,1)} all-to-all(bf16[16,256,256]{2,1,0:T(8,128)(2,1)S(1)} %copy.51), channel_id=1, replica_groups=mesh['x'=4,'yh'=4,'yl'=2,'z'=8,'c'=2] {'yl','z'}, dimensions={0} | all-to-all | bytes 4194304 | tf_op jit(solution)/shard_map/all_to_all | solution.py:155
  257.4 2.6 reduce_sum.55
  (34 shorter events, 0.3 us)
Async XLA Ops:
  6.5 17.1 %copy-start = (bf16[32,2,8,1024]{3,2,1,0:T(8,128)(2,1)S(1)}, bf16[32,2,8,1024]{3,2,1,0:T(8,128)(2,1)}, u32[]{:S(2)}) copy-start(bf16[32,2,8,1024]{3,2,1,0:T(8,128)(2,1)} %param.12) | copy-start | bytes 3145732
  12.3 9.4 %copy-start.2 = (bf16[8192]{0:T(1024)(128)(2,1)S(1)}, bf16[8192]{0:T(1024)(128)(2,1)}, u32[]{:S(2)}) copy-start(bf16[8192]{0:T(1024)(128)(2,1)} %param.9) | copy-start | bytes 49156
  12.3 10.0 %copy-start.4 = (s32[1024,1]{0,1:T(1,128)S(1)}, s32[1024,1]{0,1:T(1,128)}, u32[]{:S(2)}) copy-start(s32[1024,1]{0,1:T(1,128)} %param.14) | copy-start | bytes 12292
  12.3 10.9 %copy-start.3 = (s32[1024]{0:T(1024)S(1)}, s32[1024]{0:T(1024)}, u32[]{:S(2)}) copy-start(s32[1024]{0:T(1024)} %param.15) | copy-start | bytes 12292
  14.4 37.0 %all-to-all-start = ((bf16[4,512,320]{1,2,0:T(8,128)(2,1)}), bf16[4,512,320]{1,2,0:T(8,128)(2,1)S(1)}, u32[]{:S(2)}, u32[]{:S(2)}) async-start(bf16[4,512,320]{1,2,0:T(8,128)(2,1)} %broadcast_in_dim.19), calls=%async_computation | async-start | bytes 2621440 | tf_op jit(solution)/shard_map/all_to_all | solution.py:38
  21.0 177.6 %all-gather.2.cloned.1.call-start = ((), (), s32[]{:S(2)}) async-start(), calls=%async_computation.6 | async-start | bytes 4456448 | tf_op jit(solution)/shard_map/all_gather | solution.py:78
  51.4 110.4 %all-to-all-start.2 = ((bf16[32,2,2,8,1024]{4,3,2,1,0:T(8,128)(2,1)}), bf16[32,2,2,8,1024]{4,3,2,1,0:T(8,128)(2,1)}, u32[]{:S(2)}, u32[]{:S(2)}) async-start(bf16[32,2,2,8,1024]{4,3,2,1,0:T(8,128)(2,1)} %bitcast.130), calls=%async_computation.2 | async-start | bytes 4194304 | tf_op jit(solution)/shard_map/all_to_all | solution.py:118
  78.9 7.4 %copy-start.5 = (s32[256]{0:T(256)S(1)}, s32[256]{0:T(256)}, u32[]{:S(2)}) copy-start(s32[256]{0:T(256)} %param.13) | copy-start | bytes 3076
  80.2 48.5 %collective-permute-start.1 = (bf16[2048,320]{0,1:T(8,128)(2,1)}, bf16[2048,320]{0,1:T(8,128)(2,1)}, u32[]{:S(2)}, u32[]{:S(2)}) collective-permute-start(bf16[2048,320]{0,1:T(8,128)(2,1)} %bitcast.50), channel_id=1, source_target_pairs={{0,128},{128,256},{256,384},{384,0},{1,129},{129,257},{257,385},{3... | collective-permute-start | bytes 3932168 | tf_op jit(solution)/shard_map/ppermute | solution.py:88
  82.6 52.4 %collective-permute-start = (bf16[2048,320]{0,1:T(8,128)(2,1)}, bf16[2048,320]{0,1:T(8,128)(2,1)}, u32[]{:S(2)}, u32[]{:S(2)}) collective-permute-start(bf16[2048,320]{0,1:T(8,128)(2,1)} %bitcast.50), channel_id=1, source_target_pairs={{0,384},{128,0},{256,128},{384,256},{1,385},{129,1},{257,129},{385... | collective-permute-start | bytes 3932168 | tf_op jit(solution)/shard_map/ppermute | solution.py:89
  130.6 18.6 %collective-permute-start.2 = (bf16[1024,320]{0,1:T(8,128)(2,1)}, bf16[1024,320]{0,1:T(8,128)(2,1)}, u32[]{:S(2)}, u32[]{:S(2)}) collective-permute-start(bf16[1024,320]{0,1:T(8,128)(2,1)} %slice.64), channel_id=1, source_target_pairs={{0,128},{128,256},{256,384},{384,0},{1,129},{129,257},{257,385},{3... | collective-permute-start | bytes 1966088 | tf_op jit(solution)/shard_map/ppermute | solution.py:92
  136.9 19.6 %collective-permute-start.3 = (bf16[1024,320]{0,1:T(8,128)(2,1)}, bf16[1024,320]{0,1:T(8,128)(2,1)}, u32[]{:S(2)}, u32[]{:S(2)}) collective-permute-start(bf16[1024,320]{0,1:T(8,128)(2,1)} %slice.65), channel_id=1, source_target_pairs={{0,384},{128,0},{256,128},{384,256},{1,385},{129,1},{257,129},{385... | collective-permute-start | bytes 1966088 | tf_op jit(solution)/shard_map/ppermute | solution.py:92
  161.8 19.2 %all-to-all-start.1 = ((bf16[8,32,320]{2,0,1:T(8,128)(2,1)}), bf16[8,32,320]{2,0,1:T(8,128)(2,1)S(1)}, u32[]{:S(2)}, u32[]{:S(2)}) async-start(bf16[8,32,320]{2,0,1:T(8,128)(2,1)} %fusion.25), calls=%async_computation.1 | async-start | bytes 393216 | tf_op jit(solution)/shard_map/all_to_all | solution.py:33
  198.6 2.8 %copy-start.1 = (bf16[512,16,256]{2,0,1:T(8,128)(2,1)S(1)}, bf16[512,16,256]{2,0,1:T(8,128)(2,1)}, u32[]{:S(2)}) copy-start(bf16[512,16,256]{2,0,1:T(8,128)(2,1)} %all-gather.2.cloned.1.call-done) | copy-start | bytes 12582916
Sparse Core Ops, SparseCore 0:
  24.8 110.7 all-gather.1

commit v4 on v3

--- a/solution.py
+++ b/solution.py
@@ -38,6 +38,19 @@
     return lax.all_to_all(copies, axis, 0, 0, tiled=True).reshape((-1,) + tile.shape[1:])
 
 
+def ring_gather(piece, axis, count):
+    ahead = [(i, (i + 1) % count) for i in range(count)]
+    behind = [(i, (i - 1) % count) for i in range(count)]
+    from_left = lax.ppermute(piece, axis, ahead)
+    from_right = lax.ppermute(piece, axis, behind)
+    cut = piece.shape[0] // 2
+    far = jnp.concatenate(
+        [lax.ppermute(from_left[:cut], axis, ahead), lax.ppermute(from_right[cut:], axis, behind)],
+        axis=0,
+    )
+    return [piece, from_right, far, from_left]
+
+
 def attend(queries, fresh_key, value_new, keys, values, positions):
     beams = queries.shape[0]
     grouped_heads = queries.reshape(beams, KVH, QH // KVH, HD)
@@ -73,33 +86,32 @@
     my_column = lax.axis_index(BEAM)
     grouped_row_block = hidden.shape[0]
     own_beams = grouped_row_block // columns
-    halves = w_out.reshape(w_out.shape[0], lax.axis_size("c"), w_out.shape[1] // lax.axis_size("c"))
-    w_local = lax.all_to_all(halves, "c", 1, 0, tiled=True).reshape(-1, halves.shape[2])
-    w_pair = lax.all_gather(w_local, OWNER, axis=1, tiled=False)
+    cores = lax.axis_size("c")
+    core = lax.axis_index("c")
+    halves = w_out.reshape(w_out.shape[0], cores, w_out.shape[1] // cores)
+    assert cores == 2
+    mine = jnp.take(halves, core, axis=1)
+    other = lax.ppermute(jnp.take(halves, 1 - core, axis=1), "c", [(0, 1), (1, 0)])
+    w_local = jnp.where(core == 0, jnp.concatenate([mine, other], 0), jnp.concatenate([other, mine], 0))
+    w_pair = lax.all_gather(w_local[:, None], OWNER, axis=1, tiled=True)
     floats = hidden.astype(jnp.float32)
     scale_rms = lax.rsqrt(jnp.mean(floats * floats, axis=-1, keepdims=True) + 1e-05)
     normed = (floats * scale_rms * norm_gain.astype(jnp.float32)).astype(jnp.bfloat16)
-    stack = gather_rows(w_qkv, "yh", lax.axis_size("yh"))
     xs = lax.axis_size("x")
-    assert xs == 4
-    me = lax.axis_index("x")
-    ahead = [(i, (i + 1) % xs) for i in range(xs)]
-    behind = [(i, (i - 1) % xs) for i in range(xs)]
-    from_left = lax.ppermute(stack, "x", ahead)
-    from_right = lax.ppermute(stack, "x", behind)
-    cut = stack.shape[0] // 2
-    far = jnp.concatenate(
-        [lax.ppermute(from_left[:cut], "x", ahead), lax.ppermute(from_right[cut:], "x", behind)],
-        axis=0,
-    )
+    ys = lax.axis_size("yh")
+    assert xs == 4 and ys == 4
+    near = ring_gather(w_qkv, "yh", ys)
+    stack = jnp.concatenate(near, axis=0)
+    ordered = normed.reshape(normed.shape[0], xs, ys, w_qkv.shape[0])
+    ordered = jnp.roll(ordered, -lax.axis_index("x"), axis=1)
+    ordered = jnp.roll(ordered, -lax.axis_index("yh"), axis=2)
+    ordered = ordered.reshape(columns, own_beams, xs, ys * w_qkv.shape[0])
     rows = stack.shape[0]
     projected = None
-    for step, piece in ((0, stack), (1, from_right), (3, from_left), (2, far)):
-        start = ((me + step) % xs) * rows
-        block = lax.dynamic_slice_in_dim(normed, start, rows, axis=1)
+    for step, piece in zip((0, 1, 2, 3), ring_gather(stack, "x", xs)):
         term = jnp.einsum(
             "jbd,dc->bjc",
-            block.reshape(columns, own_beams, rows),
+            ordered[:, :, step],
             piece,
             preferred_element_type=jnp.float32,
         )
@@ -134,7 +146,6 @@
     queries = rotary_embed(query_cols, positions).astype(jnp.bfloat16)
     fresh_key = rotary_embed(key_cols, positions).astype(jnp.bfloat16)
     attn = attend(queries, fresh_key, value_new, keys, values, positions)
-    cores = lax.axis_size("c")
     pairs = columns // cores
     pair_feats = attn.reshape(own_beams, pairs, 1, cores * attn.shape[1] // columns)
     doubled = jnp.broadcast_to(pair_feats, (own_beams, pairs, cores, pair_feats.shape[3]))

time: 268 us -> 322 us (1.20)
  the two profiles are of different devices: /device:TPU:30 before, /device:TPU:56 now
where the time goes in v4:
time: 322 us; the launch traced here: 320 us
  waiting for transfers between devices  78.2 us (24%)
  blocking collectives  74.2 us (23%)
  local copies, waits for them, and re-layouts  58.9 us (18%)
  starting transfers between devices  50 us (16%)
  other arithmetic  32.3 us (10%)
  between operations  13.9 us (4%)
  matrix products  12.3 us (4%)
    all_to_all x1, blocking collectives, shards(): spread = lax.all_to_all(partial.transpose(1, 0, 2), PAIR, 0, 0, tiled=True)  53.2 us
    all_to_all x1, waiting for transfers between devices, shards(): lax.all_to_all(outgoing, BEAM, split_axis=0, concat_axis=0, tiled=True)  43.9 us
    all_to_all x1, blocking collectives, shards(): lax.all_to_all(doubled.reshape(own_beams, columns, pair_feats.shape[3]),...  20.9 us
    all_to_all x1, waiting for transfers between devices, regroup(): return lax.all_to_all(blocks, BEAM, split_axis=1, concat_axis=1, tiled=True)  17.3 us
    slice x1, local copies, waits for them, and re-layouts, shards(): ordered[:, :, step]  15.7 us
    unnamed x43, local copies, waits for them, and re-layouts  15.2 us
    all_to_all x1, starting transfers between devices, regroup(): return lax.all_to_all(blocks, BEAM, split_axis=1, concat_axis=1, tiled=True)  13.9 us
    concatenate x1, other arithmetic, shards(): ordered = jnp.roll(ordered, -lax.axis_index('yh'), axis=2)  10.9 us
  transfers between devices with their start and end apart: 12, of which 5 were waited for; matrix products, arithmetic and copies ran while one was open for 30% of the time, Pallas kernels for 0%

profile of v4, /device:TPU:56, one launch (start us, length us, event | category | flops | bytes accessed | tf_op | source)
XLA Modules:
  0.0 319.8 jit_solution(15417866532188677634)
XLA Ops:
  6.5 4.2 %collective-permute-start.1 = (bf16[512,320]{0,1:T(8,128)(2,1)}, bf16[512,320]{0,1:T(8,128)(2,1)S(1)}, u32[]{:S(2)}, u32[]{:S(2)}) collective-permute-start(bf16[512,320]{0,1:T(8,128)(2,1)} %param.12), channel_id=1, source_target_pairs={{0,96},{32,0},{64,32},{96,64},{1,97},{33,1},{65,33},{97,65},{2,98}... | collective-permute-start | bytes 983048 | tf_op jit(solution)/shard_map/ppermute | solution.py:45
  10.7 3.9 %collective-permute-start.2 = (bf16[512,320]{0,1:T(8,128)(2,1)}, bf16[512,320]{0,1:T(8,128)(2,1)S(1)}, u32[]{:S(2)}, u32[]{:S(2)}) collective-permute-start(bf16[512,320]{0,1:T(8,128)(2,1)} %param.12), channel_id=1, source_target_pairs={{0,32},{32,64},{64,96},{96,0},{1,33},{33,65},{65,97},{97,1},{2,34}... | collective-permute-start | bytes 983048 | tf_op jit(solution)/shard_map/ppermute | solution.py:44
  14.6 1.1 copy.63
  15.8 1.9 collective-permute-start
  17.8 0.7 convert_element_type.103
  18.5 3.3 %fusion = f32[256]{0:T(256)S(1)} fusion(bf16[256,8192]{1,0:T(8,128)(2,1)} %param.10), kind=kLoop, calls=%fused_computation.4 | loop fusion | flops 6291200 | bytes 4195328 | tf_op jit(solution)/shard_map/reduce_sum | solution.py:98
  21.9 3.2 fusion.2
  25.1 7.8 %reshape.275 = bf16[256,4,4,512]{3,2,1,0:T(4,128)(2,1)} reshape(bf16[256,8192]{1,0:T(8,128)(2,1)} %fusion.2) | data formatting | bytes 8388608 | tf_op jit(solution)/shard_map/reshape | solution.py:105
  32.9 7.8 %fusion.4 = bf16[256,4,4,512]{3,2,1,0:T(4,128)(2,1)} fusion(s32[]{:T(128)S(6)} %select_n.82, bf16[256,4,4,512]{3,2,1,0:T(4,128)(2,1)} %reshape.275), kind=kLoop, calls=%fused_computation.12 | loop fusion | flops 2097152 | bytes 8388612 | tf_op jit(solution)/shard_map/jit(_roll_dynamic)/concatenate | solution.py:106
  40.7 10.9 %fusion.3 = bf16[256,4,4,512]{3,2,1,0:T(4,128)(2,1)} fusion(s32[]{:T(128)S(6)} %select_n.84, bf16[256,4,4,512]{3,2,1,0:T(4,128)(2,1)} %fusion.4), kind=kLoop, calls=%fused_computation.11 | loop fusion | flops 8388608 | bytes 8388612 | tf_op jit(solution)/shard_map/jit(_roll_dynamic)/concatenate | solution.py:107
  51.7 1.9 collective-permute-start.3
  53.6 0.8 constant_dynamic-update-slice_fusion.4
  54.4 7.6 %reshape.374 = bf16[32,8,4,2048]{3,2,1,0:T(4,128)(2,1)} reshape(bf16[256,4,4,512]{3,2,1,0:T(4,128)(2,1)} %fusion.3) | data formatting | bytes 8388608 | tf_op jit(solution)/shard_map/reshape | solution.py:108
  62.0 0.5 broadcast.203
  62.5 0.7 reduce.4
  63.2 0.7 reshape.278
  63.9 4.8 %collective-permute-start.4 = (bf16[256,320]{0,1:T(8,128)(2,1)S(1)}, bf16[256,320]{0,1:T(8,128)(2,1)S(1)}, u32[]{:S(2)}, u32[]{:S(2)}) collective-permute-start(bf16[256,320]{0,1:T(8,128)(2,1)S(1)} %slice.99), channel_id=1, source_target_pairs={{0,96},{32,0},{64,32},{96,64},{1,97},{33,1},{65,33},{97,65},{2,98}... | collective-permute-start | bytes 491528 | tf_op jit(solution)/shard_map/ppermute | solution.py:48
  68.7 0.8 constant_dynamic-update-slice_fusion.3
  69.5 0.7 constant_dynamic-update-slice_fusion.2
  70.2 4.4 %collective-permute-done.4 = bf16[256,320]{0,1:T(8,128)(2,1)S(1)} collective-permute-done((bf16[256,320]{0,1:T(8,128)(2,1)S(1)}, bf16[256,320]{0,1:T(8,128)(2,1)S(1)}, u32[]{:S(2)}, u32[]{:S(2)}) %collective-permute-start.4) | collective-permute-done | bytes 163872 | tf_op jit(solution)/shard_map/ppermute | solution.py:48
  74.6 0.7 constant_dynamic-update-slice_fusion.1
  75.2 0.8 constant_dynamic-update-slice_fusion
  76.0 4.7 %collective-permute-start.6 = (bf16[2048,320]{0,1:T(8,128)(2,1)}, bf16[2048,320]{0,1:T(8,128)(2,1)}, u32[]{:S(2)}, u32[]{:S(2)}) collective-permute-start(bf16[2048,320]{0,1:T(8,128)(2,1)} %constant_dynamic-update-slice_fusion), channel_id=1, source_target_pairs={{0,128},{128,256},{256,384},{384,0},{1,129},{129,257},{257,385},{3... | collective-permute-start | bytes 3932168 | tf_op jit(solution)/shard_map/ppermute | solution.py:44
  80.7 3.4 %collective-permute-start.5 = (bf16[2048,320]{0,1:T(8,128)(2,1)}, bf16[2048,320]{0,1:T(8,128)(2,1)}, u32[]{:S(2)}, u32[]{:S(2)}) collective-permute-start(bf16[2048,320]{0,1:T(8,128)(2,1)} %constant_dynamic-update-slice_fusion), channel_id=1, source_target_pairs={{0,384},{128,0},{256,128},{384,256},{1,385},{129,1},{257,129},{385... | collective-permute-start | bytes 3932168 | tf_op jit(solution)/shard_map/ppermute | solution.py:45
  84.1 15.7 %fusion.61 = (bf16[32,8,1,2048]{3,2,1,0:T(2,128)(2,1)S(1)}, bf16[32,8,1,2048]{3,2,1,0:T(2,128)(2,1)}, bf16[32,8,1,2048]{3,2,1,0:T(2,128)(2,1)}, bf16[32,8,1,2048]{3,2,1,0:T(2,128)(2,1)}) fusion(bf16[32,8,4,2048]{3,2,1,0:T(4,128)(2,1)} %reshape.374), kind=kLoop, calls=%fused_computation.110 | loop fusion | bytes 8388608 | tf_op jit(solution)/shard_map/slice | solution.py:114
  99.8 0.8 reduce_window_sum.22
  100.6 0.7 copy-done.10
  101.3 1.1 maximum_select_fusion
  102.4 0.8 copy.64
  103.2 0.9 broadcast_add_fusion
  104.1 3.2 copy.103
  107.3 1.6 copy.104
  108.9 1.6 copy.102
  110.5 1.6 copy.101
  112.2 1.2 slice.102
  113.4 2.6 collective-permute-start.7
  116.0 1.1 slice.103
  117.1 4.4 %collective-permute-start.8 = (bf16[1024,320]{0,1:T(8,128)(2,1)S(1)}, bf16[1024,320]{0,1:T(8,128)(2,1)}, u32[]{:S(2)}, u32[]{:S(2)}) collective-permute-start(bf16[1024,320]{0,1:T(8,128)(2,1)S(1)} %slice.103), channel_id=1, source_target_pairs={{0,384},{128,0},{256,128},{384,256},{1,385},{129,1},{257,129},{385... | collective-permute-start | bytes 1966088 | tf_op jit(solution)/shard_map/ppermute | solution.py:48
  121.9 2.3 fusion.11
  124.3 2.3 fusion.13
  126.6 9.3 %collective-permute-done.7 = bf16[1024,320]{0,1:T(8,128)(2,1)} collective-permute-done((bf16[1024,320]{0,1:T(8,128)(2,1)S(1)}, bf16[1024,320]{0,1:T(8,128)(2,1)}, u32[]{:S(2)}, u32[]{:S(2)}) %collective-permute-start.7) | collective-permute-done | bytes 655392 | tf_op jit(solution)/shard_map/ppermute | solution.py:48
  135.9 3.3 %collective-permute-done.8 = bf16[1024,320]{0,1:T(8,128)(2,1)} collective-permute-done((bf16[1024,320]{0,1:T(8,128)(2,1)S(1)}, bf16[1024,320]{0,1:T(8,128)(2,1)}, u32[]{:S(2)}, u32[]{:S(2)}) %collective-permute-start.8) | collective-permute-done | bytes 655392 | tf_op jit(solution)/shard_map/ppermute | solution.py:48
  139.2 2.2 fusion.8
  141.4 1.0 fusion.31
  142.4 0.7 copy.71
  143.1 13.9 %all-to-all-start = ((bf16[8,32,320]{2,0,1:T(8,128)(2,1)}), bf16[8,32,320]{2,0,1:T(8,128)(2,1)S(1)}, u32[]{:S(2)}, u32[]{:S(2)}) async-start(bf16[8,32,320]{2,0,1:T(8,128)(2,1)} %copy.71), calls=%async_computation | async-start | bytes 393216 | tf_op jit(solution)/shard_map/all_to_all | solution.py:33
  157.1 2.0 gather_fusion
  159.1 17.3 %all-to-all-done = bf16[8,32,320]{2,0,1:T(8,128)(2,1)S(1)} async-done(((bf16[8,32,320]{2,0,1:T(8,128)(2,1)}), bf16[8,32,320]{2,0,1:T(8,128)(2,1)S(1)}, u32[]{:S(2)}, u32[]{:S(2)}) %all-to-all-start) | async-done | bytes 163872 | tf_op jit(solution)/shard_map/all_to_all | solution.py:33
  176.5 4.1 %all-to-all-start.1 = ((bf16[32,2,2,8,1024]{4,3,2,1,0:T(8,128)(2,1)}), bf16[32,2,2,8,1024]{4,3,2,1,0:T(8,128)(2,1)S(1)}, u32[]{:S(2)}, u32[]{:S(2)}) async-start(bf16[32,2,2,8,1024]{4,3,2,1,0:T(8,128)(2,1)} %bitcast.20), calls=%async_computation.1 | async-start | bytes 4194304 | tf_op jit(solution)/shard_map/all_to_all | solution.py:130
  180.6 0.7 fusion.55
  181.7 0.7 fusion.54
  183.6 43.9 %all-to-all-done.1 = bf16[32,2,2,8,1024]{4,3,2,1,0:T(8,128)(2,1)S(1)} async-done(((bf16[32,2,2,8,1024]{4,3,2,1,0:T(8,128)(2,1)}), bf16[32,2,2,8,1024]{4,3,2,1,0:T(8,128)(2,1)S(1)}, u32[]{:S(2)}, u32[]{:S(2)}) %all-to-all-start.1) | async-done | bytes 2097184 | tf_op jit(solution)/shard_map/all_to_all | solution.py:130
  227.5 1.6 gather_fusion.1
  229.1 1.5 copy.105
  230.7 0.5 fusion.65
  231.5 0.3 fusion.30
  232.1 20.9 %all_to_all.20 = bf16[8,32,512]{2,0,1:T(8,128)(2,1)S(1)} all-to-all(bf16[8,32,512]{2,0,1:T(8,128)(2,1)S(1)} %bitcast.123), channel_id=1, replica_groups=mesh['x'=4,'yh'=4,'yl'=2,'z'=8,'c'=2] {'yl','z','c'}, dimensions={1} | all-to-all | bytes 524288 | tf_op jit(solution)/shard_map/all_to_all | solution.py:152
  253.0 2.5 fusion.6
  255.5 0.3 copy-done.4
  255.9 1.0 fusion.5
  256.8 1.2 copy.82
  258.0 0.7 copy.83
  258.7 53.2 %all_to_all.21 = bf16[16,256,256]{2,1,0:T(8,128)(2,1)S(1)} all-to-all(bf16[16,256,256]{2,1,0:T(8,128)(2,1)S(1)} %copy.83), channel_id=1, replica_groups=mesh['x'=4,'yh'=4,'yl'=2,'z'=8,'c'=2] {'yl','z'}, dimensions={0} | all-to-all | bytes 4194304 | tf_op jit(solution)/shard_map/all_to_all | solution.py:166
  312.0 1.0 reduce_sum.55
  (76 shorter events, 2.9 us)
Async XLA Ops:
  6.5 150.5 %copy-start = (bf16[32,2,8,1024]{3,2,1,0:T(8,128)(2,1)S(1)}, bf16[32,2,8,1024]{3,2,1,0:T(8,128)(2,1)}, u32[]{:S(2)}) copy-start(bf16[32,2,8,1024]{3,2,1,0:T(8,128)(2,1)} %param.14) | copy-start | bytes 3145732
  6.5 246.5 %all-gather.2.cloned.1.call-start = ((), (), s32[]{:S(2)}) async-start(), calls=%async_computation.4 | async-start | bytes 4456448 | tf_op jit(solution)/shard_map/all_gather | solution.py:96
  6.5 57.3 %collective-permute-start.1 = (bf16[512,320]{0,1:T(8,128)(2,1)}, bf16[512,320]{0,1:T(8,128)(2,1)S(1)}, u32[]{:S(2)}, u32[]{:S(2)}) collective-permute-start(bf16[512,320]{0,1:T(8,128)(2,1)} %param.12), channel_id=1, source_target_pairs={{0,96},{32,0},{64,32},{96,64},{1,97},{33,1},{65,33},{97,65},{2,98}... | collective-permute-start | bytes 983048 | tf_op jit(solution)/shard_map/ppermute | solution.py:45
  10.7 40.9 %collective-permute-start.2 = (bf16[512,320]{0,1:T(8,128)(2,1)}, bf16[512,320]{0,1:T(8,128)(2,1)S(1)}, u32[]{:S(2)}, u32[]{:S(2)}) collective-permute-start(bf16[512,320]{0,1:T(8,128)(2,1)} %param.12), channel_id=1, source_target_pairs={{0,32},{32,64},{64,96},{96,0},{1,33},{33,65},{65,97},{97,1},{2,34}... | collective-permute-start | bytes 983048 | tf_op jit(solution)/shard_map/ppermute | solution.py:44
  15.8 84.9 %collective-permute-start = (bf16[256,256]{0,1:T(8,128)(2,1)S(1)}, bf16[256,256]{0,1:T(8,128)(2,1)S(1)}, u32[]{:S(2)}, u32[]{:S(2)}) collective-permute-start(bf16[256,256]{0,1:T(8,128)(2,1)S(1)} %get-tuple-element.32), channel_id=1, source_target_pairs={{0,1},{1,0},{2,3},{3,2},{4,5},{5,4},{6,7},{7,6},{8,9},{9,8},{10,11... | collective-permute-start | bytes 393224 | tf_op jit(solution)/shard_map/ppermute | solution.py:94
  18.5 3.4 %copy-start.1 = (bf16[256,8192]{1,0:T(8,128)(2,1)S(1)}, bf16[256,8192]{1,0:T(8,128)(2,1)}, u32[]{:S(2)}) copy-start(bf16[256,8192]{1,0:T(8,128)(2,1)} %param.10) | copy-start | bytes 12582916
  40.7 12.9 %copy-start.9 = (bf16[512,320]{0,1:T(8,128)(2,1)S(1)}, bf16[512,320]{0,1:T(8,128)(2,1)}, u32[]{:S(2)}) copy-start(bf16[512,320]{0,1:T(8,128)(2,1)} %param.12) | copy-start | bytes 983044
  51.7 17.8 %collective-permute-start.3 = (bf16[256,320]{0,1:T(8,128)(2,1)S(1)}, bf16[256,320]{0,1:T(8,128)(2,1)S(1)}, u32[]{:S(2)}, u32[]{:S(2)}) collective-permute-start(bf16[256,320]{0,1:T(8,128)(2,1)S(1)} %slice.98), channel_id=1, source_target_pairs={{0,32},{32,64},{64,96},{96,0},{1,33},{33,65},{65,97},{97,1},{2,34}... | collective-permute-start | bytes 491528 | tf_op jit(solution)/shard_map/ppermute | solution.py:48
  54.4 8.1 %copy-start.14 = (s32[1024,1]{0,1:T(1,128)S(1)}, s32[1024,1]{0,1:T(1,128)}, u32[]{:S(2)}) copy-start(s32[1024,1]{0,1:T(1,128)} %param.16) | copy-start | bytes 12292
  63.9 10.7 %collective-permute-start.4 = (bf16[256,320]{0,1:T(8,128)(2,1)S(1)}, bf16[256,320]{0,1:T(8,128)(2,1)S(1)}, u32[]{:S(2)}, u32[]{:S(2)}) collective-permute-start(bf16[256,320]{0,1:T(8,128)(2,1)S(1)} %slice.99), channel_id=1, source_target_pairs={{0,96},{32,0},{64,32},{96,64},{1,97},{33,1},{65,33},{97,65},{2,98}... | collective-permute-start | bytes 491528 | tf_op jit(solution)/shard_map/ppermute | solution.py:48
  76.0 23.8 %copy-start.12 = (s32[32,32]{1,0:T(8,128)S(1)}, s32[32,32]{1,0:T(8,128)}, u32[]{:S(2)}) copy-start(s32[32,32]{1,0:T(8,128)} %reshape.278) | copy-start | bytes 12292
  76.0 36.2 %collective-permute-start.6 = (bf16[2048,320]{0,1:T(8,128)(2,1)}, bf16[2048,320]{0,1:T(8,128)(2,1)}, u32[]{:S(2)}, u32[]{:S(2)}) collective-permute-start(bf16[2048,320]{0,1:T(8,128)(2,1)} %constant_dynamic-update-slice_fusion), channel_id=1, source_target_pairs={{0,128},{128,256},{256,384},{384,0},{1,129},{129,257},{257,385},{3... | collective-permute-start | bytes 3932168 | tf_op jit(solution)/shard_map/ppermute | solution.py:44
  80.7 35.3 %collective-permute-start.5 = (bf16[2048,320]{0,1:T(8,128)(2,1)}, bf16[2048,320]{0,1:T(8,128)(2,1)}, u32[]{:S(2)}, u32[]{:S(2)}) collective-permute-start(bf16[2048,320]{0,1:T(8,128)(2,1)} %constant_dynamic-update-slice_fusion), channel_id=1, source_target_pairs={{0,384},{128,0},{256,128},{384,256},{1,385},{129,1},{257,129},{385... | collective-permute-start | bytes 3932168 | tf_op jit(solution)/shard_map/ppermute | solution.py:45
  100.6 0.7 copy-start.10
  103.2 4.1 %copy-start.3 = (bf16[32,8,1,2048]{3,2,1,0:T(2,128)(2,1)S(1)}, bf16[32,8,1,2048]{3,2,1,0:T(2,128)(2,1)}, u32[]{:S(2)}) copy-start(bf16[32,8,1,2048]{3,2,1,0:T(2,128)(2,1)} %get-tuple-element.22) | copy-start | bytes 3145732
  107.3 1.6 copy-start.2
  110.5 1.6 copy-start.13
  112.1 9.8 %copy-start.8 = (bf16[32,8,1,2048]{3,1,0,2:T(8,128)(2,1)S(1)}, bf16[32,8,1,2048]{3,1,0,2:T(8,128)(2,1)}, u32[]{:S(2)}) copy-start(bf16[32,8,1,2048]{3,1,0,2:T(8,128)(2,1)} %copy.104) | copy-start | bytes 3145732
  113.4 22.6 %collective-permute-start.7 = (bf16[1024,320]{0,1:T(8,128)(2,1)S(1)}, bf16[1024,320]{0,1:T(8,128)(2,1)}, u32[]{:S(2)}, u32[]{:S(2)}) collective-permute-start(bf16[1024,320]{0,1:T(8,128)(2,1)S(1)} %slice.102), channel_id=1, source_target_pairs={{0,128},{128,256},{256,384},{384,0},{1,129},{129,257},{257,385},{3... | collective-permute-start | bytes 1966088 | tf_op jit(solution)/shard_map/ppermute | solution.py:48
  117.1 22.0 %collective-permute-start.8 = (bf16[1024,320]{0,1:T(8,128)(2,1)S(1)}, bf16[1024,320]{0,1:T(8,128)(2,1)}, u32[]{:S(2)}, u32[]{:S(2)}) collective-permute-start(bf16[1024,320]{0,1:T(8,128)(2,1)S(1)} %slice.103), channel_id=1, source_target_pairs={{0,384},{128,0},{256,128},{384,256},{1,385},{129,1},{257,129},{385... | collective-permute-start | bytes 1966088 | tf_op jit(solution)/shard_map/ppermute | solution.py:48
  121.9 2.4 copy-start.7
  124.3 14.9 %copy-start.5 = (bf16[32,8,1,2048]{3,1,0,2:T(8,128)(2,1)S(1)}, bf16[32,8,1,2048]{3,1,0,2:T(8,128)(2,1)}, u32[]{:S(2)}) copy-start(bf16[32,8,1,2048]{3,1,0,2:T(8,128)(2,1)} %copy.103) | copy-start | bytes 3145732
  126.6 14.8 %copy-start.6 = (bf16[32,8,1,2048]{3,1,0,2:T(8,128)(2,1)S(1)}, bf16[32,8,1,2048]{3,1,0,2:T(8,128)(2,1)}, u32[]{:S(2)}) copy-start(bf16[32,8,1,2048]{3,1,0,2:T(8,128)(2,1)} %copy.101) | copy-start | bytes 3145732
  126.6 14.8 %copy-start.11 = (bf16[2048,320]{0,1:T(8,128)(2,1)S(1)}, bf16[2048,320]{0,1:T(8,128)(2,1)}, u32[]{:S(2)}) copy-start(bf16[2048,320]{0,1:T(8,128)(2,1)} %constant_dynamic-update-slice_fusion) | copy-start | bytes 3932164
  143.1 33.3 %all-to-all-start = ((bf16[8,32,320]{2,0,1:T(8,128)(2,1)}), bf16[8,32,320]{2,0,1:T(8,128)(2,1)S(1)}, u32[]{:S(2)}, u32[]{:S(2)}) async-start(bf16[8,32,320]{2,0,1:T(8,128)(2,1)} %copy.71), calls=%async_computation | async-start | bytes 393216 | tf_op jit(solution)/shard_map/all_to_all | solution.py:33
  176.5 5.0 %copy-start.15 = (s32[256]{0:T(256)S(1)}, s32[256]{0:T(256)}, u32[]{:S(2)}) copy-start(s32[256]{0:T(256)} %param.15) | copy-start | bytes 3076
  176.5 51.0 %all-to-all-start.1 = ((bf16[32,2,2,8,1024]{4,3,2,1,0:T(8,128)(2,1)}), bf16[32,2,2,8,1024]{4,3,2,1,0:T(8,128)(2,1)S(1)}, u32[]{:S(2)}, u32[]{:S(2)}) async-start(bf16[32,2,2,8,1024]{4,3,2,1,0:T(8,128)(2,1)} %bitcast.20), calls=%async_computation.1 | async-start | bytes 4194304 | tf_op jit(solution)/shard_map/all_to_all | solution.py:130
  253.0 2.8 copy-start.4
Sparse Core Ops, SparseCore 0:
  103.3 89.7 all-gather.1

commit v5 on v3

--- a/solution.py
+++ b/solution.py
@@ -73,13 +73,19 @@
     my_column = lax.axis_index(BEAM)
     grouped_row_block = hidden.shape[0]
     own_beams = grouped_row_block // columns
-    halves = w_out.reshape(w_out.shape[0], lax.axis_size("c"), w_out.shape[1] // lax.axis_size("c"))
-    w_local = lax.all_to_all(halves, "c", 1, 0, tiled=True).reshape(-1, halves.shape[2])
-    w_pair = lax.all_gather(w_local, OWNER, axis=1, tiled=False)
+    cores = lax.axis_size("c")
+    core = lax.axis_index("c")
+    assert cores == 2
+    halves = w_out.reshape(w_out.shape[0], cores, w_out.shape[1] // cores)
+    mine = jnp.take(halves, core, axis=1)
+    other = lax.ppermute(jnp.take(halves, 1 - core, axis=1), "c", [(0, 1), (1, 0)])
+    w_local = jnp.where(core == 0, jnp.concatenate([mine, other], 0), jnp.concatenate([other, mine], 0))
     floats = hidden.astype(jnp.float32)
     scale_rms = lax.rsqrt(jnp.mean(floats * floats, axis=-1, keepdims=True) + 1e-05)
     normed = (floats * scale_rms * norm_gain.astype(jnp.float32)).astype(jnp.bfloat16)
     stack = gather_rows(w_qkv, "yh", lax.axis_size("yh"))
+    w_local, stack = lax.optimization_barrier((w_local, stack))
+    w_pair = lax.all_gather(w_local[:, None], OWNER, axis=1, tiled=True)
     xs = lax.axis_size("x")
     assert xs == 4
     me = lax.axis_index("x")
@@ -134,7 +140,6 @@
     queries = rotary_embed(query_cols, positions).astype(jnp.bfloat16)
     fresh_key = rotary_embed(key_cols, positions).astype(jnp.bfloat16)
     attn = attend(queries, fresh_key, value_new, keys, values, positions)
-    cores = lax.axis_size("c")
     pairs = columns // cores
     pair_feats = attn.reshape(own_beams, pairs, 1, cores * attn.shape[1] // columns)
     doubled = jnp.broadcast_to(pair_feats, (own_beams, pairs, cores, pair_feats.shape[3]))

time: 268 us -> 249 us (0.929)
  the two profiles are of different devices: /device:TPU:30 before, /device:TPU:56 now
where the time goes in v5:
time: 249 us; the launch traced here: 247 us
  waiting for transfers between devices  77.1 us (31%)
  blocking collectives  68.3 us (27%)
  starting transfers between devices  45.8 us (18%)
  local copies, waits for them, and re-layouts  19.9 us (8%)
  between operations  13.9 us (6%)
  other arithmetic  12.6 us (5%)
  matrix products  8.94 us (4%)
    all_to_all x1, blocking collectives, shards(): spread = lax.all_to_all(partial.transpose(1, 0, 2), PAIR, 0, 0, tiled=True)  53.2 us
    ppermute x1, waiting for transfers between devices, shards(): from_left = lax.ppermute(stack, 'x', ahead)  27.8 us
    ppermute x1, waiting for transfers between devices, shards(): lax.ppermute(from_left[:cut], 'x', ahead)  20.6 us
    all_to_all x1, waiting for transfers between devices, gather_rows(): lax.all_to_all(copies, axis, 0, 0, tiled=True)  17.8 us
    all_to_all x1, blocking collectives, shards(): lax.all_to_all(doubled.reshape(own_beams, columns, pair_feats.shape[3]),...  15.1 us
    all_to_all x1, starting transfers between devices, shards(): lax.all_to_all(outgoing, BEAM, split_axis=0, concat_axis=0, tiled=True)  13.9 us
    all_to_all x1, starting transfers between devices, regroup(): return lax.all_to_all(blocks, BEAM, split_axis=1, concat_axis=1, tiled=True)  8.69 us
    all_to_all x1, waiting for transfers between devices, regroup(): return lax.all_to_all(blocks, BEAM, split_axis=1, concat_axis=1, tiled=True)  7.39 us
  transfers between devices with their start and end apart: 9, of which 5 were waited for; matrix products, arithmetic and copies ran while one was open for 13% of the time, Pallas kernels for 0%

profile of v5, /device:TPU:56, one launch (start us, length us, event | category | flops | bytes accessed | tf_op | source)
XLA Modules:
  0.0 246.6 jit_solution(14115493747293617382)
XLA Ops:
  6.5 2.3 broadcast_in_dim.29
  8.8 7.1 %all-to-all-start = ((bf16[4,512,320]{1,2,0:T(8,128)(2,1)}), bf16[4,512,320]{1,2,0:T(8,128)(2,1)S(1)}, u32[]{:S(2)}, u32[]{:S(2)}) async-start(bf16[4,512,320]{1,2,0:T(8,128)(2,1)} %broadcast_in_dim.29), calls=%async_computation | async-start | bytes 2621440 | tf_op jit(solution)/shard_map/all_to_all | solution.py:38
  15.9 0.1 copy.82
  16.1 1.9 collective-permute-start
  18.0 0.5 broadcast.199
  18.5 0.7 reduce.4
  19.2 0.1 reshape.236
  19.3 0.2 reduce_window_sum.22
  19.5 0.1 mul.217
  19.6 0.1 multiply_reduce_fusion
  19.7 0.1 copy.94
  19.8 0.1 reshape.237
  19.9 3.1 %fusion = f32[256]{0:T(256)S(1)} fusion(bf16[256,8192]{1,0:T(8,128)(2,1)} %param.10), kind=kLoop, calls=%fused_computation.4 | loop fusion | flops 6291200 | bytes 4195328 | tf_op jit(solution)/shard_map/reduce_sum | solution.py:84
  23.1 2.0 gather_fusion
  25.2 0.8 maximum_select_fusion
  26.0 17.8 %all-to-all-done = bf16[4,512,320]{1,2,0:T(8,128)(2,1)S(1)} async-done(((bf16[4,512,320]{1,2,0:T(8,128)(2,1)}), bf16[4,512,320]{1,2,0:T(8,128)(2,1)S(1)}, u32[]{:S(2)}, u32[]{:S(2)}) %all-to-all-start) | async-done | bytes 1310752 | tf_op jit(solution)/shard_map/all_to_all | solution.py:38
  43.8 13.9 %all-to-all-start.2 = ((bf16[32,2,2,8,1024]{4,3,2,1,0:T(8,128)(2,1)}), bf16[32,2,2,8,1024]{4,3,2,1,0:T(8,128)(2,1)}, u32[]{:S(2)}, u32[]{:S(2)}) async-start(bf16[32,2,2,8,1024]{4,3,2,1,0:T(8,128)(2,1)} %bitcast.19), calls=%async_computation.2 | async-start | bytes 4194304 | tf_op jit(solution)/shard_map/all_to_all | solution.py:124
  57.8 1.3 copy.118
  59.2 5.4 %fusion.2 = bf16[256,8192]{1,0:T(8,128)(2,1)} fusion(bf16[256,8192]{1,0:T(8,128)(2,1)} %param.10, f32[8192]{0:T(1024)S(1)} %convert_element_type.103, f32[256]{0:T(256)S(1)} %add_rsqrt_fusion), kind=kLoop, calls=%fused_computation.6 | loop fusion | flops 8388608 | bytes 8422400 | tf_op jit(solution)/shard_map/convert_element_type | solution.py:85
  64.6 3.4 %collective-permute-start.2 = (bf16[2048,320]{0,1:T(8,128)(2,1)S(1)}, bf16[2048,320]{0,1:T(8,128)(2,1)}, u32[]{:S(2)}, u32[]{:S(2)}) collective-permute-start(bf16[2048,320]{0,1:T(8,128)(2,1)S(1)} %bitcast.122), channel_id=1, source_target_pairs={{0,128},{128,256},{256,384},{384,0},{1,129},{129,257},{257,385},{3... | collective-permute-start | bytes 3932168 | tf_op jit(solution)/shard_map/ppermute | solution.py:94
  68.0 3.7 %collective-permute-start.1 = (bf16[2048,320]{0,1:T(8,128)(2,1)S(1)}, bf16[2048,320]{0,1:T(8,128)(2,1)}, u32[]{:S(2)}, u32[]{:S(2)}) collective-permute-start(bf16[2048,320]{0,1:T(8,128)(2,1)S(1)} %bitcast.123), channel_id=1, source_target_pairs={{0,384},{128,0},{256,128},{384,256},{1,385},{129,1},{257,129},{385... | collective-permute-start | bytes 3932168 | tf_op jit(solution)/shard_map/ppermute | solution.py:95
  71.7 0.1 fusion.52
  71.7 0.1 reduce_window_sum.23
  71.8 0.1 fusion.61
  71.9 0.2 select_reduce_fusion
  72.1 0.1 iota_compare_fusion.2
  72.2 0.1 multiply_cosine_fusion
  72.3 2.8 %dynamic-slice_bitcast_fusion.2 = (bf16[32,8,2048]{2,1,0:T(8,128)(2,1)S(1)}, bf16[32,8,2048]{2,1,0:T(8,128)(2,1)S(1)}, bf16[32,8,2048]{2,1,0:T(8,128)(2,1)S(1)}, bf16[32,8,2048]{2,1,0:T(8,128)(2,1)S(1)}) fusion(bf16[256,8192]{1,0:T(8,128)(2,1)} %fusion.2, s32[]{:T(128)S(6)} %select_n.85, s32[]{:T(128)S(6)} %select_n.89, s32[]{:T(128)S(6)} %select_n.87, ...), kind=kLoop, calls=%fused_computation.34 | loop fusion | bytes 8388624 | tf_op jit(solution)/shard_map/reshape | solution.py:108
  75.1 27.8 %collective-permute-done.2 = bf16[2048,320]{0,1:T(8,128)(2,1)} collective-permute-done((bf16[2048,320]{0,1:T(8,128)(2,1)S(1)}, bf16[2048,320]{0,1:T(8,128)(2,1)}, u32[]{:S(2)}, u32[]{:S(2)}) %collective-permute-start.2) | collective-permute-done | bytes 1310752 | tf_op jit(solution)/shard_map/ppermute | solution.py:94
  102.9 1.1 slice.76
  104.0 2.2 collective-permute-start.3
  106.2 1.1 slice.77
  107.3 4.9 %collective-permute-start.4 = (bf16[1024,320]{0,1:T(8,128)(2,1)S(1)}, bf16[1024,320]{0,1:T(8,128)(2,1)S(1)}, u32[]{:S(2)}, u32[]{:S(2)}) collective-permute-start(bf16[1024,320]{0,1:T(8,128)(2,1)S(1)} %slice.77), channel_id=1, source_target_pairs={{0,384},{128,0},{256,128},{384,256},{1,385},{129,1},{257,129},{385... | collective-permute-start | bytes 1966088 | tf_op jit(solution)/shard_map/ppermute | solution.py:98
  112.2 0.9 fusion.11
  113.1 2.2 fusion.7
  115.3 20.6 %collective-permute-done.3 = bf16[1024,320]{0,1:T(8,128)(2,1)S(1)} collective-permute-done((bf16[1024,320]{0,1:T(8,128)(2,1)S(1)}, bf16[1024,320]{0,1:T(8,128)(2,1)S(1)}, u32[]{:S(2)}, u32[]{:S(2)}) %collective-permute-start.3) | collective-permute-done | bytes 655392 | tf_op jit(solution)/shard_map/ppermute | solution.py:98
  136.0 3.4 %collective-permute-done.4 = bf16[1024,320]{0,1:T(8,128)(2,1)S(1)} collective-permute-done((bf16[1024,320]{0,1:T(8,128)(2,1)S(1)}, bf16[1024,320]{0,1:T(8,128)(2,1)S(1)}, u32[]{:S(2)}, u32[]{:S(2)}) %collective-permute-start.4) | collective-permute-done | bytes 655392 | tf_op jit(solution)/shard_map/ppermute | solution.py:98
  139.4 0.9 fusion.4
  140.3 2.3 fusion.27
  142.6 0.7 copy.90
  143.4 8.7 %all-to-all-start.1 = ((bf16[8,32,320]{2,0,1:T(8,128)(2,1)}), bf16[8,32,320]{2,0,1:T(8,128)(2,1)S(1)}, u32[]{:S(2)}, u32[]{:S(2)}) async-start(bf16[8,32,320]{2,0,1:T(8,128)(2,1)} %copy.90), calls=%async_computation.1 | async-start | bytes 393216 | tf_op jit(solution)/shard_map/all_to_all | solution.py:33
  152.1 2.2 gather_fusion.1
  154.3 0.3 copy.119
  154.6 0.1 fusion.63
  154.7 7.4 %all-to-all-done.1 = bf16[8,32,320]{2,0,1:T(8,128)(2,1)S(1)} async-done(((bf16[8,32,320]{2,0,1:T(8,128)(2,1)}), bf16[8,32,320]{2,0,1:T(8,128)(2,1)S(1)}, u32[]{:S(2)}, u32[]{:S(2)}) %all-to-all-start.1) | async-done | bytes 163872 | tf_op jit(solution)/shard_map/all_to_all | solution.py:33
  162.1 0.2 reshape.235
  162.3 0.1 subtract_convert_fusion.1
  162.4 0.1 maximum_bitcast_fusion.2
  162.5 0.1 fusion.65
  162.7 0.1 fusion.39
  162.8 0.3 fusion.47
  163.1 0.5 fusion.66
  163.6 0.3 fusion.38
  163.9 0.3 fusion.26
  164.2 0.1 convert_element_type.120
  164.3 0.1 copy.98
  164.5 15.1 %all_to_all.25 = bf16[8,32,512]{2,0,1:T(8,128)(2,1)S(1)} all-to-all(bf16[8,32,512]{2,0,1:T(8,128)(2,1)S(1)} %bitcast.126), channel_id=1, replica_groups=mesh['x'=4,'yh'=4,'yl'=2,'z'=8,'c'=2] {'yl','z','c'}, dimensions={1} | all-to-all | bytes 524288 | tf_op jit(solution)/shard_map/all_to_all | solution.py:146
  179.6 2.5 %fusion.62 = (bf16[256,4096]{0,1:T(8,128)(2,1)S(1)}, bf16[256,4096]{0,1:T(8,128)(2,1)S(1)}) fusion(bf16[512,4096]{0,1:T(8,128)(2,1)} %all-gather.3.cloned.1.call-done), kind=kLoop, calls=%fused_computation.100 | loop fusion | bytes 8388608 | tf_op jit(solution)/shard_map/slice | solution.py:155
  182.1 0.7 fusion.42
  182.9 0.7 fusion.3
  183.6 1.2 copy.103
  184.8 0.7 copy.104
  185.5 53.2 %all_to_all.26 = bf16[16,256,256]{2,1,0:T(8,128)(2,1)S(1)} all-to-all(bf16[16,256,256]{2,1,0:T(8,128)(2,1)S(1)} %copy.104), channel_id=1, replica_groups=mesh['x'=4,'yh'=4,'yl'=2,'z'=8,'c'=2] {'yl','z'}, dimensions={0} | all-to-all | bytes 4194304 | tf_op jit(solution)/shard_map/all_to_all | solution.py:160
  238.8 1.0 reduce_sum.55
  (39 shorter events, 0.4 us)
Async XLA Ops:
  6.5 16.6 %copy-start = (bf16[32,2,8,1024]{3,2,1,0:T(8,128)(2,1)S(1)}, bf16[32,2,8,1024]{3,2,1,0:T(8,128)(2,1)}, u32[]{:S(2)}) copy-start(bf16[32,2,8,1024]{3,2,1,0:T(8,128)(2,1)} %param.14) | copy-start | bytes 3145732
  6.5 9.4 %copy-start.2 = (bf16[256,512]{1,0:T(8,128)(2,1)S(1)}, bf16[256,512]{1,0:T(8,128)(2,1)}, u32[]{:S(2)}) copy-start(bf16[256,512]{1,0:T(8,128)(2,1)} %param.13) | copy-start | bytes 786436
  8.8 9.8 %copy-start.5 = (s32[1024,1]{0,1:T(1,128)S(1)}, s32[1024,1]{0,1:T(1,128)}, u32[]{:S(2)}) copy-start(s32[1024,1]{0,1:T(1,128)} %param.16) | copy-start | bytes 12292
  8.8 10.7 %copy-start.4 = (s32[1024]{0:T(1024)S(1)}, s32[1024]{0:T(1024)}, u32[]{:S(2)}) copy-start(s32[1024]{0:T(1024)} %param.17) | copy-start | bytes 12292
  8.8 35.0 %all-to-all-start = ((bf16[4,512,320]{1,2,0:T(8,128)(2,1)}), bf16[4,512,320]{1,2,0:T(8,128)(2,1)S(1)}, u32[]{:S(2)}, u32[]{:S(2)}) async-start(bf16[4,512,320]{1,2,0:T(8,128)(2,1)} %broadcast_in_dim.29), calls=%async_computation | async-start | bytes 2621440 | tf_op jit(solution)/shard_map/all_to_all | solution.py:38
  16.1 9.1 %collective-permute-start = (bf16[256,256]{0,1:T(8,128)(2,1)S(1)}, bf16[256,256]{0,1:T(8,128)(2,1)S(1)}, u32[]{:S(2)}, u32[]{:S(2)}) collective-permute-start(bf16[256,256]{0,1:T(8,128)(2,1)S(1)} %get-tuple-element.38), channel_id=1, source_target_pairs={{0,1},{1,0},{2,3},{3,2},{4,5},{5,4},{6,7},{7,6},{8,9},{9,8},{10,11... | collective-permute-start | bytes 393224 | tf_op jit(solution)/shard_map/ppermute | solution.py:81
  19.9 3.2 %copy-start.3 = (bf16[8192]{0:T(1024)(128)(2,1)S(1)}, bf16[8192]{0:T(1024)(128)(2,1)}, u32[]{:S(2)}) copy-start(bf16[8192]{0:T(1024)(128)(2,1)} %param.11) | copy-start | bytes 49156
  43.8 99.5 %all-to-all-start.2 = ((bf16[32,2,2,8,1024]{4,3,2,1,0:T(8,128)(2,1)}), bf16[32,2,2,8,1024]{4,3,2,1,0:T(8,128)(2,1)}, u32[]{:S(2)}, u32[]{:S(2)}) async-start(bf16[32,2,2,8,1024]{4,3,2,1,0:T(8,128)(2,1)} %bitcast.19), calls=%async_computation.2 | async-start | bytes 4194304 | tf_op jit(solution)/shard_map/all_to_all | solution.py:124
  57.8 121.9 %all-gather.3.cloned.1.call-start = ((), (), s32[]{:S(2)}) async-start(), calls=%async_computation.5 | async-start | bytes 4456448 | tf_op jit(solution)/shard_map/all_gather | solution.py:88
  59.1 5.5 %copy-start.1 = (bf16[4,40,8,512]{3,2,0,1:T(8,128)(2,1)S(1)}, bf16[4,40,8,512]{3,2,0,1:T(8,128)(2,1)}, u32[]{:S(2)}) copy-start(bf16[4,40,8,512]{3,2,0,1:T(8,128)(2,1)} %copy.118) | copy-start | bytes 3932164
  59.1 12.7 %copy-start.6 = (s32[256]{0:T(256)S(1)}, s32[256]{0:T(256)}, u32[]{:S(2)}) copy-start(s32[256]{0:T(256)} %param.15) | copy-start | bytes 3076
  64.6 38.2 %collective-permute-start.2 = (bf16[2048,320]{0,1:T(8,128)(2,1)S(1)}, bf16[2048,320]{0,1:T(8,128)(2,1)}, u32[]{:S(2)}, u32[]{:S(2)}) collective-permute-start(bf16[2048,320]{0,1:T(8,128)(2,1)S(1)} %bitcast.122), channel_id=1, source_target_pairs={{0,128},{128,256},{256,384},{384,0},{1,129},{129,257},{257,385},{3... | collective-permute-start | bytes 3932168 | tf_op jit(solution)/shard_map/ppermute | solution.py:94
  68.0 38.2 %collective-permute-start.1 = (bf16[2048,320]{0,1:T(8,128)(2,1)S(1)}, bf16[2048,320]{0,1:T(8,128)(2,1)}, u32[]{:S(2)}, u32[]{:S(2)}) collective-permute-start(bf16[2048,320]{0,1:T(8,128)(2,1)S(1)} %bitcast.123), channel_id=1, source_target_pairs={{0,384},{128,0},{256,128},{384,256},{1,385},{129,1},{257,129},{385... | collective-permute-start | bytes 3932168 | tf_op jit(solution)/shard_map/ppermute | solution.py:95
  104.0 32.0 %collective-permute-start.3 = (bf16[1024,320]{0,1:T(8,128)(2,1)S(1)}, bf16[1024,320]{0,1:T(8,128)(2,1)S(1)}, u32[]{:S(2)}, u32[]{:S(2)}) collective-permute-start(bf16[1024,320]{0,1:T(8,128)(2,1)S(1)} %slice.76), channel_id=1, source_target_pairs={{0,128},{128,256},{256,384},{384,0},{1,129},{129,257},{257,385},{3... | collective-permute-start | bytes 1966088 | tf_op jit(solution)/shard_map/ppermute | solution.py:98
  107.3 32.1 %collective-permute-start.4 = (bf16[1024,320]{0,1:T(8,128)(2,1)S(1)}, bf16[1024,320]{0,1:T(8,128)(2,1)S(1)}, u32[]{:S(2)}, u32[]{:S(2)}) collective-permute-start(bf16[1024,320]{0,1:T(8,128)(2,1)S(1)} %slice.77), channel_id=1, source_target_pairs={{0,384},{128,0},{256,128},{384,256},{1,385},{129,1},{257,129},{385... | collective-permute-start | bytes 1966088 | tf_op jit(solution)/shard_map/ppermute | solution.py:98
  143.4 18.7 %all-to-all-start.1 = ((bf16[8,32,320]{2,0,1:T(8,128)(2,1)}), bf16[8,32,320]{2,0,1:T(8,128)(2,1)S(1)}, u32[]{:S(2)}, u32[]{:S(2)}) async-start(bf16[8,32,320]{2,0,1:T(8,128)(2,1)} %copy.90), calls=%async_computation.1 | async-start | bytes 393216 | tf_op jit(solution)/shard_map/all_to_all | solution.py:33
Sparse Core Ops, SparseCore 0:
  61.6 83.4 all-gather.2

commit v6 on v5

--- a/solution.py
+++ b/solution.py
@@ -84,8 +84,6 @@
     scale_rms = lax.rsqrt(jnp.mean(floats * floats, axis=-1, keepdims=True) + 1e-05)
     normed = (floats * scale_rms * norm_gain.astype(jnp.float32)).astype(jnp.bfloat16)
     stack = gather_rows(w_qkv, "yh", lax.axis_size("yh"))
-    w_local, stack = lax.optimization_barrier((w_local, stack))
-    w_pair = lax.all_gather(w_local[:, None], OWNER, axis=1, tiled=True)
     xs = lax.axis_size("x")
     assert xs == 4
     me = lax.axis_index("x")
@@ -93,6 +91,8 @@
     behind = [(i, (i - 1) % xs) for i in range(xs)]
     from_left = lax.ppermute(stack, "x", ahead)
     from_right = lax.ppermute(stack, "x", behind)
+    w_local, from_left, from_right = lax.optimization_barrier((w_local, from_left, from_right))
+    w_pair = lax.all_gather(w_local[:, None], OWNER, axis=1, tiled=True)
     cut = stack.shape[0] // 2
     far = jnp.concatenate(
         [lax.ppermute(from_left[:cut], "x", ahead), lax.ppermute(from_right[cut:], "x", behind)],

time: 249 us -> 248 us (level)
  waiting for transfers between devices: 77.1 us -> 52.4 us
  blocking collectives: 68.3 us -> 77.1 us
  starting transfers between devices: 45.8 us -> 52 us
  local copies, waits for them, and re-layouts: 19.9 us -> 25.7 us
  matrix products: 8.94 us -> 12.8 us
    ppermute x1, waiting for transfers between devices: 27.8 us -> 0.01 us  [shards(): from_left = lax.ppermute(stack, 'x', ahead)]
    ppermute x1, waiting for transfers between devices: 20.6 us -> 1.16 us  [shards(): lax.ppermute(from_left[:cut], 'x', ahead)]
    all_to_all x1, waiting for transfers between devices: 7.39 us -> 15.5 us  [regroup(): return lax.all_to_all(blocks, BEAM, split_axis=1, concat_axis=1, tiled=True)]
    all_to_all x1, waiting for transfers between devices: 0.01 us -> 7.18 us  [shards(): lax.all_to_all(outgoing, BEAM, split_axis=0, concat_axis=0, tiled=True)]
    all_to_all x1, starting transfers between devices: 8.69 us -> 15 us  [regroup(): return lax.all_to_all(blocks, BEAM, split_axis=1, concat_axis=1, tiled=True)]
    all_to_all x1, waiting for transfers between devices: 17.8 us -> 23.9 us  [gather_rows(): lax.all_to_all(copies, axis, 0, 0, tiled=True)]
    all_to_all x1, blocking collectives: 15.1 us -> 20.7 us  [shards(): lax.all_to_all(doubled.reshape(own_beams, columns, pair_feats.shape[3]),...]
    dot_general x4, matrix products: 6.32 us -> 10.1 us  [shards(): jnp.einsum('jbd,dc->bjc', block.reshape(columns, own_beams, rows), piece,...]
  transfers between devices with their start and end apart: 9 -> 9, of which waited for: 5 -> 5; matrix products, arithmetic and copies ran while one was open for 13% -> 16% of each run, Pallas kernels for 0% -> 0%
where the time goes in v6:
time: 248 us; the launch traced here: 246 us
  blocking collectives  77.1 us (31%)
  waiting for transfers between devices  52.4 us (21%)
  starting transfers between devices  52 us (21%)
  local copies, waits for them, and re-layouts  25.7 us (10%)
  between operations  13.9 us (6%)
  matrix products  12.8 us (5%)
  other arithmetic  12.4 us (5%)
    all_to_all x1, blocking collectives, shards(): spread = lax.all_to_all(partial.transpose(1, 0, 2), PAIR, 0, 0, tiled=True)  56.4 us
    all_to_all x1, waiting for transfers between devices, gather_rows(): lax.all_to_all(copies, axis, 0, 0, tiled=True)  23.9 us
    all_to_all x1, blocking collectives, shards(): lax.all_to_all(doubled.reshape(own_beams, columns, pair_feats.shape[3]),...  20.7 us
    all_to_all x1, waiting for transfers between devices, regroup(): return lax.all_to_all(blocks, BEAM, split_axis=1, concat_axis=1, tiled=True)  15.5 us
    all_to_all x1, starting transfers between devices, regroup(): return lax.all_to_all(blocks, BEAM, split_axis=1, concat_axis=1, tiled=True)  15 us
    all_to_all x1, starting transfers between devices, shards(): lax.all_to_all(outgoing, BEAM, split_axis=0, concat_axis=0, tiled=True)  13.9 us
    dot_general x4, matrix products, shards(): jnp.einsum('jbd,dc->bjc', block.reshape(columns, own_beams, rows), piece,...  10.1 us
    all_to_all x1, waiting for transfers between devices, shards(): lax.all_to_all(outgoing, BEAM, split_axis=0, concat_axis=0, tiled=True)  7.18 us
  transfers between devices with their start and end apart: 9, of which 5 were waited for; matrix products, arithmetic and copies ran while one was open for 16% of the time, Pallas kernels for 0%

profile of v6, /device:TPU:56, one launch (start us, length us, event | category | flops | bytes accessed | tf_op | source)
XLA Modules:
  0.0 246.2 jit_solution(4027103860592162126)
XLA Ops:
  6.5 2.2 broadcast_in_dim.29
  8.8 7.1 %all-to-all-start = ((bf16[4,512,320]{1,2,0:T(8,128)(2,1)}), bf16[4,512,320]{1,2,0:T(8,128)(2,1)S(1)}, u32[]{:S(2)}, u32[]{:S(2)}) async-start(bf16[4,512,320]{1,2,0:T(8,128)(2,1)} %broadcast_in_dim.29), calls=%async_computation | async-start | bytes 2621440 | tf_op jit(solution)/shard_map/all_to_all | solution.py:38
  15.9 0.1 copy.71
  16.1 1.9 collective-permute-start
  18.0 0.5 broadcast.199
  18.5 0.7 reduce.4
  19.2 0.1 reshape.236
  19.3 0.2 reduce_window_sum.22
  19.6 0.1 multiply_reduce_fusion
  19.7 0.1 copy.84
  19.8 0.1 reshape.237
  19.9 23.9 %all-to-all-done = bf16[4,512,320]{1,2,0:T(8,128)(2,1)S(1)} async-done(((bf16[4,512,320]{1,2,0:T(8,128)(2,1)}), bf16[4,512,320]{1,2,0:T(8,128)(2,1)S(1)}, u32[]{:S(2)}, u32[]{:S(2)}) %all-to-all-start) | async-done | bytes 1310752 | tf_op jit(solution)/shard_map/all_to_all | solution.py:38
  43.8 1.3 copy.108
  45.1 3.4 %collective-permute-start.1 = (bf16[2048,320]{0,1:T(8,128)(2,1)}, bf16[2048,320]{0,1:T(8,128)(2,1)}, u32[]{:S(2)}, u32[]{:S(2)}) collective-permute-start(bf16[2048,320]{0,1:T(8,128)(2,1)} %bitcast.52), channel_id=1, source_target_pairs={{0,128},{128,256},{256,384},{384,0},{1,129},{129,257},{257,385},{3... | collective-permute-start | bytes 3932168 | tf_op jit(solution)/shard_map/ppermute | solution.py:92
  48.5 3.7 %collective-permute-start.2 = (bf16[2048,320]{0,1:T(8,128)(2,1)}, bf16[2048,320]{0,1:T(8,128)(2,1)}, u32[]{:S(2)}, u32[]{:S(2)}) collective-permute-start(bf16[2048,320]{0,1:T(8,128)(2,1)} %bitcast.52), channel_id=1, source_target_pairs={{0,384},{128,0},{256,128},{384,256},{1,385},{129,1},{257,129},{385... | collective-permute-start | bytes 3932168 | tf_op jit(solution)/shard_map/ppermute | solution.py:93
  52.2 2.0 gather_fusion
  54.2 13.9 %all-to-all-start.2 = ((bf16[32,2,2,8,1024]{4,3,2,1,0:T(8,128)(2,1)}), bf16[32,2,2,8,1024]{4,3,2,1,0:T(8,128)(2,1)}, u32[]{:S(2)}, u32[]{:S(2)}) async-start(bf16[32,2,2,8,1024]{4,3,2,1,0:T(8,128)(2,1)} %bitcast.128), calls=%async_computation.2 | async-start | bytes 4194304 | tf_op jit(solution)/shard_map/all_to_all | solution.py:124
  68.2 0.1 fusion.41
  68.2 3.1 %fusion = f32[256]{0:T(256)S(1)} fusion(bf16[256,8192]{1,0:T(8,128)(2,1)} %param.10), kind=kLoop, calls=%fused_computation.4 | loop fusion | flops 6291200 | bytes 4195328 | tf_op jit(solution)/shard_map/reduce_sum | solution.py:84
  71.4 0.1 fusion.51
  71.5 0.8 maximum_select_fusion
  72.4 0.1 iota_compare_fusion.2
  72.6 0.2 select_reduce_fusion
  72.8 0.1 multiply_cosine_fusion
  72.9 3.6 %fusion.2 = bf16[256,8192]{1,0:T(8,128)(2,1)S(1)} fusion(bf16[256,8192]{1,0:T(8,128)(2,1)} %param.10, f32[8192]{0:T(1024)S(1)} %convert_element_type.100, f32[256]{0:T(256)S(1)} %add_rsqrt_fusion), kind=kLoop, calls=%fused_computation.6 | loop fusion | flops 8388608 | bytes 8422400 | tf_op jit(solution)/shard_map/convert_element_type | solution.py:85
  76.5 1.9 dynamic-slice_bitcast_fusion.2
  78.4 0.7 copy-done.1
  79.1 2.0 slice.46
  81.1 3.3 %collective-permute-start.3 = (bf16[1024,320]{0,1:T(8,128)(2,1)}, bf16[1024,320]{0,1:T(8,128)(2,1)}, u32[]{:S(2)}, u32[]{:S(2)}) collective-permute-start(bf16[1024,320]{0,1:T(8,128)(2,1)} %slice.46), channel_id=1, source_target_pairs={{0,128},{128,256},{256,384},{384,0},{1,129},{129,257},{257,385},{3... | collective-permute-start | bytes 1966088 | tf_op jit(solution)/shard_map/ppermute | solution.py:98
  84.3 2.0 slice.47
  86.3 3.8 %collective-permute-start.4 = (bf16[1024,320]{0,1:T(8,128)(2,1)}, bf16[1024,320]{0,1:T(8,128)(2,1)}, u32[]{:S(2)}, u32[]{:S(2)}) collective-permute-start(bf16[1024,320]{0,1:T(8,128)(2,1)} %slice.47), channel_id=1, source_target_pairs={{0,384},{128,0},{256,128},{384,256},{1,385},{129,1},{257,129},{385... | collective-permute-start | bytes 1966088 | tf_op jit(solution)/shard_map/ppermute | solution.py:98
  90.1 2.1 copy.74
  92.2 3.0 %reshape.322 = bf16[2048,320,1]{0,1,2:T(8,128)(2,1)S(1)} reshape(bf16[4,512,320]{1,0,2:T(4,128)(2,1)} %copy.74) | data formatting | bytes 2621440 | tf_op jit(solution)/shard_map/reshape | solution.py:38
  95.3 2.6 %fusion.7 = f32[320,32,8]{0,1,2:T(8,128)S(1)} fusion(bf16[2048,320]{0,1:T(8,128)(2,1)} %collective-permute-done.1, bf16[32,8,2048]{2,1,0:T(8,128)(2,1)} %get-tuple-element.29), kind=kOutput, calls=%fused_computation.13 | convolution fusion | flops 335544320 | bytes 2686976 | tf_op jit(solution)/shard_map/jbd,dc->bjc/dot_general | solution.py:106
  97.9 2.2 fusion.9
  100.1 1.2 collective-permute-done.3
  101.3 4.5 %collective-permute-done.4 = bf16[1024,320]{0,1:T(8,128)(2,1)} collective-permute-done((bf16[1024,320]{0,1:T(8,128)(2,1)}, bf16[1024,320]{0,1:T(8,128)(2,1)}, u32[]{:S(2)}, u32[]{:S(2)}) %collective-permute-start.4) | collective-permute-done | bytes 655392 | tf_op jit(solution)/shard_map/ppermute | solution.py:98
  105.8 2.2 fusion.4
  108.0 3.1 %fusion.24 = bf16[8,32,320]{2,0,1:T(8,128)(2,1)} fusion(f32[320,32,8]{0,1,2:T(8,128)S(1)} %fusion.4, f32[320,32,8]{0,1,2:T(8,128)S(1)} %fusion.7, bf16[2048,320,1]{0,1,2:T(8,128)(2,1)S(1)} %reshape.322, bf16[256,8192]{1,0:T(8,128)(2,1)} %copy-done.1, s32[]{:T(128)S(6)} %select_n.83, f32[320,32,8]{0,1,2:T(8,128)S(1)} %fusion.9), kind=kOutput, calls=%fused_computation.37 | convolution fusion | flops 335872000 | bytes 3506180 | tf_op jit(solution)/shard_map/jbd,dc->bjc/dot_general | solution.py:106
  111.1 7.2 %all-to-all-done.2 = bf16[32,2,2,8,1024]{4,3,2,1,0:T(8,128)(2,1)} async-done(((bf16[32,2,2,8,1024]{4,3,2,1,0:T(8,128)(2,1)}), bf16[32,2,2,8,1024]{4,3,2,1,0:T(8,128)(2,1)}, u32[]{:S(2)}, u32[]{:S(2)}) %all-to-all-start.2) | async-done | bytes 2097184 | tf_op jit(solution)/shard_map/all_to_all | solution.py:124
  118.3 15.0 %all-to-all-start.1 = ((bf16[8,32,320]{2,0,1:T(8,128)(2,1)}), bf16[8,32,320]{2,0,1:T(8,128)(2,1)S(1)}, u32[]{:S(2)}, u32[]{:S(2)}) async-start(bf16[8,32,320]{2,0,1:T(8,128)(2,1)} %fusion.24), calls=%async_computation.1 | async-start | bytes 393216 | tf_op jit(solution)/shard_map/all_to_all | solution.py:33
  133.3 2.2 gather_fusion.1
  135.5 0.3 copy.109
  135.8 0.1 fusion.53
  135.9 15.5 %all-to-all-done.1 = bf16[8,32,320]{2,0,1:T(8,128)(2,1)S(1)} async-done(((bf16[8,32,320]{2,0,1:T(8,128)(2,1)}), bf16[8,32,320]{2,0,1:T(8,128)(2,1)S(1)}, u32[]{:S(2)}, u32[]{:S(2)}) %all-to-all-start.1) | async-done | bytes 163872 | tf_op jit(solution)/shard_map/all_to_all | solution.py:33
  151.4 0.2 reshape.235
  151.6 0.1 subtract_convert_fusion.1
  151.7 0.1 maximum_bitcast_fusion.2
  151.8 0.1 fusion.55
  151.9 0.1 fusion.28
  152.1 0.3 fusion.36
  152.3 0.5 fusion.56
  152.9 0.3 fusion.27
  153.2 0.3 fusion.14
  153.5 0.1 convert_element_type.116
  153.6 0.1 copy.88
  153.7 20.7 %all_to_all.25 = bf16[8,32,512]{2,0,1:T(8,128)(2,1)S(1)} all-to-all(bf16[8,32,512]{2,0,1:T(8,128)(2,1)S(1)} %bitcast.135), channel_id=1, replica_groups=mesh['x'=4,'yh'=4,'yl'=2,'z'=8,'c'=2] {'yl','z','c'}, dimensions={1} | all-to-all | bytes 524288 | tf_op jit(solution)/shard_map/all_to_all | solution.py:146
  174.5 2.5 %fusion.52 = (bf16[256,4096]{0,1:T(8,128)(2,1)S(1)}, bf16[256,4096]{0,1:T(8,128)(2,1)S(1)}) fusion(bf16[512,4096]{0,1:T(8,128)(2,1)} %all-gather.3.cloned.1.call-done), kind=kLoop, calls=%fused_computation.99 | loop fusion | bytes 8388608 | tf_op jit(solution)/shard_map/slice | solution.py:155
  177.0 0.7 fusion.31
  177.7 0.7 fusion.3
  178.5 1.2 copy.93
  179.7 0.7 copy.94
  180.4 56.4 %all_to_all.26 = bf16[16,256,256]{2,1,0:T(8,128)(2,1)} all-to-all(bf16[16,256,256]{2,1,0:T(8,128)(2,1)S(1)} %copy.94), channel_id=1, replica_groups=mesh['x'=4,'yh'=4,'yl'=2,'z'=8,'c'=2] {'yl','z'}, dimensions={0} | all-to-all | bytes 4194304 | tf_op jit(solution)/shard_map/all_to_all | solution.py:160
  236.8 2.6 %reduce_sum.55 = bf16[256,256]{1,0:T(8,128)(2,1)} reduce(bf16[16,256,256]{2,1,0:T(8,128)(2,1)} %all_to_all.26, bf16[]{:T(256)} %constant.113.clone.1), dimensions={0}, to_apply=%region_7.9 | reduce | flops 983040 | bytes 2228226 | tf_op jit(solution)/shard_map/reduce_sum | solution.py:161
  (42 shorter events, 0.5 us)
Async XLA Ops:
  6.5 45.6 %copy-start = (bf16[32,2,8,1024]{3,2,1,0:T(8,128)(2,1)S(1)}, bf16[32,2,8,1024]{3,2,1,0:T(8,128)(2,1)}, u32[]{:S(2)}) copy-start(bf16[32,2,8,1024]{3,2,1,0:T(8,128)(2,1)} %param.14) | copy-start | bytes 3145732
  6.5 9.4 %copy-start.3 = (bf16[256,512]{1,0:T(8,128)(2,1)S(1)}, bf16[256,512]{1,0:T(8,128)(2,1)}, u32[]{:S(2)}) copy-start(bf16[256,512]{1,0:T(8,128)(2,1)} %param.13) | copy-start | bytes 786436
  8.8 9.8 %copy-start.6 = (s32[1024,1]{0,1:T(1,128)S(1)}, s32[1024,1]{0,1:T(1,128)}, u32[]{:S(2)}) copy-start(s32[1024,1]{0,1:T(1,128)} %param.16) | copy-start | bytes 12292
  8.8 10.7 %copy-start.5 = (s32[1024]{0:T(1024)S(1)}, s32[1024]{0:T(1024)}, u32[]{:S(2)}) copy-start(s32[1024]{0:T(1024)} %param.17) | copy-start | bytes 12292
  8.8 35.0 %all-to-all-start = ((bf16[4,512,320]{1,2,0:T(8,128)(2,1)}), bf16[4,512,320]{1,2,0:T(8,128)(2,1)S(1)}, u32[]{:S(2)}, u32[]{:S(2)}) async-start(bf16[4,512,320]{1,2,0:T(8,128)(2,1)} %broadcast_in_dim.29), calls=%async_computation | async-start | bytes 2621440 | tf_op jit(solution)/shard_map/all_to_all | solution.py:38
  16.1 55.4 %collective-permute-start = (bf16[256,256]{0,1:T(8,128)(2,1)S(1)}, bf16[256,256]{0,1:T(8,128)(2,1)S(1)}, u32[]{:S(2)}, u32[]{:S(2)}) collective-permute-start(bf16[256,256]{0,1:T(8,128)(2,1)S(1)} %get-tuple-element.39), channel_id=1, source_target_pairs={{0,1},{1,0},{2,3},{3,2},{4,5},{5,4},{6,7},{7,6},{8,9},{9,8},{10,11... | collective-permute-start | bytes 393224 | tf_op jit(solution)/shard_map/ppermute | solution.py:81
  45.1 27.3 %collective-permute-start.1 = (bf16[2048,320]{0,1:T(8,128)(2,1)}, bf16[2048,320]{0,1:T(8,128)(2,1)}, u32[]{:S(2)}, u32[]{:S(2)}) collective-permute-start(bf16[2048,320]{0,1:T(8,128)(2,1)} %bitcast.52), channel_id=1, source_target_pairs={{0,128},{128,256},{256,384},{384,0},{1,129},{129,257},{257,385},{3... | collective-permute-start | bytes 3932168 | tf_op jit(solution)/shard_map/ppermute | solution.py:92
  48.5 23.9 %collective-permute-start.2 = (bf16[2048,320]{0,1:T(8,128)(2,1)}, bf16[2048,320]{0,1:T(8,128)(2,1)}, u32[]{:S(2)}, u32[]{:S(2)}) collective-permute-start(bf16[2048,320]{0,1:T(8,128)(2,1)} %bitcast.52), channel_id=1, source_target_pairs={{0,384},{128,0},{256,128},{384,256},{1,385},{129,1},{257,129},{385... | collective-permute-start | bytes 3932168 | tf_op jit(solution)/shard_map/ppermute | solution.py:93
  54.2 64.1 %all-to-all-start.2 = ((bf16[32,2,2,8,1024]{4,3,2,1,0:T(8,128)(2,1)}), bf16[32,2,2,8,1024]{4,3,2,1,0:T(8,128)(2,1)}, u32[]{:S(2)}, u32[]{:S(2)}) async-start(bf16[32,2,2,8,1024]{4,3,2,1,0:T(8,128)(2,1)} %bitcast.128), calls=%async_computation.2 | async-start | bytes 4194304 | tf_op jit(solution)/shard_map/all_to_all | solution.py:124
  68.1 106.4 %all-gather.3.cloned.1.call-start = ((), (), s32[]{:S(2)}) async-start(), calls=%async_computation.5 | async-start | bytes 4456448 | tf_op jit(solution)/shard_map/all_gather | solution.py:95
  68.2 3.2 %copy-start.7 = (s32[256]{0:T(256)S(1)}, s32[256]{0:T(256)}, u32[]{:S(2)}) copy-start(s32[256]{0:T(256)} %param.15) | copy-start | bytes 3076
  68.2 4.2 %copy-start.4 = (bf16[8192]{0:T(1024)(128)(2,1)S(1)}, bf16[8192]{0:T(1024)(128)(2,1)}, u32[]{:S(2)}) copy-start(bf16[8192]{0:T(1024)(128)(2,1)} %param.11) | copy-start | bytes 49156
  76.5 2.6 %copy-start.1 = (bf16[256,8192]{1,0:T(8,128)(2,1)}, bf16[256,8192]{1,0:T(8,128)(2,1)S(1)}, u32[]{:S(2)}) copy-start(bf16[256,8192]{1,0:T(8,128)(2,1)S(1)} %fusion.2) | copy-start | bytes 12582916
  81.1 20.2 %collective-permute-start.3 = (bf16[1024,320]{0,1:T(8,128)(2,1)}, bf16[1024,320]{0,1:T(8,128)(2,1)}, u32[]{:S(2)}, u32[]{:S(2)}) collective-permute-start(bf16[1024,320]{0,1:T(8,128)(2,1)} %slice.46), channel_id=1, source_target_pairs={{0,128},{128,256},{256,384},{384,0},{1,129},{129,257},{257,385},{3... | collective-permute-start | bytes 1966088 | tf_op jit(solution)/shard_map/ppermute | solution.py:98
  86.3 19.5 %collective-permute-start.4 = (bf16[1024,320]{0,1:T(8,128)(2,1)}, bf16[1024,320]{0,1:T(8,128)(2,1)}, u32[]{:S(2)}, u32[]{:S(2)}) collective-permute-start(bf16[1024,320]{0,1:T(8,128)(2,1)} %slice.47), channel_id=1, source_target_pairs={{0,384},{128,0},{256,128},{384,256},{1,385},{129,1},{257,129},{385... | collective-permute-start | bytes 1966088 | tf_op jit(solution)/shard_map/ppermute | solution.py:98
  95.3 2.6 %copy-start.2 = (bf16[32,8,2048]{2,1,0:T(8,128)(2,1)S(1)}, bf16[32,8,2048]{2,1,0:T(8,128)(2,1)}, u32[]{:S(2)}) copy-start(bf16[32,8,2048]{2,1,0:T(8,128)(2,1)} %get-tuple-element.27) | copy-start | bytes 3145732
  118.3 33.0 %all-to-all-start.1 = ((bf16[8,32,320]{2,0,1:T(8,128)(2,1)}), bf16[8,32,320]{2,0,1:T(8,128)(2,1)S(1)}, u32[]{:S(2)}, u32[]{:S(2)}) async-start(bf16[8,32,320]{2,0,1:T(8,128)(2,1)} %fusion.24), calls=%async_computation.1 | async-start | bytes 393216 | tf_op jit(solution)/shard_map/all_to_all | solution.py:33
Sparse Core Ops, SparseCore 0:
  72.5 93.3 all-gather.2

commit v7 on v4

--- a/solution.py
+++ b/solution.py
@@ -38,11 +38,16 @@
     return lax.all_to_all(copies, axis, 0, 0, tiled=True).reshape((-1,) + tile.shape[1:])
 
 
-def ring_gather(piece, axis, count):
+def ring_near(piece, axis, count):
     ahead = [(i, (i + 1) % count) for i in range(count)]
     behind = [(i, (i - 1) % count) for i in range(count)]
-    from_left = lax.ppermute(piece, axis, ahead)
-    from_right = lax.ppermute(piece, axis, behind)
+    return lax.ppermute(piece, axis, ahead), lax.ppermute(piece, axis, behind)
+
+
+def ring_far(piece, near, axis, count):
+    ahead = [(i, (i + 1) % count) for i in range(count)]
+    behind = [(i, (i - 1) % count) for i in range(count)]
+    from_left, from_right = near
     cut = piece.shape[0] // 2
     far = jnp.concatenate(
         [lax.ppermute(from_left[:cut], axis, ahead), lax.ppermute(from_right[cut:], axis, behind)],
@@ -88,34 +93,59 @@
     own_beams = grouped_row_block // columns
     cores = lax.axis_size("c")
     core = lax.axis_index("c")
+    assert cores == 2
     halves = w_out.reshape(w_out.shape[0], cores, w_out.shape[1] // cores)
-    assert cores == 2
     mine = jnp.take(halves, core, axis=1)
     other = lax.ppermute(jnp.take(halves, 1 - core, axis=1), "c", [(0, 1), (1, 0)])
     w_local = jnp.where(core == 0, jnp.concatenate([mine, other], 0), jnp.concatenate([other, mine], 0))
-    w_pair = lax.all_gather(w_local[:, None], OWNER, axis=1, tiled=True)
     floats = hidden.astype(jnp.float32)
     scale_rms = lax.rsqrt(jnp.mean(floats * floats, axis=-1, keepdims=True) + 1e-05)
     normed = (floats * scale_rms * norm_gain.astype(jnp.float32)).astype(jnp.bfloat16)
     xs = lax.axis_size("x")
     ys = lax.axis_size("yh")
     assert xs == 4 and ys == 4
-    near = ring_gather(w_qkv, "yh", ys)
-    stack = jnp.concatenate(near, axis=0)
-    ordered = normed.reshape(normed.shape[0], xs, ys, w_qkv.shape[0])
-    ordered = jnp.roll(ordered, -lax.axis_index("x"), axis=1)
-    ordered = jnp.roll(ordered, -lax.axis_index("yh"), axis=2)
-    ordered = ordered.reshape(columns, own_beams, xs, ys * w_qkv.shape[0])
-    rows = stack.shape[0]
-    projected = None
-    for step, piece in zip((0, 1, 2, 3), ring_gather(stack, "x", xs)):
+    me = lax.axis_index("x")
+    mine_y = lax.axis_index("yh")
+    rows = w_qkv.shape[0]
+    wide = 192
+    stack = gather_rows(w_qkv[:, :wide], "yh", ys)
+    by_x = ring_near(w_qkv[:, wide:], "x", xs)
+    near = ring_near(stack, "x", xs)
+    w_local, near, by_x = lax.optimization_barrier((w_local, near, by_x))
+    w_pair = lax.all_gather(w_local[:, None], OWNER, axis=1, tiled=True)
+    stack_b = jnp.concatenate(ring_far(w_qkv[:, wide:], by_x, "x", xs), axis=0)
+    pieces_b = ring_far(stack_b, ring_near(stack_b, "yh", ys), "yh", ys)
+    pieces_a = ring_far(stack, near, "x", xs)
+    part_a = None
+    for step, piece in enumerate(pieces_a):
+        start = ((me + step) % xs) * ys * rows
+        block = lax.dynamic_slice_in_dim(normed, start, ys * rows, axis=1)
         term = jnp.einsum(
             "jbd,dc->bjc",
-            ordered[:, :, step],
+            block.reshape(columns, own_beams, ys * rows),
             piece,
             preferred_element_type=jnp.float32,
         )
-        projected = term if projected is None else projected + term
+        part_a = term if part_a is None else part_a + term
+    part_b = None
+    for step, piece in enumerate(pieces_b):
+        block = jnp.concatenate(
+            [
+                lax.dynamic_slice_in_dim(
+                    normed, (((me + dx) % xs) * ys + (mine_y + step) % ys) * rows, rows, axis=1
+                )
+                for dx in range(xs)
+            ],
+            axis=1,
+        )
+        term = jnp.einsum(
+            "jbd,dc->bjc",
+            block.reshape(columns, own_beams, xs * rows),
+            piece,
+            preferred_element_type=jnp.float32,
+        )
+        part_b = term if part_b is None else part_b + term
+    projected = jnp.concatenate([part_a, part_b], axis=-1)
     own_qkv = regroup(projected.astype(jnp.bfloat16)).reshape(own_beams, QKV)
     blk_dev = kv_cache.shape[0]
     most_slots = max(2, 2 * blk_dev // columns)

time: 322 us -> 344 us (1.068)
  starting transfers between devices: 50 us -> 97.2 us
  local copies, waits for them, and re-layouts: 58.9 us -> 36.3 us
  other arithmetic: 32.3 us -> 13.2 us
  waiting for transfers between devices: 78.2 us -> 94.1 us
    all_to_all x1, starting transfers between devices: 13.9 us -> 40.6 us  [regroup(): return lax.all_to_all(blocks, BEAM, split_axis=1, concat_axis=1, tiled=True)]
    concatenate x2 -> x1, other arithmetic: 18.7 us -> 0.79 us  [shards(): projected = jnp.concatenate([part_a, part_b], axis=-1)]
    ppermute x8 -> x12, starting transfers between devices: 30 us -> 43.7 us  [the longest x6 22.8 us: ring_near(): return (lax.ppermute(piece, axis, ahead), lax.ppermute(piece, axis, behind))]
    reshape x2 -> x3, local copies, waits for them, and re-layouts: 15.4 us -> 2.47 us  [the longest x1 1.81 us: shards(): block.reshape(columns, own_beams, ys * rows)]
    all_to_all x0 -> x1, waiting for transfers between devices: none -> 10.3 us  [gather_rows(): lax.all_to_all(copies, axis, 0, 0, tiled=True)]
    slice x5 -> x10, local copies, waits for them, and re-layouts: 18 us -> 9.35 us  [the longest x3 3.25 us: ring_far(): from_right[cut:]]
    all_to_all x0 -> x1, starting transfers between devices: none -> 6.97 us  [gather_rows(): lax.all_to_all(copies, axis, 0, 0, tiled=True)]
    ppermute x8 -> x12, waiting for transfers between devices: 17 us -> 23.3 us  [the longest x6 14.6 us: ring_near(): return (lax.ppermute(piece, axis, ahead), lax.ppermute(piece, axis, behind))]
  transfers between devices with their start and end apart: 12 -> 17, of which waited for: 5 -> 6; matrix products, arithmetic and copies ran while one was open for 30% -> 16% of each run, Pallas kernels for 0% -> 0%
where the time goes in v7:
time: 344 us; the launch traced here: 343 us
  starting transfers between devices  97.2 us (28%)
  waiting for transfers between devices  94.1 us (27%)
  blocking collectives  73.1 us (21%)
  local copies, waits for them, and re-layouts  36.3 us (11%)
  matrix products  14.7 us (4%)
  between operations  14.3 us (4%)
  other arithmetic  13.2 us (4%)
    all_to_all x1, blocking collectives, shards(): spread = lax.all_to_all(partial.transpose(1, 0, 2), PAIR, 0, 0, tiled=True)  53.2 us
    all_to_all x1, waiting for transfers between devices, shards(): lax.all_to_all(outgoing, BEAM, split_axis=0, concat_axis=0, tiled=True)  48.5 us
    all_to_all x1, starting transfers between devices, regroup(): return lax.all_to_all(blocks, BEAM, split_axis=1, concat_axis=1, tiled=True)  40.6 us
    ppermute x6, starting transfers between devices, ring_near(): return (lax.ppermute(piece, axis, ahead), lax.ppermute(piece, axis, behind))  22.8 us
    all_to_all x1, blocking collectives, shards(): lax.all_to_all(doubled.reshape(own_beams, columns, pair_feats.shape[3]),...  19.9 us
    ppermute x6, waiting for transfers between devices, ring_near(): return (lax.ppermute(piece, axis, ahead), lax.ppermute(piece, axis, behind))  14.6 us
    ppermute x3, starting transfers between devices, ring_far(): lax.ppermute(from_right[cut:], axis, behind)  14 us
    all_to_all x1, waiting for transfers between devices, regroup(): return lax.all_to_all(blocks, BEAM, split_axis=1, concat_axis=1, tiled=True)  12 us
  transfers between devices with their start and end apart: 17, of which 6 were waited for; matrix products, arithmetic and copies ran while one was open for 16% of the time, Pallas kernels for 0%

profile of v7, /device:TPU:56, one launch (start us, length us, event | category | flops | bytes accessed | tf_op | source)
XLA Modules:
  0.0 342.8 jit_solution(9053897651199613312)
XLA Ops:
  6.5 1.0 slice.65
  7.7 3.4 collective-permute-start.3
  11.1 3.7 %collective-permute-start.4 = (bf16[512,128]{1,0:T(8,128)(2,1)S(1)}, bf16[512,128]{1,0:T(8,128)(2,1)}, u32[]{:S(2)}, u32[]{:S(2)}) collective-permute-start(bf16[512,128]{1,0:T(8,128)(2,1)S(1)} %copy.153), channel_id=1, source_target_pairs={{0,384},{128,0},{256,128},{384,256},{1,385},{129,1},{257,129},{385... | collective-permute-start | bytes 393224 | tf_op jit(solution)/shard_map/ppermute | solution.py:44
  14.8 1.1 copy.103
  15.9 1.9 collective-permute-start
  17.9 1.0 broadcast_in_dim.29
  18.8 7.0 %all-to-all-start = ((bf16[4,512,192]{1,2,0:T(8,128)(2,1)}), bf16[4,512,192]{1,2,0:T(8,128)(2,1)S(1)}, u32[]{:S(2)}, u32[]{:S(2)}) async-start(bf16[4,512,192]{1,2,0:T(8,128)(2,1)} %broadcast_in_dim.29), calls=%async_computation | async-start | bytes 1572864 | tf_op jit(solution)/shard_map/all_to_all | solution.py:38
  25.8 3.1 fusion
  28.9 0.5 broadcast.203
  29.5 0.7 reduce.4
  30.4 5.3 %fusion.2 = bf16[256,8192]{1,0:T(8,128)(2,1)} fusion(bf16[256,8192]{1,0:T(8,128)(2,1)} %param.10, f32[8192]{0:T(1024)S(1)} %convert_element_type.98, f32[256]{0:T(256)S(1)} %add_rsqrt_fusion), kind=kLoop, calls=%fused_computation.6 | loop fusion | flops 8388608 | bytes 8422400 | tf_op jit(solution)/shard_map/convert_element_type | solution.py:103
  35.8 10.3 %all-to-all-done = bf16[4,512,192]{1,2,0:T(8,128)(2,1)S(1)} async-done(((bf16[4,512,192]{1,2,0:T(8,128)(2,1)}), bf16[4,512,192]{1,2,0:T(8,128)(2,1)S(1)}, u32[]{:S(2)}, u32[]{:S(2)}) %all-to-all-start) | async-done | bytes 786464 | tf_op jit(solution)/shard_map/all_to_all | solution.py:38
  46.2 1.9 collective-permute-start.1
  48.1 5.1 %collective-permute-start.2 = (bf16[2048,192]{0,1:T(8,128)(2,1)S(1)}, bf16[2048,192]{0,1:T(8,128)(2,1)}, u32[]{:S(2)}, u32[]{:S(2)}) collective-permute-start(bf16[2048,192]{0,1:T(8,128)(2,1)S(1)} %bitcast.157), channel_id=1, source_target_pairs={{0,384},{128,0},{256,128},{384,256},{1,385},{129,1},{257,129},{385... | collective-permute-start | bytes 2359304 | tf_op jit(solution)/shard_map/ppermute | solution.py:44
  53.2 4.4 %constant_dynamic-slice_fusion.16 = (bf16[256,512]{1,0:T(8,128)(2,1)}, bf16[256,512]{1,0:T(8,128)(2,1)}, bf16[256,512]{1,0:T(8,128)(2,1)}, bf16[256,512]{1,0:T(8...) fusion(bf16[256,8192]{1,0:T(8,128)(2,1)} %fusion.2, ...), kind=kLoop, calls=%fused_computation.145 | loop fusion | bytes 8388672 | tf_op jit(solution)/shard_map/dynamic_slice | solution.py:134
  57.7 1.8 dynamic-slice_bitcast_fusion.2
  59.5 0.7 constant_dynamic-update-slice_fusion.4
  60.4 0.7 reshape.253
  61.1 0.8 maximum_select_fusion
  61.9 0.6 copy.106
  62.5 0.6 reshape.338
  63.1 1.1 slice.67
  64.2 3.1 collective-permute-start.5
  67.3 1.8 slice.68
  69.1 4.0 %collective-permute-start.6 = (bf16[1024,192]{0,1:T(8,128)(2,1)}, bf16[1024,192]{0,1:T(8,128)(2,1)}, u32[]{:S(2)}, u32[]{:S(2)}) collective-permute-start(bf16[1024,192]{0,1:T(8,128)(2,1)} %slice.68), channel_id=1, source_target_pairs={{0,384},{128,0},{256,128},{384,256},{1,385},{129,1},{257,129},{385... | collective-permute-start | bytes 1179656 | tf_op jit(solution)/shard_map/ppermute | solution.py:53
  73.1 2.3 fusion.42
  75.5 2.8 fusion.46
  78.3 1.5 slice.69
  79.8 1.9 collective-permute-start.7
  81.7 1.6 constant_dynamic-update-slice_fusion.3
  83.3 1.5 slice.70
  84.7 5.1 %collective-permute-start.8 = (bf16[256,128]{1,0:T(8,128)(2,1)}, bf16[256,128]{1,0:T(8,128)(2,1)}, u32[]{:S(2)}, u32[]{:S(2)}) collective-permute-start(bf16[256,128]{1,0:T(8,128)(2,1)} %slice.70), channel_id=1, source_target_pairs={{0,384},{128,0},{256,128},{384,256},{1,385},{129,1},{257,129},{385... | collective-permute-start | bytes 196616 | tf_op jit(solution)/shard_map/ppermute | solution.py:53
  89.9 1.5 constant_dynamic-update-slice_fusion.2
  91.4 0.7 collective-permute-done.8
  92.1 1.5 constant_dynamic-update-slice_fusion.1
  93.5 1.6 constant_dynamic-update-slice_fusion
  95.1 4.2 %collective-permute-start.9 = (bf16[2048,128]{1,0:T(8,128)(2,1)}, bf16[2048,128]{1,0:T(8,128)(2,1)S(1)}, u32[]{:S(2)}, u32[]{:S(2)}) collective-permute-start(bf16[2048,128]{1,0:T(8,128)(2,1)} %constant_dynamic-update-slice_fusion), channel_id=1, source_target_pairs={{0,96},{32,0},{64,32},{96,64},{1,97},{33,1},{65,33},{97,65},{2,98}... | collective-permute-start | bytes 1572872 | tf_op jit(solution)/shard_map/ppermute | solution.py:44
  99.3 4.5 %collective-permute-start.10 = (bf16[2048,128]{1,0:T(8,128)(2,1)}, bf16[2048,128]{1,0:T(8,128)(2,1)S(1)}, u32[]{:S(2)}, u32[]{:S(2)}) collective-permute-start(bf16[2048,128]{1,0:T(8,128)(2,1)} %constant_dynamic-update-slice_fusion), channel_id=1, source_target_pairs={{0,32},{32,64},{64,96},{96,0},{1,33},{33,65},{65,97},{97,1},{2,34}... | collective-permute-start | bytes 1572872 | tf_op jit(solution)/shard_map/ppermute | solution.py:44
  103.8 2.0 fusion.44
  105.9 2.1 fusion.8
  108.0 14.6 %collective-permute-done.10 = bf16[2048,128]{1,0:T(8,128)(2,1)S(1)} collective-permute-done((bf16[2048,128]{1,0:T(8,128)(2,1)}, bf16[2048,128]{1,0:T(8,128)(2,1)S(1)}, u32[]{:S(2)}, u32[]{:S(2)}) %collective-permute-start.10) | collective-permute-done | bytes 524320 | tf_op jit(solution)/shard_map/ppermute | solution.py:44
  122.6 1.9 collective-permute-start.11
  124.6 4.8 %collective-permute-start.12 = (bf16[1024,128]{1,0:T(8,128)(2,1)S(1)}, bf16[1024,128]{1,0:T(8,128)(2,1)S(1)}, u32[]{:S(2)}, u32[]{:S(2)}) collective-permute-start(bf16[1024,128]{1,0:T(8,128)(2,1)S(1)} %slice.102), channel_id=1, source_target_pairs={{0,96},{32,0},{64,32},{96,64},{1,97},{33,1},{65,33},{97,65},{2,98}... | collective-permute-start | bytes 786440 | tf_op jit(solution)/shard_map/ppermute | solution.py:53
  129.9 0.5 copy-done.12
  131.1 8.0 %collective-permute-done.11 = bf16[1024,128]{1,0:T(8,128)(2,1)S(1)} collective-permute-done((bf16[1024,128]{1,0:T(8,128)(2,1)S(1)}, bf16[1024,128]{1,0:T(8,128)(2,1)S(1)}, u32[]{:S(2)}, u32[]{:S(2)}) %collective-permute-start.11) | collective-permute-done | bytes 262176 | tf_op jit(solution)/shard_map/ppermute | solution.py:53
  139.6 0.5 copy-done.4
  140.3 1.5 fusion.13
  141.8 0.8 pad_maximum_fusion
  142.6 40.6 %all-to-all-start.1 = ((bf16[8,32,320]{2,0,1:T(8,128)(2,1)}), bf16[8,32,320]{2,0,1:T(8,128)(2,1)S(1)}, u32[]{:S(2)}, u32[]{:S(2)}) async-start(bf16[8,32,320]{2,0,1:T(8,128)(2,1)} %pad_maximum_fusion), calls=%async_computation.1 | async-start | bytes 393216 | tf_op jit(solution)/shard_map/all_to_all | solution.py:33
  183.3 2.0 gather_fusion
  185.4 12.0 %all-to-all-done.1 = bf16[8,32,320]{2,0,1:T(8,128)(2,1)S(1)} async-done(((bf16[8,32,320]{2,0,1:T(8,128)(2,1)}), bf16[8,32,320]{2,0,1:T(8,128)(2,1)S(1)}, u32[]{:S(2)}, u32[]{:S(2)}) %all-to-all-start.1) | async-done | bytes 163872 | tf_op jit(solution)/shard_map/all_to_all | solution.py:33
  197.4 3.9 %all-to-all-start.2 = ((bf16[32,2,2,8,1024]{4,3,2,1,0:T(8,128)(2,1)}), bf16[32,2,2,8,1024]{4,3,2,1,0:T(8,128)(2,1)S(1)}, u32[]{:S(2)}, u32[]{:S(2)}) async-start(bf16[32,2,2,8,1024]{4,3,2,1,0:T(8,128)(2,1)} %bitcast.30), calls=%async_computation.2 | async-start | bytes 4194304 | tf_op jit(solution)/shard_map/all_to_all | solution.py:160
  202.9 48.5 %all-to-all-done.2 = bf16[32,2,2,8,1024]{4,3,2,1,0:T(8,128)(2,1)S(1)} async-done(((bf16[32,2,2,8,1024]{4,3,2,1,0:T(8,128)(2,1)}), bf16[32,2,2,8,1024]{4,3,2,1,0:T(8,128)(2,1)S(1)}, u32[]{:S(2)}, u32[]{:S(2)}) %all-to-all-start.2) | async-done | bytes 2097184 | tf_op jit(solution)/shard_map/all_to_all | solution.py:160
  251.4 1.6 gather_fusion.1
  253.0 1.5 copy.159
  254.6 0.5 fusion.95
  256.0 19.9 %all_to_all.25 = bf16[8,32,512]{2,0,1:T(8,128)(2,1)S(1)} all-to-all(bf16[8,32,512]{2,0,1:T(8,128)(2,1)S(1)} %bitcast.155), channel_id=1, replica_groups=mesh['x'=4,'yh'=4,'yl'=2,'z'=8,'c'=2] {'yl','z','c'}, dimensions={1} | all-to-all | bytes 524288 | tf_op jit(solution)/shard_map/all_to_all | solution.py:182
  275.9 2.5 fusion.91
  278.4 0.7 fusion.66
  279.1 0.7 fusion.3
  279.9 1.2 copy.134
  281.1 0.7 copy.135
  281.8 53.2 %all_to_all.26 = bf16[16,256,256]{2,1,0:T(8,128)(2,1)S(1)} all-to-all(bf16[16,256,256]{2,1,0:T(8,128)(2,1)S(1)} %copy.135), channel_id=1, replica_groups=mesh['x'=4,'yh'=4,'yl'=2,'z'=8,'c'=2] {'yl','z'}, dimensions={0} | all-to-all | bytes 4194304 | tf_op jit(solution)/shard_map/all_to_all | solution.py:196
  335.0 1.0 reduce_sum.55
  (113 shorter events, 5.3 us)
Async XLA Ops:
  6.5 176.8 %copy-start = (bf16[32,2,8,1024]{3,2,1,0:T(8,128)(2,1)S(1)}, bf16[32,2,8,1024]{3,2,1,0:T(8,128)(2,1)}, u32[]{:S(2)}) copy-start(bf16[32,2,8,1024]{3,2,1,0:T(8,128)(2,1)} %param.14) | copy-start | bytes 3145732
  6.5 11.3 %slice-start = ((bf16[512,320]{0,1:T(8,128)(2,1)}), bf16[512,192]{0,1:T(8,128)(2,1)S(1)}, s32[]{:S(2)}) async-start(bf16[512,320]{0,1:T(8,128)(2,1)} %param.12), calls=%async_computation.6 | async-start | bytes 393216 | tf_op jit(solution)/shard_map/slice | solution.py:111
  7.7 55.4 %collective-permute-start.3 = (bf16[512,128]{1,0:T(8,128)(2,1)S(1)}, bf16[512,128]{1,0:T(8,128)(2,1)}, u32[]{:S(2)}, u32[]{:S(2)}) collective-permute-start(bf16[512,128]{1,0:T(8,128)(2,1)S(1)} %copy.153), channel_id=1, source_target_pairs={{0,128},{128,256},{256,384},{384,0},{1,129},{129,257},{257,385},{3... | collective-permute-start | bytes 393224 | tf_op jit(solution)/shard_map/ppermute | solution.py:44
  11.1 52.0 %collective-permute-start.4 = (bf16[512,128]{1,0:T(8,128)(2,1)S(1)}, bf16[512,128]{1,0:T(8,128)(2,1)}, u32[]{:S(2)}, u32[]{:S(2)}) collective-permute-start(bf16[512,128]{1,0:T(8,128)(2,1)S(1)} %copy.153), channel_id=1, source_target_pairs={{0,384},{128,0},{256,128},{384,256},{1,385},{129,1},{257,129},{385... | collective-permute-start | bytes 393224 | tf_op jit(solution)/shard_map/ppermute | solution.py:44
  14.8 11.0 %copy-start.21 = (bf16[8192]{0:T(1024)(128)(2,1)S(1)}, bf16[8192]{0:T(1024)(128)(2,1)}, u32[]{:S(2)}) copy-start(bf16[8192]{0:T(1024)(128)(2,1)} %param.11) | copy-start | bytes 49156
  15.9 45.2 %collective-permute-start = (bf16[256,256]{0,1:T(8,128)(2,1)S(1)}, bf16[256,256]{0,1:T(8,128)(2,1)S(1)}, u32[]{:S(2)}, u32[]{:S(2)}) collective-permute-start(bf16[256,256]{0,1:T(8,128)(2,1)S(1)} %get-tuple-element.59), channel_id=1, source_target_pairs={{0,1},{1,0},{2,3},{3,2},{4,5},{5,4},{6,7},{7,6},{8,9},{9,8},{10,11... | collective-permute-start | bytes 393224 | tf_op jit(solution)/shard_map/ppermute | solution.py:99
  18.8 27.3 %all-to-all-start = ((bf16[4,512,192]{1,2,0:T(8,128)(2,1)}), bf16[4,512,192]{1,2,0:T(8,128)(2,1)S(1)}, u32[]{:S(2)}, u32[]{:S(2)}) async-start(bf16[4,512,192]{1,2,0:T(8,128)(2,1)} %broadcast_in_dim.29), calls=%async_computation | async-start | bytes 1572864 | tf_op jit(solution)/shard_map/all_to_all | solution.py:38
  25.8 250.1 %all-gather.3.cloned.1.call-start = ((), (), s32[]{:S(2)}) async-start(), calls=%async_computation.5 | async-start | bytes 4456448 | tf_op jit(solution)/shard_map/all_gather | solution.py:115
  25.8 3.7 %copy-start.23 = (s32[1024,1]{0,1:T(1,128)S(1)}, s32[1024,1]{0,1:T(1,128)}, u32[]{:S(2)}) copy-start(s32[1024,1]{0,1:T(1,128)} %param.16) | copy-start | bytes 12292
  46.2 17.0 %collective-permute-start.1 = (bf16[2048,192]{0,1:T(8,128)(2,1)S(1)}, bf16[2048,192]{0,1:T(8,128)(2,1)}, u32[]{:S(2)}, u32[]{:S(2)}) collective-permute-start(bf16[2048,192]{0,1:T(8,128)(2,1)S(1)} %bitcast.156), channel_id=1, source_target_pairs={{0,128},{128,256},{256,384},{384,0},{1,129},{129,257},{257,385},{3... | collective-permute-start | bytes 2359304 | tf_op jit(solution)/shard_map/ppermute | solution.py:44
  48.1 15.0 %collective-permute-start.2 = (bf16[2048,192]{0,1:T(8,128)(2,1)S(1)}, bf16[2048,192]{0,1:T(8,128)(2,1)}, u32[]{:S(2)}, u32[]{:S(2)}) collective-permute-start(bf16[2048,192]{0,1:T(8,128)(2,1)S(1)} %bitcast.157), channel_id=1, source_target_pairs={{0,384},{128,0},{256,128},{384,256},{1,385},{129,1},{257,129},{385... | collective-permute-start | bytes 2359304 | tf_op jit(solution)/shard_map/ppermute | solution.py:44
  53.2 4.4 %copy-start.1 = (bf16[256,8192]{1,0:T(8,128)(2,1)S(1)}, bf16[256,8192]{1,0:T(8,128)(2,1)}, u32[]{:S(2)}) copy-start(bf16[256,8192]{1,0:T(8,128)(2,1)} %fusion.2) | copy-start | bytes 12582916
  57.7 2.5 copy-start.22
  63.1 12.4 %copy-start.3 = (bf16[32,8,2048]{2,1,0:T(8,128)(2,1)S(1)}, bf16[32,8,2048]{2,1,0:T(8,128)(2,1)}, u32[]{:S(2)}) copy-start(bf16[32,8,2048]{2,1,0:T(8,128)(2,1)} %get-tuple-element.31) | copy-start | bytes 3145732
  64.2 39.5 %collective-permute-start.5 = (bf16[1024,192]{0,1:T(8,128)(2,1)S(1)}, bf16[1024,192]{0,1:T(8,128)(2,1)}, u32[]{:S(2)}, u32[]{:S(2)}) collective-permute-start(bf16[1024,192]{0,1:T(8,128)(2,1)S(1)} %slice.67), channel_id=1, source_target_pairs={{0,128},{128,256},{256,384},{384,0},{1,129},{129,257},{257,385},{3... | collective-permute-start | bytes 1179656 | tf_op jit(solution)/shard_map/ppermute | solution.py:53
  69.1 34.7 %collective-permute-start.6 = (bf16[1024,192]{0,1:T(8,128)(2,1)}, bf16[1024,192]{0,1:T(8,128)(2,1)}, u32[]{:S(2)}, u32[]{:S(2)}) collective-permute-start(bf16[1024,192]{0,1:T(8,128)(2,1)} %slice.68), channel_id=1, source_target_pairs={{0,384},{128,0},{256,128},{384,256},{1,385},{129,1},{257,129},{385... | collective-permute-start | bytes 1179656 | tf_op jit(solution)/shard_map/ppermute | solution.py:53
  75.5 28.3 %copy-start.2 = (bf16[32,8,2048]{2,1,0:T(8,128)(2,1)S(1)}, bf16[32,8,2048]{2,1,0:T(8,128)(2,1)}, u32[]{:S(2)}) copy-start(bf16[32,8,2048]{2,1,0:T(8,128)(2,1)} %get-tuple-element.33) | copy-start | bytes 3145732
  79.8 10.1 %collective-permute-start.7 = (bf16[256,128]{1,0:T(8,128)(2,1)}, bf16[256,128]{1,0:T(8,128)(2,1)}, u32[]{:S(2)}, u32[]{:S(2)}) collective-permute-start(bf16[256,128]{1,0:T(8,128)(2,1)} %slice.69), channel_id=1, source_target_pairs={{0,128},{128,256},{256,384},{384,0},{1,129},{129,257},{257,385},{3... | collective-permute-start | bytes 196616 | tf_op jit(solution)/shard_map/ppermute | solution.py:53
  84.7 7.3 %collective-permute-start.8 = (bf16[256,128]{1,0:T(8,128)(2,1)}, bf16[256,128]{1,0:T(8,128)(2,1)}, u32[]{:S(2)}, u32[]{:S(2)}) collective-permute-start(bf16[256,128]{1,0:T(8,128)(2,1)} %slice.70), channel_id=1, source_target_pairs={{0,384},{128,0},{256,128},{384,256},{1,385},{129,1},{257,129},{385... | collective-permute-start | bytes 196616 | tf_op jit(solution)/shard_map/ppermute | solution.py:53
  95.1 29.5 %collective-permute-start.9 = (bf16[2048,128]{1,0:T(8,128)(2,1)}, bf16[2048,128]{1,0:T(8,128)(2,1)S(1)}, u32[]{:S(2)}, u32[]{:S(2)}) collective-permute-start(bf16[2048,128]{1,0:T(8,128)(2,1)} %constant_dynamic-update-slice_fusion), channel_id=1, source_target_pairs={{0,96},{32,0},{64,32},{96,64},{1,97},{33,1},{65,33},{97,65},{2,98}... | collective-permute-start | bytes 1572872 | tf_op jit(solution)/shard_map/ppermute | solution.py:44
  99.3 23.3 %collective-permute-start.10 = (bf16[2048,128]{1,0:T(8,128)(2,1)}, bf16[2048,128]{1,0:T(8,128)(2,1)S(1)}, u32[]{:S(2)}, u32[]{:S(2)}) collective-permute-start(bf16[2048,128]{1,0:T(8,128)(2,1)} %constant_dynamic-update-slice_fusion), channel_id=1, source_target_pairs={{0,32},{32,64},{64,96},{96,0},{1,33},{33,65},{65,97},{97,1},{2,34}... | collective-permute-start | bytes 1572872 | tf_op jit(solution)/shard_map/ppermute | solution.py:44
  103.8 2.0 copy-start.20
  105.9 23.6 %copy-start.16 = (bf16[256,512]{1,0:T(8,128)(2,1)S(1)}, bf16[256,512]{1,0:T(8,128)(2,1)}, u32[]{:S(2)}) copy-start(bf16[256,512]{1,0:T(8,128)(2,1)} %get-tuple-element.43) | copy-start | bytes 786436
  105.9 23.6 %copy-start.17 = (bf16[256,512]{1,0:T(8,128)(2,1)S(1)}, bf16[256,512]{1,0:T(8,128)(2,1)}, u32[]{:S(2)}) copy-start(bf16[256,512]{1,0:T(8,128)(2,1)} %get-tuple-element.44) | copy-start | bytes 786436
  105.9 23.6 %copy-start.18 = (bf16[256,512]{1,0:T(8,128)(2,1)S(1)}, bf16[256,512]{1,0:T(8,128)(2,1)}, u32[]{:S(2)}) copy-start(bf16[256,512]{1,0:T(8,128)(2,1)} %get-tuple-element.45) | copy-start | bytes 786436
  105.9 23.6 %copy-start.19 = (bf16[256,512]{1,0:T(8,128)(2,1)S(1)}, bf16[256,512]{1,0:T(8,128)(2,1)}, u32[]{:S(2)}) copy-start(bf16[256,512]{1,0:T(8,128)(2,1)} %get-tuple-element.46) | copy-start | bytes 786436
  122.6 16.5 %collective-permute-start.11 = (bf16[1024,128]{1,0:T(8,128)(2,1)S(1)}, bf16[1024,128]{1,0:T(8,128)(2,1)S(1)}, u32[]{:S(2)}, u32[]{:S(2)}) collective-permute-start(bf16[1024,128]{1,0:T(8,128)(2,1)S(1)} %slice.101), channel_id=1, source_target_pairs={{0,32},{32,64},{64,96},{96,0},{1,33},{33,65},{65,97},{97,1},{2,34}... | collective-permute-start | bytes 786440 | tf_op jit(solution)/shard_map/ppermute | solution.py:53
  124.6 14.5 %collective-permute-start.12 = (bf16[1024,128]{1,0:T(8,128)(2,1)S(1)}, bf16[1024,128]{1,0:T(8,128)(2,1)S(1)}, u32[]{:S(2)}, u32[]{:S(2)}) collective-permute-start(bf16[1024,128]{1,0:T(8,128)(2,1)S(1)} %slice.102), channel_id=1, source_target_pairs={{0,96},{32,0},{64,32},{96,64},{1,97},{33,1},{65,33},{97,65},{2,98}... | collective-permute-start | bytes 786440 | tf_op jit(solution)/shard_map/ppermute | solution.py:53
  129.5 1.0 copy-start.12
  129.5 1.0 copy-start.13
  129.5 1.1 copy-start.14
  129.5 1.2 copy-start.15
  130.6 8.5 %copy-start.8 = (bf16[256,512]{1,0:T(8,128)(2,1)S(1)}, bf16[256,512]{1,0:T(8,128)(2,1)}, u32[]{:S(2)}) copy-start(bf16[256,512]{1,0:T(8,128)(2,1)} %get-tuple-element.39) | copy-start | bytes 786436
  130.7 8.5 %copy-start.9 = (bf16[256,512]{1,0:T(8,128)(2,1)S(1)}, bf16[256,512]{1,0:T(8,128)(2,1)}, u32[]{:S(2)}) copy-start(bf16[256,512]{1,0:T(8,128)(2,1)} %get-tuple-element.40) | copy-start | bytes 786436
  130.7 8.5 %copy-start.10 = (bf16[256,512]{1,0:T(8,128)(2,1)S(1)}, bf16[256,512]{1,0:T(8,128)(2,1)}, u32[]{:S(2)}) copy-start(bf16[256,512]{1,0:T(8,128)(2,1)} %get-tuple-element.41) | copy-start | bytes 786436
  130.7 8.5 %copy-start.11 = (bf16[256,512]{1,0:T(8,128)(2,1)S(1)}, bf16[256,512]{1,0:T(8,128)(2,1)}, u32[]{:S(2)}) copy-start(bf16[256,512]{1,0:T(8,128)(2,1)} %get-tuple-element.42) | copy-start | bytes 786436
  139.1 1.0 copy-start.4
  139.2 1.0 copy-start.5
  139.2 1.1 copy-start.6
  139.2 1.2 copy-start.7
  140.3 42.9 %copy-start.24 = (s32[64,1]{0,1:T(1,128)S(1)}, s32[64,1]{0,1:T(1,128)}, u32[]{:S(2)}) copy-start(s32[64,1]{0,1:T(1,128)} %reshape.253) | copy-start | bytes 772
  142.6 54.7 %all-to-all-start.1 = ((bf16[8,32,320]{2,0,1:T(8,128)(2,1)}), bf16[8,32,320]{2,0,1:T(8,128)(2,1)S(1)}, u32[]{:S(2)}, u32[]{:S(2)}) async-start(bf16[8,32,320]{2,0,1:T(8,128)(2,1)} %pad_maximum_fusion), calls=%async_computation.1 | async-start | bytes 393216 | tf_op jit(solution)/shard_map/all_to_all | solution.py:33
  197.4 4.1 %copy-start.25 = (s32[256]{0:T(256)S(1)}, s32[256]{0:T(256)}, u32[]{:S(2)}) copy-start(s32[256]{0:T(256)} %param.15) | copy-start | bytes 3076
  197.4 54.0 %all-to-all-start.2 = ((bf16[32,2,2,8,1024]{4,3,2,1,0:T(8,128)(2,1)}), bf16[32,2,2,8,1024]{4,3,2,1,0:T(8,128)(2,1)S(1)}, u32[]{:S(2)}, u32[]{:S(2)}) async-start(bf16[32,2,2,8,1024]{4,3,2,1,0:T(8,128)(2,1)} %bitcast.30), calls=%async_computation.2 | async-start | bytes 4194304 | tf_op jit(solution)/shard_map/all_to_all | solution.py:160
Sparse Core Ops, SparseCore 0:
  90.0 103.1 all-gather.2

commit v8 on v6

--- a/solution.py
+++ b/solution.py
@@ -83,21 +83,36 @@
     floats = hidden.astype(jnp.float32)
     scale_rms = lax.rsqrt(jnp.mean(floats * floats, axis=-1, keepdims=True) + 1e-05)
     normed = (floats * scale_rms * norm_gain.astype(jnp.float32)).astype(jnp.bfloat16)
+    blk_dev = kv_cache.shape[0]
+    most_slots = max(2, 2 * blk_dev // columns)
+    sources = kept_parent_device.reshape(columns, blk_dev)
+    picked = keep_block.reshape(columns, blk_dev)
+    is_mine = (sources == my_column).astype(jnp.int32)
+    ranks = jnp.cumsum(is_mine, axis=1) - 1
+    slot_ids = jnp.arange(most_slots, dtype=jnp.int32)
+    chosen = is_mine[:, :, None] * (ranks[:, :, None] == slot_ids[None, None, :]).astype(jnp.int32)
+    send_table = jnp.sum(chosen * picked[:, :, None], axis=1)
+    outgoing = kv_cache[send_table.reshape(-1)].reshape((columns, most_slots) + kv_cache.shape[1:])
+    incoming_blocks = lax.all_to_all(outgoing, BEAM, split_axis=0, concat_axis=0, tiled=True)
     stack = gather_rows(w_qkv, "yh", lax.axis_size("yh"))
     xs = lax.axis_size("x")
     assert xs == 4
     me = lax.axis_index("x")
     ahead = [(i, (i + 1) % xs) for i in range(xs)]
     behind = [(i, (i - 1) % xs) for i in range(xs)]
-    from_left = lax.ppermute(stack, "x", ahead)
-    from_right = lax.ppermute(stack, "x", behind)
-    w_local, from_left, from_right = lax.optimization_barrier((w_local, from_left, from_right))
+    cut = stack.shape[0] // 2
+    left_top = lax.ppermute(stack[:cut], "x", ahead)
+    left_low = lax.ppermute(stack[cut:], "x", ahead)
+    right_top = lax.ppermute(stack[:cut], "x", behind)
+    right_low = lax.ppermute(stack[cut:], "x", behind)
+    w_local, left_top, right_low = lax.optimization_barrier((w_local, left_top, right_low))
     w_pair = lax.all_gather(w_local[:, None], OWNER, axis=1, tiled=True)
-    cut = stack.shape[0] // 2
-    far = jnp.concatenate(
-        [lax.ppermute(from_left[:cut], "x", ahead), lax.ppermute(from_right[cut:], "x", behind)],
-        axis=0,
-    )
+    far_top = lax.ppermute(left_top, "x", ahead)
+    far_low = lax.ppermute(right_low, "x", behind)
+    incoming_blocks, far_top, far_low = lax.optimization_barrier((incoming_blocks, far_top, far_low))
+    from_left = jnp.concatenate([left_top, left_low], axis=0)
+    from_right = jnp.concatenate([right_top, right_low], axis=0)
+    far = jnp.concatenate([far_top, far_low], axis=0)
     rows = stack.shape[0]
     projected = None
     for step, piece in ((0, stack), (1, from_right), (3, from_left), (2, far)):
@@ -111,17 +126,6 @@
         )
         projected = term if projected is None else projected + term
     own_qkv = regroup(projected.astype(jnp.bfloat16)).reshape(own_beams, QKV)
-    blk_dev = kv_cache.shape[0]
-    most_slots = max(2, 2 * blk_dev // columns)
-    sources = kept_parent_device.reshape(columns, blk_dev)
-    picked = keep_block.reshape(columns, blk_dev)
-    is_mine = (sources == my_column).astype(jnp.int32)
-    ranks = jnp.cumsum(is_mine, axis=1) - 1
-    slot_ids = jnp.arange(most_slots, dtype=jnp.int32)
-    chosen = is_mine[:, :, None] * (ranks[:, :, None] == slot_ids[None, None, :]).astype(jnp.int32)
-    send_table = jnp.sum(chosen * picked[:, :, None], axis=1)
-    outgoing = kv_cache[send_table.reshape(-1)].reshape((columns, most_slots) + kv_cache.shape[1:])
-    incoming_blocks = lax.all_to_all(outgoing, BEAM, split_axis=0, concat_axis=0, tiled=True)
     own_sources = lax.dynamic_index_in_dim(sources, my_column, 0, keepdims=False)
     one_hot = (own_sources[:, None] == jnp.arange(columns, dtype=jnp.int32)[None, :]).astype(
         jnp.int32

time: 248 us -> 254 us (1.024)
  waiting for transfers between devices: 52.4 us -> 67.3 us
  blocking collectives: 77.1 us -> 69.1 us
  local copies, waits for them, and re-layouts: 25.7 us -> 22.5 us
    ppermute x4 -> x6, waiting for transfers between devices: 5.71 us -> 32 us  [the longest x1 11 us: shards(): left_top = lax.ppermute(stack[:cut], 'x', ahead)]
    all_to_all x1, starting transfers between devices: 15 us -> 6.76 us  [regroup(): return lax.all_to_all(blocks, BEAM, split_axis=1, concat_axis=1, tiled=True)]
    all_to_all x1, waiting for transfers between devices: 7.18 us -> 0.01 us  [shards(): lax.all_to_all(outgoing, BEAM, split_axis=0, concat_axis=0, tiled=True)]
    ppermute x4 -> x6, starting transfers between devices: 14.1 us -> 20.8 us  [the longest x1 4.85 us: shards(): right_top = lax.ppermute(stack[:cut], 'x', behind)]
    all_to_all x1, waiting for transfers between devices: 23.9 us -> 18.8 us  [gather_rows(): lax.all_to_all(copies, axis, 0, 0, tiled=True)]
    all_to_all x1, blocking collectives: 20.7 us -> 15.7 us  [shards(): lax.all_to_all(doubled.reshape(own_beams, columns, pair_feats.shape[3]),...]
    all_to_all x1, blocking collectives: 56.4 us -> 53.3 us  [shards(): spread = lax.all_to_all(partial.transpose(1, 0, 2), PAIR, 0, 0, tiled=True)]
  transfers between devices with their start and end apart: 9 -> 11, of which waited for: 5 -> 7; matrix products, arithmetic and copies ran while one was open for 16% -> 15% of each run, Pallas kernels for 0% -> 0%
where the time goes in v8:
time: 254 us; the launch traced here: 250 us
  blocking collectives  69.1 us (27%)
  waiting for transfers between devices  67.3 us (26%)
  starting transfers between devices  50.6 us (20%)
  local copies, waits for them, and re-layouts  22.5 us (9%)
  matrix products  14.3 us (6%)
  between operations  13.8 us (5%)
  other arithmetic  12.3 us (5%)
    all_to_all x1, blocking collectives, shards(): spread = lax.all_to_all(partial.transpose(1, 0, 2), PAIR, 0, 0, tiled=True)  53.3 us
    all_to_all x1, waiting for transfers between devices, gather_rows(): lax.all_to_all(copies, axis, 0, 0, tiled=True)  18.8 us
    all_to_all x1, waiting for transfers between devices, regroup(): return lax.all_to_all(blocks, BEAM, split_axis=1, concat_axis=1, tiled=True)  16.5 us
    all_to_all x1, blocking collectives, shards(): lax.all_to_all(doubled.reshape(own_beams, columns, pair_feats.shape[3]),...  15.7 us
    all_to_all x1, starting transfers between devices, shards(): lax.all_to_all(outgoing, BEAM, split_axis=0, concat_axis=0, tiled=True)  13.9 us
    dot_general x4, matrix products, shards(): jnp.einsum('jbd,dc->bjc', block.reshape(columns, own_beams, rows), piece,...  11.7 us
    ppermute x1, waiting for transfers between devices, shards(): left_top = lax.ppermute(stack[:cut], 'x', ahead)  11 us
    ppermute x1, waiting for transfers between devices, shards(): far_top = lax.ppermute(left_top, 'x', ahead)  10.5 us
  transfers between devices with their start and end apart: 11, of which 7 were waited for; matrix products, arithmetic and copies ran while one was open for 15% of the time, Pallas kernels for 0%

profile of v8, /device:TPU:56, one launch (start us, length us, event | category | flops | bytes accessed | tf_op | source)
XLA Modules:
  0.0 250.0 jit_solution(14059543299069492502)
XLA Ops:
  6.5 2.3 broadcast_in_dim.29
  8.8 7.1 %all-to-all-start = ((bf16[4,512,320]{1,2,0:T(8,128)(2,1)}), bf16[4,512,320]{1,2,0:T(8,128)(2,1)S(1)}, u32[]{:S(2)}, u32[]{:S(2)}) async-start(bf16[4,512,320]{1,2,0:T(8,128)(2,1)} %broadcast_in_dim.29), calls=%async_computation | async-start | bytes 2621440 | tf_op jit(solution)/shard_map/all_to_all | solution.py:38
  15.9 0.1 copy.73
  16.1 1.9 collective-permute-start
  18.0 0.5 broadcast.199
  18.6 0.7 reduce.4
  19.3 0.2 reduce_window_sum.22
  19.6 0.1 multiply_reduce_fusion
  19.7 0.1 copy.83
  19.8 0.1 reshape.237
  19.9 2.0 gather_fusion
  21.9 3.1 %fusion = f32[256]{0:T(256)S(1)} fusion(bf16[256,8192]{1,0:T(8,128)(2,1)} %param.10), kind=kLoop, calls=%fused_computation.4 | loop fusion | flops 6291200 | bytes 4195328 | tf_op jit(solution)/shard_map/reduce_sum | solution.py:84
  25.1 18.8 %all-to-all-done = bf16[4,512,320]{1,2,0:T(8,128)(2,1)S(1)} async-done(((bf16[4,512,320]{1,2,0:T(8,128)(2,1)}), bf16[4,512,320]{1,2,0:T(8,128)(2,1)S(1)}, u32[]{:S(2)}, u32[]{:S(2)}) %all-to-all-start) | async-done | bytes 1310752 | tf_op jit(solution)/shard_map/all_to_all | solution.py:38
  43.8 13.9 %all-to-all-start.1 = ((bf16[32,2,2,8,1024]{4,3,2,1,0:T(8,128)(2,1)}), bf16[32,2,2,8,1024]{4,3,2,1,0:T(8,128)(2,1)}, u32[]{:S(2)}, u32[]{:S(2)}) async-start(bf16[32,2,2,8,1024]{4,3,2,1,0:T(8,128)(2,1)} %bitcast.127), calls=%async_computation.1 | async-start | bytes 4194304 | tf_op jit(solution)/shard_map/all_to_all | solution.py:96
  57.8 0.1 slice_bitcast_fusion
  57.9 0.9 copy.112
  58.8 3.4 %collective-permute-start.1 = (bf16[1024,320]{0,1:T(8,128)(2,1)}, bf16[1024,320]{0,1:T(8,128)(2,1)}, u32[]{:S(2)}, u32[]{:S(2)}) collective-permute-start(bf16[1024,320]{0,1:T(8,128)(2,1)} %bitcast.52), channel_id=1, source_target_pairs={{0,128},{128,256},{256,384},{384,0},{1,129},{129,257},{257,385},{3... | collective-permute-start | bytes 1966088 | tf_op jit(solution)/shard_map/ppermute | solution.py:104
  62.2 0.9 copy.113
  63.1 3.6 %collective-permute-start.2 = (bf16[1024,320]{0,1:T(8,128)(2,1)}, bf16[1024,320]{0,1:T(8,128)(2,1)}, u32[]{:S(2)}, u32[]{:S(2)}) collective-permute-start(bf16[1024,320]{0,1:T(8,128)(2,1)} %bitcast.54), channel_id=1, source_target_pairs={{0,384},{128,0},{256,128},{384,256},{1,385},{129,1},{257,129},{385... | collective-permute-start | bytes 1966088 | tf_op jit(solution)/shard_map/ppermute | solution.py:107
  66.9 0.1 fusion.53
  67.0 0.2 select_reduce_fusion
  67.2 0.8 maximum_select_fusion
  68.1 11.0 %collective-permute-done.1 = bf16[1024,320]{0,1:T(8,128)(2,1)} collective-permute-done((bf16[1024,320]{0,1:T(8,128)(2,1)}, bf16[1024,320]{0,1:T(8,128)(2,1)}, u32[]{:S(2)}, u32[]{:S(2)}) %collective-permute-start.1) | collective-permute-done | bytes 655392 | tf_op jit(solution)/shard_map/ppermute | solution.py:104
  79.0 2.8 %collective-permute-done.2 = bf16[1024,320]{0,1:T(8,128)(2,1)} collective-permute-done((bf16[1024,320]{0,1:T(8,128)(2,1)}, bf16[1024,320]{0,1:T(8,128)(2,1)}, u32[]{:S(2)}, u32[]{:S(2)}) %collective-permute-start.2) | collective-permute-done | bytes 655392 | tf_op jit(solution)/shard_map/ppermute | solution.py:107
  81.9 3.6 %fusion.2 = bf16[256,8192]{1,0:T(8,128)(2,1)S(1)} fusion(bf16[256,8192]{1,0:T(8,128)(2,1)} %param.10, f32[8192]{0:T(1024)S(1)} %convert_element_type.100, f32[256]{0:T(256)S(1)} %add_rsqrt_fusion), kind=kLoop, calls=%fused_computation.6 | loop fusion | flops 8388608 | bytes 8422400 | tf_op jit(solution)/shard_map/convert_element_type | solution.py:85
  85.5 1.9 dynamic-slice_bitcast_fusion.2
  87.4 0.7 copy-done.1
  88.1 4.9 %collective-permute-start.3 = (bf16[1024,320]{0,1:T(8,128)(2,1)}, bf16[1024,320]{0,1:T(8,128)(2,1)}, u32[]{:S(2)}, u32[]{:S(2)}) collective-permute-start(bf16[1024,320]{0,1:T(8,128)(2,1)} %bitcast.52), channel_id=1, source_target_pairs={{0,384},{128,0},{256,128},{384,256},{1,385},{129,1},{257,129},{385... | collective-permute-start | bytes 1966088 | tf_op jit(solution)/shard_map/ppermute | solution.py:106
  93.0 0.1 multiply_cosine_fusion
  93.1 1.9 collective-permute-start.4
  95.1 2.4 collective-permute-start.5
  97.5 4.6 %collective-permute-start.6 = (bf16[1024,320]{0,1:T(8,128)(2,1)}, bf16[1024,320]{0,1:T(8,128)(2,1)}, u32[]{:S(2)}, u32[]{:S(2)}) collective-permute-start(bf16[1024,320]{0,1:T(8,128)(2,1)} %collective-permute-done.2), channel_id=1, source_target_pairs={{0,384},{128,0},{256,128},{384,256},{1,385},{129,1},{257,129},{385... | collective-permute-start | bytes 1966088 | tf_op jit(solution)/shard_map/ppermute | solution.py:111
  102.2 2.1 copy.78
  104.3 3.0 %reshape.324 = bf16[2048,320,1]{0,1,2:T(8,128)(2,1)S(1)} reshape(bf16[4,512,320]{1,0,2:T(4,128)(2,1)} %copy.78) | data formatting | bytes 2621440 | tf_op jit(solution)/shard_map/reshape | solution.py:38
  107.3 5.3 %collective-permute-done.3 = bf16[1024,320]{0,1:T(8,128)(2,1)} collective-permute-done((bf16[1024,320]{0,1:T(8,128)(2,1)}, bf16[1024,320]{0,1:T(8,128)(2,1)}, u32[]{:S(2)}, u32[]{:S(2)}) %collective-permute-start.3) | collective-permute-done | bytes 655392 | tf_op jit(solution)/shard_map/ppermute | solution.py:106
  112.7 3.4 %fusion.4 = f32[320,32,8]{0,1,2:T(8,128)} fusion(bf16[1024,320]{0,1:T(8,128)(2,1)} %collective-permute-done.2, bf16[1024,320]{0,1:T(8,128)(2,1)} %collective-permute-done.3, bf16[32,8,2048]{2,1,0:T(8,128)(2,1)} %get-tuple-element.33), kind=kOutput, calls=%fused_computation.10 | convolution fusion | flops 338165760 | bytes 2686976 | tf_op jit(solution)/shard_map/jbd,dc->bjc/dot_general | solution.py:121
  116.0 2.3 collective-permute-done.4
  118.4 2.9 %fusion.7 = f32[320,32,8]{0,1,2:T(8,128)} fusion(bf16[1024,320]{0,1:T(8,128)(2,1)} %collective-permute-done.4, bf16[1024,320]{0,1:T(8,128)(2,1)} %collective-permute-done.1, bf16[32,8,2048]{2,1,0:T(8,128)(2,1)S(1)} %copy-done.2), kind=kOutput, calls=%fused_computation.14 | convolution fusion | flops 338165760 | bytes 2686976 | tf_op jit(solution)/shard_map/jbd,dc->bjc/dot_general | solution.py:121
  121.3 10.5 %collective-permute-done.5 = bf16[1024,320]{0,1:T(8,128)(2,1)} collective-permute-done((bf16[1024,320]{0,1:T(8,128)(2,1)}, bf16[1024,320]{0,1:T(8,128)(2,1)}, u32[]{:S(2)}, u32[]{:S(2)}) %collective-permute-start.5) | collective-permute-done | bytes 655392 | tf_op jit(solution)/shard_map/ppermute | solution.py:110
  131.9 2.3 fusion.10
  134.1 3.2 %fusion.24 = bf16[8,32,320]{2,0,1:T(8,128)(2,1)} fusion(f32[320,32,8]{0,1,2:T(8,128)S(1)} %fusion.10, f32[320,32,8]{0,1,2:T(8,128)S(1)} %copy-done.4, f32[320,32,8]{0,1,2:T(8,128)S(1)} %copy-done.3, bf16[2048,320,1]{0,1,2:T(8,128)(2,1)S(1)} %reshape.324, bf16[256,8192]{1,0:T(8,128)(2,1)} %copy-done.1, s32[]{:T(128)S(6)} %select_n.83), kind=kOutput, calls=%fused_computation.41 | convolution fusion | flops 335872000 | bytes 3506180 | tf_op jit(solution)/shard_map/jbd,dc->bjc/dot_general | solution.py:121
  137.3 6.8 %all-to-all-start.2 = ((bf16[8,32,320]{2,0,1:T(8,128)(2,1)}), bf16[8,32,320]{2,0,1:T(8,128)(2,1)S(1)}, u32[]{:S(2)}, u32[]{:S(2)}) async-start(bf16[8,32,320]{2,0,1:T(8,128)(2,1)} %fusion.24), calls=%async_computation.2 | async-start | bytes 393216 | tf_op jit(solution)/shard_map/all_to_all | solution.py:33
  144.1 2.2 gather_fusion.1
  146.3 0.3 copy.114
  146.7 16.5 %all-to-all-done.2 = bf16[8,32,320]{2,0,1:T(8,128)(2,1)S(1)} async-done(((bf16[8,32,320]{2,0,1:T(8,128)(2,1)}), bf16[8,32,320]{2,0,1:T(8,128)(2,1)S(1)}, u32[]{:S(2)}, u32[]{:S(2)}) %all-to-all-start.2) | async-done | bytes 163872 | tf_op jit(solution)/shard_map/all_to_all | solution.py:33
  163.2 0.2 reshape.240
  163.5 0.1 subtract_convert_fusion.1
  163.5 0.1 maximum_bitcast_fusion.6
  163.6 0.1 fusion.57
  163.8 0.1 fusion.26
  163.9 0.3 fusion.34
  164.2 0.5 fusion.58
  164.7 0.3 fusion.25
  165.0 0.3 fusion.14
  165.4 0.1 convert_element_type.116
  165.5 0.1 copy.92
  165.6 15.7 %all_to_all.25 = bf16[8,32,512]{2,0,1:T(8,128)(2,1)S(1)} all-to-all(bf16[8,32,512]{2,0,1:T(8,128)(2,1)S(1)} %bitcast.134), channel_id=1, replica_groups=mesh['x'=4,'yh'=4,'yl'=2,'z'=8,'c'=2] {'yl','z','c'}, dimensions={1} | all-to-all | bytes 524288 | tf_op jit(solution)/shard_map/all_to_all | solution.py:150
  181.4 2.5 fusion.54
  183.9 0.7 fusion.29
  184.6 0.7 fusion.3
  185.4 1.2 copy.97
  186.5 0.7 copy.98
  187.3 53.3 %all_to_all.26 = bf16[16,256,256]{2,1,0:T(8,128)(2,1)} all-to-all(bf16[16,256,256]{2,1,0:T(8,128)(2,1)S(1)} %copy.98), channel_id=1, replica_groups=mesh['x'=4,'yh'=4,'yl'=2,'z'=8,'c'=2] {'yl','z'}, dimensions={0} | all-to-all | bytes 4194304 | tf_op jit(solution)/shard_map/all_to_all | solution.py:164
  240.6 2.6 %reduce_sum.55 = bf16[256,256]{1,0:T(8,128)(2,1)} reduce(bf16[16,256,256]{2,1,0:T(8,128)(2,1)} %all_to_all.26, bf16[]{:T(256)} %constant.113.clone.1), dimensions={0}, to_apply=%region_7.9 | reduce | flops 983040 | bytes 2228226 | tf_op jit(solution)/shard_map/reduce_sum | solution.py:165
  (50 shorter events, 0.8 us)
Async XLA Ops:
  6.5 13.4 %copy-start = (bf16[32,2,8,1024]{3,2,1,0:T(8,128)(2,1)S(1)}, bf16[32,2,8,1024]{3,2,1,0:T(8,128)(2,1)}, u32[]{:S(2)}) copy-start(bf16[32,2,8,1024]{3,2,1,0:T(8,128)(2,1)} %param.14) | copy-start | bytes 3145732
  6.5 9.4 %copy-start.5 = (bf16[256,512]{1,0:T(8,128)(2,1)S(1)}, bf16[256,512]{1,0:T(8,128)(2,1)}, u32[]{:S(2)}) copy-start(bf16[256,512]{1,0:T(8,128)(2,1)} %param.13) | copy-start | bytes 786436
  8.8 9.8 %copy-start.8 = (s32[1024,1]{0,1:T(1,128)S(1)}, s32[1024,1]{0,1:T(1,128)}, u32[]{:S(2)}) copy-start(s32[1024,1]{0,1:T(1,128)} %param.16) | copy-start | bytes 12292
  8.8 10.7 %copy-start.7 = (s32[1024]{0:T(1024)S(1)}, s32[1024]{0:T(1024)}, u32[]{:S(2)}) copy-start(s32[1024]{0:T(1024)} %param.17) | copy-start | bytes 12292
  8.8 35.0 %all-to-all-start = ((bf16[4,512,320]{1,2,0:T(8,128)(2,1)}), bf16[4,512,320]{1,2,0:T(8,128)(2,1)S(1)}, u32[]{:S(2)}, u32[]{:S(2)}) async-start(bf16[4,512,320]{1,2,0:T(8,128)(2,1)} %broadcast_in_dim.29), calls=%async_computation | async-start | bytes 2621440 | tf_op jit(solution)/shard_map/all_to_all | solution.py:38
  16.1 51.1 %collective-permute-start = (bf16[256,256]{0,1:T(8,128)(2,1)S(1)}, bf16[256,256]{0,1:T(8,128)(2,1)S(1)}, u32[]{:S(2)}, u32[]{:S(2)}) collective-permute-start(bf16[256,256]{0,1:T(8,128)(2,1)S(1)} %get-tuple-element.47), channel_id=1, source_target_pairs={{0,1},{1,0},{2,3},{3,2},{4,5},{5,4},{6,7},{7,6},{8,9},{9,8},{10,11... | collective-permute-start | bytes 393224 | tf_op jit(solution)/shard_map/ppermute | solution.py:81
  43.8 88.0 %all-to-all-start.1 = ((bf16[32,2,2,8,1024]{4,3,2,1,0:T(8,128)(2,1)}), bf16[32,2,2,8,1024]{4,3,2,1,0:T(8,128)(2,1)}, u32[]{:S(2)}, u32[]{:S(2)}) async-start(bf16[32,2,2,8,1024]{4,3,2,1,0:T(8,128)(2,1)} %bitcast.127), calls=%async_computation.1 | async-start | bytes 4194304 | tf_op jit(solution)/shard_map/all_to_all | solution.py:96
  57.8 9.1 %copy-start.9 = (s32[256]{0:T(256)S(1)}, s32[256]{0:T(256)}, u32[]{:S(2)}) copy-start(s32[256]{0:T(256)} %param.15) | copy-start | bytes 3076
  57.8 9.2 %copy-start.6 = (bf16[8192]{0:T(1024)(128)(2,1)S(1)}, bf16[8192]{0:T(1024)(128)(2,1)}, u32[]{:S(2)}) copy-start(bf16[8192]{0:T(1024)(128)(2,1)} %param.11) | copy-start | bytes 49156
  57.8 123.6 %all-gather.3.cloned.1.call-start = ((), (), s32[]{:S(2)}) async-start(), calls=%async_computation.5 | async-start | bytes 4456448 | tf_op jit(solution)/shard_map/all_gather | solution.py:109
  58.8 20.2 %collective-permute-start.1 = (bf16[1024,320]{0,1:T(8,128)(2,1)}, bf16[1024,320]{0,1:T(8,128)(2,1)}, u32[]{:S(2)}, u32[]{:S(2)}) collective-permute-start(bf16[1024,320]{0,1:T(8,128)(2,1)} %bitcast.52), channel_id=1, source_target_pairs={{0,128},{128,256},{256,384},{384,0},{1,129},{129,257},{257,385},{3... | collective-permute-start | bytes 1966088 | tf_op jit(solution)/shard_map/ppermute | solution.py:104
  63.1 18.7 %collective-permute-start.2 = (bf16[1024,320]{0,1:T(8,128)(2,1)}, bf16[1024,320]{0,1:T(8,128)(2,1)}, u32[]{:S(2)}, u32[]{:S(2)}) collective-permute-start(bf16[1024,320]{0,1:T(8,128)(2,1)} %bitcast.54), channel_id=1, source_target_pairs={{0,384},{128,0},{256,128},{384,256},{1,385},{129,1},{257,129},{385... | collective-permute-start | bytes 1966088 | tf_op jit(solution)/shard_map/ppermute | solution.py:107
  85.5 2.6 %copy-start.1 = (bf16[256,8192]{1,0:T(8,128)(2,1)}, bf16[256,8192]{1,0:T(8,128)(2,1)S(1)}, u32[]{:S(2)}) copy-start(bf16[256,8192]{1,0:T(8,128)(2,1)S(1)} %fusion.2) | copy-start | bytes 12582916
  88.1 24.6 %collective-permute-start.3 = (bf16[1024,320]{0,1:T(8,128)(2,1)}, bf16[1024,320]{0,1:T(8,128)(2,1)}, u32[]{:S(2)}, u32[]{:S(2)}) collective-permute-start(bf16[1024,320]{0,1:T(8,128)(2,1)} %bitcast.52), channel_id=1, source_target_pairs={{0,384},{128,0},{256,128},{384,256},{1,385},{129,1},{257,129},{385... | collective-permute-start | bytes 1966088 | tf_op jit(solution)/shard_map/ppermute | solution.py:106
  93.1 25.3 %collective-permute-start.4 = (bf16[1024,320]{0,1:T(8,128)(2,1)}, bf16[1024,320]{0,1:T(8,128)(2,1)}, u32[]{:S(2)}, u32[]{:S(2)}) collective-permute-start(bf16[1024,320]{0,1:T(8,128)(2,1)} %bitcast.54), channel_id=1, source_target_pairs={{0,128},{128,256},{256,384},{384,0},{1,129},{129,257},{257,385},{3... | collective-permute-start | bytes 1966088 | tf_op jit(solution)/shard_map/ppermute | solution.py:105
  95.1 36.8 %collective-permute-start.5 = (bf16[1024,320]{0,1:T(8,128)(2,1)}, bf16[1024,320]{0,1:T(8,128)(2,1)}, u32[]{:S(2)}, u32[]{:S(2)}) collective-permute-start(bf16[1024,320]{0,1:T(8,128)(2,1)} %collective-permute-done.1), channel_id=1, source_target_pairs={{0,128},{128,256},{256,384},{384,0},{1,129},{129,257},{257,385},{3... | collective-permute-start | bytes 1966088 | tf_op jit(solution)/shard_map/ppermute | solution.py:110
  97.5 34.3 %collective-permute-start.6 = (bf16[1024,320]{0,1:T(8,128)(2,1)}, bf16[1024,320]{0,1:T(8,128)(2,1)}, u32[]{:S(2)}, u32[]{:S(2)}) collective-permute-start(bf16[1024,320]{0,1:T(8,128)(2,1)} %collective-permute-done.2), channel_id=1, source_target_pairs={{0,384},{128,0},{256,128},{384,256},{1,385},{129,1},{257,129},{385... | collective-permute-start | bytes 1966088 | tf_op jit(solution)/shard_map/ppermute | solution.py:111
  112.7 5.7 %copy-start.2 = (bf16[32,8,2048]{2,1,0:T(8,128)(2,1)S(1)}, bf16[32,8,2048]{2,1,0:T(8,128)(2,1)}, u32[]{:S(2)}) copy-start(bf16[32,8,2048]{2,1,0:T(8,128)(2,1)} %get-tuple-element.35) | copy-start | bytes 3145732
  131.8 2.3 copy-start.3
  131.9 2.3 copy-start.4
  137.3 25.9 %all-to-all-start.2 = ((bf16[8,32,320]{2,0,1:T(8,128)(2,1)}), bf16[8,32,320]{2,0,1:T(8,128)(2,1)S(1)}, u32[]{:S(2)}, u32[]{:S(2)}) async-start(bf16[8,32,320]{2,0,1:T(8,128)(2,1)} %fusion.24), calls=%async_computation.2 | async-start | bytes 393216 | tf_op jit(solution)/shard_map/all_to_all | solution.py:33
Sparse Core Ops, SparseCore 0:
  82.0 82.7 all-gather.2

commit v9 on v6

--- a/solution.py
+++ b/solution.py
@@ -36,6 +36,28 @@
 def gather_rows(tile, axis, count):
     copies = jnp.broadcast_to(tile[None], (count,) + tile.shape)
     return lax.all_to_all(copies, axis, 0, 0, tiled=True).reshape((-1,) + tile.shape[1:])
+
+
+def place_ring(piece, axis, inner):
+    count = lax.axis_size(axis)
+    me = lax.axis_index(axis)
+    source = piece if inner is None else inner
+    ahead = [(i, (i + 1) % count) for i in range(count)]
+    behind = [(i, (i - 1) % count) for i in range(count)]
+    from_left = lax.ppermute(source, axis, ahead)
+    from_right = lax.ppermute(source, axis, behind)
+    cut = source.shape[0] // 2
+    far = jnp.concatenate(
+        [lax.ppermute(from_left[:cut], axis, ahead), lax.ppermute(from_right[cut:], axis, behind)],
+        axis=0,
+    )
+    placed = jnp.zeros((count,) + source.shape, source.dtype)
+    for step, part in ((0, source), (1, from_right), (2, far), (3, from_left)):
+        where = ((me + step) % count,) + (0,) * source.ndim
+        placed = lax.dynamic_update_slice(placed, part[None], where)
+    if inner is None:
+        return placed
+    return placed.reshape((-1,) + source.shape[1:])
 
 
 def attend(queries, fresh_key, value_new, keys, values, positions):
@@ -92,7 +114,7 @@
     from_left = lax.ppermute(stack, "x", ahead)
     from_right = lax.ppermute(stack, "x", behind)
     w_local, from_left, from_right = lax.optimization_barrier((w_local, from_left, from_right))
-    w_pair = lax.all_gather(w_local[:, None], OWNER, axis=1, tiled=True)
+    w_blocks = place_ring(w_local, "x", place_ring(w_local, "yh", None))
     cut = stack.shape[0] // 2
     far = jnp.concatenate(
         [lax.ppermute(from_left[:cut], "x", ahead), lax.ppermute(from_right[cut:], "x", behind)],
@@ -150,9 +172,9 @@
     partial = None
     for half in range(cores):
         term = jnp.einsum(
-            "bjh,hpc->jbpc",
+            "bjh,phc->jbpc",
             head_rows[:, :, half * block : (half + 1) * block],
-            w_pair[half * block : (half + 1) * block],
+            w_blocks[:, half * block : (half + 1) * block],
             preferred_element_type=jnp.float32,
         ).astype(jnp.bfloat16).astype(jnp.float32)
         partial = term if partial is None else partial + term

time: 248 us -> 269 us (1.085)
  starting transfers between devices: 52 us -> 81.1 us
  blocking collectives: 77.1 us -> 55.5 us
  between operations: 13.9 us -> 0.62 us
  local copies, waits for them, and re-layouts: 25.7 us -> 38.4 us
  other arithmetic: 12.4 us -> 19 us
  waiting for transfers between devices: 52.4 us -> 57.3 us
    ppermute x0 -> x8, starting transfers between devices: none -> 27.2 us  [the longest x2 7.19 us: place_ring(): lax.ppermute(from_right[cut:], axis, behind)]
    ppermute x0 -> x8, waiting for transfers between devices: none -> 22.9 us  [the longest x2 9.23 us: place_ring(): lax.ppermute(from_left[:cut], axis, ahead)]
    all_to_all x1 -> x0, blocking collectives: 20.7 us -> none  [shards(): lax.all_to_all(doubled.reshape(own_beams, columns, pair_feats.shape[3]),...]
    all_to_all x1, waiting for transfers between devices: 15.5 us -> 0.01 us  [regroup(): return lax.all_to_all(blocks, BEAM, split_axis=1, concat_axis=1, tiled=True)]
    ppermute x1, waiting for transfers between devices: 0.01 us -> 14.7 us  [shards(): from_left = lax.ppermute(stack, 'x', ahead)]
    all_to_all x0 -> x1, starting transfers between devices: none -> 8.31 us  [shards(): lax.all_to_all(doubled.reshape(own_beams, columns, pair_feats.shape[3]),...]
    dynamic_update_slice x0 -> x6, local copies, waits for them, and re-layouts: none -> 7.65 us  [place_ring(): placed = lax.dynamic_update_slice(placed, part[None], where)]
    all_to_all x1, waiting for transfers between devices: 7.18 us -> 0.01 us  [shards(): lax.all_to_all(outgoing, BEAM, split_axis=0, concat_axis=0, tiled=True)]
  transfers between devices with their start and end apart: 9 -> 17, of which waited for: 5 -> 8; matrix products, arithmetic and copies ran while one was open for 16% -> 21% of each run, Pallas kernels for 0% -> 0%
where the time goes in v9:
time: 269 us; the launch traced here: 266 us
  starting transfers between devices  81.1 us (30%)
  waiting for transfers between devices  57.3 us (21%)
  blocking collectives  55.5 us (21%)
  local copies, waits for them, and re-layouts  38.4 us (14%)
  other arithmetic  19 us (7%)
  matrix products  14.4 us (5%)
    all_to_all x1, blocking collectives, shards(): spread = lax.all_to_all(partial.transpose(1, 0, 2), PAIR, 0, 0, tiled=True)  55.5 us
    all_to_all x1, waiting for transfers between devices, gather_rows(): lax.all_to_all(copies, axis, 0, 0, tiled=True)  17.8 us
    ppermute x1, waiting for transfers between devices, shards(): from_left = lax.ppermute(stack, 'x', ahead)  14.7 us
    all_to_all x1, starting transfers between devices, shards(): lax.all_to_all(outgoing, BEAM, split_axis=0, concat_axis=0, tiled=True)  13.9 us
    ppermute x2, waiting for transfers between devices, place_ring(): lax.ppermute(from_left[:cut], axis, ahead)  9.23 us
    all_to_all x1, starting transfers between devices, regroup(): return lax.all_to_all(blocks, BEAM, split_axis=1, concat_axis=1, tiled=True)  8.5 us
    dot_general x4, matrix products, shards(): jnp.einsum('jbd,dc->bjc', block.reshape(columns, own_beams, rows), piece,...  8.47 us
    all_to_all x1, starting transfers between devices, shards(): lax.all_to_all(doubled.reshape(own_beams, columns, pair_feats.shape[3]),...  8.31 us
  transfers between devices with their start and end apart: 17, of which 8 were waited for; matrix products, arithmetic and copies ran while one was open for 21% of the time, Pallas kernels for 0%

profile of v9, /device:TPU:56, one launch (start us, length us, event | category | flops | bytes accessed | tf_op | source)
XLA Modules:
  0.0 266.3 jit_solution(16079245950051420669)
XLA Ops:
  0.0 2.3 broadcast_in_dim.53
  2.3 7.1 %all-to-all-start = ((bf16[4,512,320]{1,2,0:T(8,128)(2,1)}), bf16[4,512,320]{1,2,0:T(8,128)(2,1)S(1)}, u32[]{:S(2)}, u32[]{:S(2)}) async-start(bf16[4,512,320]{1,2,0:T(8,128)(2,1)} %broadcast_in_dim.53), calls=%async_computation | async-start | bytes 2621440 | tf_op jit(solution)/shard_map/all_to_all | solution.py:38
  10.0 0.7 fusion.35
  10.7 1.9 collective-permute-start
  13.1 0.6 reduce.4
  14.4 2.0 gather_fusion
  16.4 3.1 %fusion = f32[256]{0:T(256)S(1)} fusion(bf16[256,8192]{1,0:T(8,128)(2,1)} %param.10), kind=kLoop, calls=%fused_computation.4 | loop fusion | flops 6291200 | bytes 4195328 | tf_op jit(solution)/shard_map/reduce_sum | solution.py:106
  19.6 17.8 %all-to-all-done = bf16[4,512,320]{1,2,0:T(8,128)(2,1)S(1)} async-done(((bf16[4,512,320]{1,2,0:T(8,128)(2,1)}), bf16[4,512,320]{1,2,0:T(8,128)(2,1)S(1)}, u32[]{:S(2)}, u32[]{:S(2)}) %all-to-all-start) | async-done | bytes 1310752 | tf_op jit(solution)/shard_map/all_to_all | solution.py:38
  37.3 13.9 %all-to-all-start.2 = ((bf16[32,2,2,8,1024]{4,3,2,1,0:T(8,128)(2,1)}), bf16[32,2,2,8,1024]{4,3,2,1,0:T(8,128)(2,1)}, u32[]{:S(2)}, u32[]{:S(2)}) async-start(bf16[32,2,2,8,1024]{4,3,2,1,0:T(8,128)(2,1)} %bitcast.148), calls=%async_computation.2 | async-start | bytes 4194304 | tf_op jit(solution)/shard_map/all_to_all | solution.py:146
  51.2 5.3 %fusion.2 = bf16[256,8192]{1,0:T(8,128)(2,1)} fusion(bf16[256,8192]{1,0:T(8,128)(2,1)} %param.10, f32[8192]{0:T(1024)S(1)} %convert_element_type.100, f32[256]{0:T(256)S(1)} %add_rsqrt_fusion), kind=kLoop, calls=%fused_computation.6 | loop fusion | flops 8388608 | bytes 8422400 | tf_op jit(solution)/shard_map/convert_element_type | solution.py:107
  57.0 0.6 iota_compare_fusion.2
  57.6 1.2 copy.80
  58.8 3.4 %collective-permute-start.1 = (bf16[2048,320]{0,1:T(8,128)(2,1)}, bf16[2048,320]{0,1:T(8,128)(2,1)}, u32[]{:S(2)}, u32[]{:S(2)}) collective-permute-start(bf16[2048,320]{0,1:T(8,128)(2,1)} %bitcast.56), channel_id=1, source_target_pairs={{0,128},{128,256},{256,384},{384,0},{1,129},{129,257},{257,385},{3... | collective-permute-start | bytes 3932168 | tf_op jit(solution)/shard_map/ppermute | solution.py:114
  62.2 3.7 %collective-permute-start.2 = (bf16[2048,320]{0,1:T(8,128)(2,1)}, bf16[2048,320]{0,1:T(8,128)(2,1)}, u32[]{:S(2)}, u32[]{:S(2)}) collective-permute-start(bf16[2048,320]{0,1:T(8,128)(2,1)} %bitcast.56), channel_id=1, source_target_pairs={{0,384},{128,0},{256,128},{384,256},{1,385},{129,1},{257,129},{385... | collective-permute-start | bytes 3932168 | tf_op jit(solution)/shard_map/ppermute | solution.py:115
  65.9 0.7 multiply_cosine_fusion
  66.6 3.5 %dynamic-slice_bitcast_fusion.2 = (bf16[32,8,2048]{2,1,0:T(8,128)(2,1)}, bf16[32,8,2048]{2,1,0:T(8,128)(2,1)}, bf16[32,8,2048]{2,1,0:T(8,128)(2,1)S(1)}) fusion(bf16[256,8192]{1,0:T(8,128)(2,1)} %fusion.2, s32[]{:T(128)S(6)} %select_n.147, s32[]{:T(128)S(6)} %select_n.149, s32[]{:T(128)S(6)} %select_n.148), kind=kLoop, calls=%fused_computation.39 | loop fusion | bytes 6291468 | tf_op jit(solution)/shard_map/reshape | solution.py:130
  70.1 0.6 fusion.50
  70.7 0.7 pad_clamp_fusion
  71.4 1.7 maximum_select_fusion
  73.2 2.1 copy.51
  75.3 3.0 %reshape.323 = bf16[2048,320,1]{0,1,2:T(8,128)(2,1)S(1)} reshape(bf16[4,512,320]{1,0,2:T(4,128)(2,1)} %copy.51) | data formatting | bytes 2621440 | tf_op jit(solution)/shard_map/reshape | solution.py:38
  78.3 14.7 %collective-permute-done.1 = bf16[2048,320]{0,1:T(8,128)(2,1)} collective-permute-done((bf16[2048,320]{0,1:T(8,128)(2,1)}, bf16[2048,320]{0,1:T(8,128)(2,1)}, u32[]{:S(2)}, u32[]{:S(2)}) %collective-permute-start.1) | collective-permute-done | bytes 1310752 | tf_op jit(solution)/shard_map/ppermute | solution.py:114
  93.1 1.9 collective-permute-done.2
  95.0 3.4 %collective-permute-start.3 = (bf16[512,256]{1,0:T(8,128)(2,1)}, bf16[512,256]{1,0:T(8,128)(2,1)S(1)}, u32[]{:S(2)}, u32[]{:S(2)}) collective-permute-start(bf16[512,256]{1,0:T(8,128)(2,1)} %maximum_select_fusion), channel_id=1, source_target_pairs={{0,96},{32,0},{64,32},{96,64},{1,97},{33,1},{65,33},{97,65},{2,98}... | collective-permute-start | bytes 786440 | tf_op jit(solution)/shard_map/ppermute | solution.py:48
  98.4 4.5 %collective-permute-start.4 = (bf16[512,256]{1,0:T(8,128)(2,1)}, bf16[512,256]{1,0:T(8,128)(2,1)S(1)}, u32[]{:S(2)}, u32[]{:S(2)}) collective-permute-start(bf16[512,256]{1,0:T(8,128)(2,1)} %maximum_select_fusion), channel_id=1, source_target_pairs={{0,32},{32,64},{64,96},{96,0},{1,33},{33,65},{65,97},{97,1},{2,34}... | collective-permute-start | bytes 786440 | tf_op jit(solution)/shard_map/ppermute | solution.py:47
  102.9 1.1 slice.62
  104.1 3.4 %collective-permute-start.11 = (bf16[1024,320]{0,1:T(8,128)(2,1)S(1)}, bf16[1024,320]{0,1:T(8,128)(2,1)S(1)}, u32[]{:S(2)}, u32[]{:S(2)}) collective-permute-start(bf16[1024,320]{0,1:T(8,128)(2,1)S(1)} %slice.62), channel_id=1, source_target_pairs={{0,128},{128,256},{256,384},{384,0},{1,129},{129,257},{257,385},{3... | collective-permute-start | bytes 1966088 | tf_op jit(solution)/shard_map/ppermute | solution.py:120
  107.5 1.1 slice.63
  108.6 3.7 %collective-permute-start.12 = (bf16[1024,320]{0,1:T(8,128)(2,1)S(1)}, bf16[1024,320]{0,1:T(8,128)(2,1)S(1)}, u32[]{:S(2)}, u32[]{:S(2)}) collective-permute-start(bf16[1024,320]{0,1:T(8,128)(2,1)S(1)} %slice.63), channel_id=1, source_target_pairs={{0,384},{128,0},{256,128},{384,256},{1,385},{129,1},{257,129},{385... | collective-permute-start | bytes 1966088 | tf_op jit(solution)/shard_map/ppermute | solution.py:120
  112.3 2.2 fusion.11
  114.5 2.2 fusion.9
  116.8 1.0 bitcast_dynamic-update-slice_fusion.5
  117.9 4.3 %collective-permute-start.5 = (bf16[256,256]{1,0:T(8,128)(2,1)S(1)}, bf16[256,256]{1,0:T(8,128)(2,1)S(1)}, u32[]{:S(2)}, u32[]{:S(2)}) collective-permute-start(bf16[256,256]{1,0:T(8,128)(2,1)S(1)} %slice.89), channel_id=1, source_target_pairs={{0,32},{32,64},{64,96},{96,0},{1,33},{33,65},{65,97},{97,1},{2,34}... | collective-permute-start | bytes 393224 | tf_op jit(solution)/shard_map/ppermute | solution.py:51
  122.3 2.4 collective-permute-start.6
  124.7 2.1 collective-permute-done.5
  126.9 5.8 %collective-permute-done.6 = bf16[256,256]{1,0:T(8,128)(2,1)S(1)} collective-permute-done((bf16[256,256]{1,0:T(8,128)(2,1)S(1)}, bf16[256,256]{1,0:T(8,128)(2,1)S(1)}, u32[]{:S(2)}, u32[]{:S(2)}) %collective-permute-start.6) | collective-permute-done | bytes 131104 | tf_op jit(solution)/shard_map/ppermute | solution.py:51
  132.7 0.9 fusion.6
  133.6 3.1 %fusion.27 = bf16[8,32,320]{2,0,1:T(8,128)(2,1)} fusion(f32[320,32,8]{0,1,2:T(8,128)S(1)} %fusion.6, f32[320,32,8]{0,1,2:T(8,128)S(1)} %fusion.9, bf16[2048,320,1]{0,1,2:T(8,128)(2,1)S(1)} %reshape.323, bf16[256,8192]{1,0:T(8,128)(2,1)} %fusion.2, s32[]{:T(128)S(6)} %select_n.146, f32[320,32,8]{0,1,2:T(8,128)S(1)} %fusion.11), kind=kOutput, calls=%fused_computation.46 | convolution fusion | flops 335872000 | bytes 3506180 | tf_op jit(solution)/shard_map/jbd,dc->bjc/dot_general | solution.py:128
  136.7 8.5 %all-to-all-start.1 = ((bf16[8,32,320]{2,0,1:T(8,128)(2,1)}), bf16[8,32,320]{2,0,1:T(8,128)(2,1)S(1)}, u32[]{:S(2)}, u32[]{:S(2)}) async-start(bf16[8,32,320]{2,0,1:T(8,128)(2,1)} %fusion.27), calls=%async_computation.1 | async-start | bytes 393216 | tf_op jit(solution)/shard_map/all_to_all | solution.py:33
  145.3 1.0 bitcast_dynamic-update-slice_fusion.3
  146.2 3.6 %collective-permute-start.7 = (bf16[4,512,256]{2,1,0:T(8,128)(2,1)S(1)}, bf16[4,512,256]{2,1,0:T(8,128)(2,1)}, u32[]{:S(2)}, u32[]{:S(2)}) collective-permute-start(bf16[4,512,256]{2,1,0:T(8,128)(2,1)S(1)} %bitcast_dynamic-update-slice_fusion.3), channel_id=1, source_target_pairs={{0,384},{128,0},{256,128},{384,256},{1,385},{129,1},{257,129},{385... | collective-permute-start | bytes 3145736 | tf_op jit(solution)/shard_map/ppermute | solution.py:48
  149.8 2.3 collective-permute-start.8
  152.1 2.2 gather_fusion.1
  154.6 0.9 fusion.57
  157.9 0.7 broadcast_in_dim.106
  158.7 8.3 %all-to-all-start.3 = ((bf16[8,32,512]{2,0,1:T(8,128)(2,1)}), bf16[8,32,512]{2,0,1:T(8,128)(2,1)S(1)}, u32[]{:S(2)}, u32[]{:S(2)}) async-start(bf16[8,32,512]{2,0,1:T(8,128)(2,1)} %bitcast.43), calls=%async_computation.3 | async-start | bytes 524288 | tf_op jit(solution)/shard_map/all_to_all | solution.py:168
  167.0 6.5 %collective-permute-done.7 = bf16[4,512,256]{2,1,0:T(8,128)(2,1)} collective-permute-done((bf16[4,512,256]{2,1,0:T(8,128)(2,1)S(1)}, bf16[4,512,256]{2,1,0:T(8,128)(2,1)}, u32[]{:S(2)}, u32[]{:S(2)}) %collective-permute-start.7) | collective-permute-done | bytes 1048608 | tf_op jit(solution)/shard_map/ppermute | solution.py:48
  173.4 1.9 slice.92
  175.3 4.8 %collective-permute-start.10 = (bf16[2,512,256]{2,1,0:T(8,128)(2,1)}, bf16[2,512,256]{2,1,0:T(8,128)(2,1)S(1)}, u32[]{:S(2)}, u32[]{:S(2)}) collective-permute-start(bf16[2,512,256]{2,1,0:T(8,128)(2,1)} %slice.92), channel_id=1, source_target_pairs={{0,384},{128,0},{256,128},{384,256},{1,385},{129,1},{257,129},{385... | collective-permute-start | bytes 1572872 | tf_op jit(solution)/shard_map/ppermute | solution.py:51
  180.1 1.9 slice.91
  182.0 1.9 collective-permute-start.9
  183.9 2.4 broadcast_in_dim.51
  186.3 1.0 bitcast_dynamic-update-slice_fusion.2
  187.3 2.3 bitcast_dynamic-update-slice_fusion.1
  189.6 1.4 collective-permute-done.10
  191.1 7.1 %collective-permute-done.9 = bf16[2,512,256]{2,1,0:T(8,128)(2,1)S(1)} collective-permute-done((bf16[2,512,256]{2,1,0:T(8,128)(2,1)}, bf16[2,512,256]{2,1,0:T(8,128)(2,1)S(1)}, u32[]{:S(2)}, u32[]{:S(2)}) %collective-permute-start.9) | collective-permute-done | bytes 524320 | tf_op jit(solution)/shard_map/ppermute | solution.py:51
  198.2 1.0 fusion.17
  199.2 2.3 bitcast_dynamic-update-slice_fusion
  201.5 2.3 fusion.5
  203.8 2.5 fusion.3
  206.4 1.2 copy.68
  207.6 0.7 copy.69
  208.3 55.5 %all_to_all.25 = bf16[16,256,256]{2,1,0:T(8,128)(2,1)} all-to-all(bf16[16,256,256]{2,1,0:T(8,128)(2,1)S(1)} %copy.69), channel_id=1, replica_groups=mesh['x'=4,'yh'=4,'yl'=2,'z'=8,'c'=2] {'yl','z'}, dimensions={0} | all-to-all | bytes 4194304 | tf_op jit(solution)/shard_map/all_to_all | solution.py:182
  263.7 2.6 reduce_sum.55
  (81 shorter events, 5.0 us)
Async XLA Ops:
  0.0 14.4 %copy-start = (bf16[32,2,8,1024]{3,2,1,0:T(8,128)(2,1)S(1)}, bf16[32,2,8,1024]{3,2,1,0:T(8,128)(2,1)}, u32[]{:S(2)}) copy-start(bf16[32,2,8,1024]{3,2,1,0:T(8,128)(2,1)} %param.14) | copy-start | bytes 3145732
  0.0 9.4 %copy-start.5 = (bf16[256,512]{1,0:T(8,128)(2,1)S(1)}, bf16[256,512]{1,0:T(8,128)(2,1)}, u32[]{:S(2)}) copy-start(bf16[256,512]{1,0:T(8,128)(2,1)} %param.13) | copy-start | bytes 786436
  2.3 10.4 %copy-start.8 = (bf16[8192]{0:T(1024)(128)(2,1)S(1)}, bf16[8192]{0:T(1024)(128)(2,1)}, u32[]{:S(2)}) copy-start(bf16[8192]{0:T(1024)(128)(2,1)} %param.11) | copy-start | bytes 49156
  2.3 10.9 %copy-start.11 = (s32[1024,1]{0,1:T(1,128)S(1)}, s32[1024,1]{0,1:T(1,128)}, u32[]{:S(2)}) copy-start(s32[1024,1]{0,1:T(1,128)} %param.16) | copy-start | bytes 12292
  2.3 11.7 %copy-start.10 = (s32[1024]{0:T(1024)S(1)}, s32[1024]{0:T(1024)}, u32[]{:S(2)}) copy-start(s32[1024]{0:T(1024)} %param.17) | copy-start | bytes 12292
  2.3 35.0 %all-to-all-start = ((bf16[4,512,320]{1,2,0:T(8,128)(2,1)}), bf16[4,512,320]{1,2,0:T(8,128)(2,1)S(1)}, u32[]{:S(2)}, u32[]{:S(2)}) async-start(bf16[4,512,320]{1,2,0:T(8,128)(2,1)} %broadcast_in_dim.53), calls=%async_computation | async-start | bytes 2621440 | tf_op jit(solution)/shard_map/all_to_all | solution.py:38
  10.7 60.7 %collective-permute-start = (bf16[256,256]{1,0:T(8,128)(2,1)}, bf16[256,256]{1,0:T(8,128)(2,1)}, u32[]{:S(2)}, u32[]{:S(2)}) collective-permute-start(bf16[256,256]{1,0:T(8,128)(2,1)} %fusion.35), channel_id=1, source_target_pairs={{0,1},{1,0},{2,3},{3,2},{4,5},{5,4},{6,7},{7,6},{8,9},{9,8},{10,11... | collective-permute-start | bytes 393224 | tf_op jit(solution)/shard_map/ppermute | solution.py:103
  37.3 99.4 %all-to-all-start.2 = ((bf16[32,2,2,8,1024]{4,3,2,1,0:T(8,128)(2,1)}), bf16[32,2,2,8,1024]{4,3,2,1,0:T(8,128)(2,1)}, u32[]{:S(2)}, u32[]{:S(2)}) async-start(bf16[32,2,2,8,1024]{4,3,2,1,0:T(8,128)(2,1)} %bitcast.148), calls=%async_computation.2 | async-start | bytes 4194304 | tf_op jit(solution)/shard_map/all_to_all | solution.py:146
  51.2 5.5 %copy-start.12 = (s32[256]{0:T(256)S(1)}, s32[256]{0:T(256)}, u32[]{:S(2)}) copy-start(s32[256]{0:T(256)} %param.15) | copy-start | bytes 3076
  58.8 34.2 %collective-permute-start.1 = (bf16[2048,320]{0,1:T(8,128)(2,1)}, bf16[2048,320]{0,1:T(8,128)(2,1)}, u32[]{:S(2)}, u32[]{:S(2)}) collective-permute-start(bf16[2048,320]{0,1:T(8,128)(2,1)} %bitcast.56), channel_id=1, source_target_pairs={{0,128},{128,256},{256,384},{384,0},{1,129},{129,257},{257,385},{3... | collective-permute-start | bytes 3932168 | tf_op jit(solution)/shard_map/ppermute | solution.py:114
  62.2 32.8 %collective-permute-start.2 = (bf16[2048,320]{0,1:T(8,128)(2,1)}, bf16[2048,320]{0,1:T(8,128)(2,1)}, u32[]{:S(2)}, u32[]{:S(2)}) collective-permute-start(bf16[2048,320]{0,1:T(8,128)(2,1)} %bitcast.56), channel_id=1, source_target_pairs={{0,384},{128,0},{256,128},{384,256},{1,385},{129,1},{257,129},{385... | collective-permute-start | bytes 3932168 | tf_op jit(solution)/shard_map/ppermute | solution.py:115
  78.3 34.0 %copy-start.2 = (bf16[32,8,2048]{2,1,0:T(8,128)(2,1)S(1)}, bf16[32,8,2048]{2,1,0:T(8,128)(2,1)}, u32[]{:S(2)}) copy-start(bf16[32,8,2048]{2,1,0:T(8,128)(2,1)} %get-tuple-element.25) | copy-start | bytes 3145732
  95.0 27.3 %collective-permute-start.3 = (bf16[512,256]{1,0:T(8,128)(2,1)}, bf16[512,256]{1,0:T(8,128)(2,1)S(1)}, u32[]{:S(2)}, u32[]{:S(2)}) collective-permute-start(bf16[512,256]{1,0:T(8,128)(2,1)} %maximum_select_fusion), channel_id=1, source_target_pairs={{0,96},{32,0},{64,32},{96,64},{1,97},{33,1},{65,33},{97,65},{2,98}... | collective-permute-start | bytes 786440 | tf_op jit(solution)/shard_map/ppermute | solution.py:48
  98.4 19.5 %collective-permute-start.4 = (bf16[512,256]{1,0:T(8,128)(2,1)}, bf16[512,256]{1,0:T(8,128)(2,1)S(1)}, u32[]{:S(2)}, u32[]{:S(2)}) collective-permute-start(bf16[512,256]{1,0:T(8,128)(2,1)} %maximum_select_fusion), channel_id=1, source_target_pairs={{0,32},{32,64},{64,96},{96,0},{1,33},{33,65},{65,97},{97,1},{2,34}... | collective-permute-start | bytes 786440 | tf_op jit(solution)/shard_map/ppermute | solution.py:47
  104.1 28.6 %collective-permute-start.11 = (bf16[1024,320]{0,1:T(8,128)(2,1)S(1)}, bf16[1024,320]{0,1:T(8,128)(2,1)S(1)}, u32[]{:S(2)}, u32[]{:S(2)}) collective-permute-start(bf16[1024,320]{0,1:T(8,128)(2,1)S(1)} %slice.62), channel_id=1, source_target_pairs={{0,128},{128,256},{256,384},{384,0},{1,129},{129,257},{257,385},{3... | collective-permute-start | bytes 1966088 | tf_op jit(solution)/shard_map/ppermute | solution.py:120
  108.6 24.0 %collective-permute-start.12 = (bf16[1024,320]{0,1:T(8,128)(2,1)S(1)}, bf16[1024,320]{0,1:T(8,128)(2,1)S(1)}, u32[]{:S(2)}, u32[]{:S(2)}) collective-permute-start(bf16[1024,320]{0,1:T(8,128)(2,1)S(1)} %slice.63), channel_id=1, source_target_pairs={{0,384},{128,0},{256,128},{384,256},{1,385},{129,1},{257,129},{385... | collective-permute-start | bytes 1966088 | tf_op jit(solution)/shard_map/ppermute | solution.py:120
  116.7 16.0 %copy-start.1 = (bf16[32,8,2048]{2,1,0:T(8,128)(2,1)S(1)}, bf16[32,8,2048]{2,1,0:T(8,128)(2,1)}, u32[]{:S(2)}) copy-start(bf16[32,8,2048]{2,1,0:T(8,128)(2,1)} %get-tuple-element.26) | copy-start | bytes 3145732
  117.9 14.8 %copy-start.3 = (bf16[512,256]{1,0:T(8,128)(2,1)}, bf16[512,256]{1,0:T(8,128)(2,1)S(1)}, u32[]{:S(2)}) copy-start(bf16[512,256]{1,0:T(8,128)(2,1)S(1)} %collective-permute-done.4) | copy-start | bytes 786436
  117.9 9.0 %collective-permute-start.5 = (bf16[256,256]{1,0:T(8,128)(2,1)S(1)}, bf16[256,256]{1,0:T(8,128)(2,1)S(1)}, u32[]{:S(2)}, u32[]{:S(2)}) collective-permute-start(bf16[256,256]{1,0:T(8,128)(2,1)S(1)} %slice.89), channel_id=1, source_target_pairs={{0,32},{32,64},{64,96},{96,0},{1,33},{33,65},{65,97},{97,1},{2,34}... | collective-permute-start | bytes 393224 | tf_op jit(solution)/shard_map/ppermute | solution.py:51
  122.3 10.3 %collective-permute-start.6 = (bf16[256,256]{1,0:T(8,128)(2,1)S(1)}, bf16[256,256]{1,0:T(8,128)(2,1)S(1)}, u32[]{:S(2)}, u32[]{:S(2)}) collective-permute-start(bf16[256,256]{1,0:T(8,128)(2,1)S(1)} %slice.90), channel_id=1, source_target_pairs={{0,96},{32,0},{64,32},{96,64},{1,97},{33,1},{65,33},{97,65},{2,98}... | collective-permute-start | bytes 393224 | tf_op jit(solution)/shard_map/ppermute | solution.py:51
  136.7 18.8 %all-to-all-start.1 = ((bf16[8,32,320]{2,0,1:T(8,128)(2,1)}), bf16[8,32,320]{2,0,1:T(8,128)(2,1)S(1)}, u32[]{:S(2)}, u32[]{:S(2)}) async-start(bf16[8,32,320]{2,0,1:T(8,128)(2,1)} %fusion.27), calls=%async_computation.1 | async-start | bytes 393216 | tf_op jit(solution)/shard_map/all_to_all | solution.py:33
  146.2 27.2 %collective-permute-start.7 = (bf16[4,512,256]{2,1,0:T(8,128)(2,1)S(1)}, bf16[4,512,256]{2,1,0:T(8,128)(2,1)}, u32[]{:S(2)}, u32[]{:S(2)}) collective-permute-start(bf16[4,512,256]{2,1,0:T(8,128)(2,1)S(1)} %bitcast_dynamic-update-slice_fusion.3), channel_id=1, source_target_pairs={{0,384},{128,0},{256,128},{384,256},{1,385},{129,1},{257,129},{385... | collective-permute-start | bytes 3145736 | tf_op jit(solution)/shard_map/ppermute | solution.py:48
  149.8 30.3 %collective-permute-start.8 = (bf16[4,512,256]{2,1,0:T(8,128)(2,1)S(1)}, bf16[4,512,256]{2,1,0:T(8,128)(2,1)}, u32[]{:S(2)}, u32[]{:S(2)}) collective-permute-start(bf16[4,512,256]{2,1,0:T(8,128)(2,1)S(1)} %bitcast_dynamic-update-slice_fusion.3), channel_id=1, source_target_pairs={{0,128},{128,256},{256,384},{384,0},{1,129},{129,257},{257,385},{3... | collective-permute-start | bytes 3145736 | tf_op jit(solution)/shard_map/ppermute | solution.py:47
  154.6 1.4 copy-start.6
  154.6 1.4 copy-start.7
  155.5 0.8 copy-start.9
  155.8 1.6 copy-start.4
  158.7 30.9 %all-to-all-start.3 = ((bf16[8,32,512]{2,0,1:T(8,128)(2,1)}), bf16[8,32,512]{2,0,1:T(8,128)(2,1)S(1)}, u32[]{:S(2)}, u32[]{:S(2)}) async-start(bf16[8,32,512]{2,0,1:T(8,128)(2,1)} %bitcast.43), calls=%async_computation.3 | async-start | bytes 524288 | tf_op jit(solution)/shard_map/all_to_all | solution.py:168
  175.3 15.8 %collective-permute-start.10 = (bf16[2,512,256]{2,1,0:T(8,128)(2,1)}, bf16[2,512,256]{2,1,0:T(8,128)(2,1)S(1)}, u32[]{:S(2)}, u32[]{:S(2)}) collective-permute-start(bf16[2,512,256]{2,1,0:T(8,128)(2,1)} %slice.92), channel_id=1, source_target_pairs={{0,384},{128,0},{256,128},{384,256},{1,385},{129,1},{257,129},{385... | collective-permute-start | bytes 1572872 | tf_op jit(solution)/shard_map/ppermute | solution.py:51
  182.0 16.2 %collective-permute-start.9 = (bf16[2,512,256]{2,1,0:T(8,128)(2,1)}, bf16[2,512,256]{2,1,0:T(8,128)(2,1)S(1)}, u32[]{:S(2)}, u32[]{:S(2)}) collective-permute-start(bf16[2,512,256]{2,1,0:T(8,128)(2,1)} %slice.91), channel_id=1, source_target_pairs={{0,128},{128,256},{256,384},{384,0},{1,129},{129,257},{257,385},{3... | collective-permute-start | bytes 1572872 | tf_op jit(solution)/shard_map/ppermute | solution.py:51

commit v10 on v9

--- a/solution.py
+++ b/solution.py
@@ -106,6 +106,8 @@
     scale_rms = lax.rsqrt(jnp.mean(floats * floats, axis=-1, keepdims=True) + 1e-05)
     normed = (floats * scale_rms * norm_gain.astype(jnp.float32)).astype(jnp.bfloat16)
     stack = gather_rows(w_qkv, "yh", lax.axis_size("yh"))
+    w_local, stack = lax.optimization_barrier((w_local, stack))
+    w_blocks = place_ring(w_local, "x", place_ring(w_local, "yh", None))
     xs = lax.axis_size("x")
     assert xs == 4
     me = lax.axis_index("x")
@@ -113,8 +115,6 @@
     behind = [(i, (i - 1) % xs) for i in range(xs)]
     from_left = lax.ppermute(stack, "x", ahead)
     from_right = lax.ppermute(stack, "x", behind)
-    w_local, from_left, from_right = lax.optimization_barrier((w_local, from_left, from_right))
-    w_blocks = place_ring(w_local, "x", place_ring(w_local, "yh", None))
     cut = stack.shape[0] // 2
     far = jnp.concatenate(
         [lax.ppermute(from_left[:cut], "x", ahead), lax.ppermute(from_right[cut:], "x", behind)],

time: 269 us -> 250 us (0.929)
  local copies, waits for them, and re-layouts: 38.4 us -> 29 us
  waiting for transfers between devices: 57.3 us -> 49.3 us
  starting transfers between devices: 81.1 us -> 86.9 us
  other arithmetic: 19 us -> 14 us
    ppermute x1, waiting for transfers between devices: 14.7 us -> 0.01 us  [shards(): from_left = lax.ppermute(stack, 'x', ahead)]
    ppermute x2, waiting for transfers between devices: 9.23 us -> 0.01 us  [place_ring(): lax.ppermute(from_left[:cut], axis, ahead)]
    ppermute x2, waiting for transfers between devices: 7.21 us -> 0.01 us  [place_ring(): lax.ppermute(from_right[cut:], axis, behind)]
    ppermute x2, waiting for transfers between devices: 6.48 us -> 13.1 us  [place_ring(): from_right = lax.ppermute(source, axis, behind)]
    all_to_all x1, waiting for transfers between devices: 0.01 us -> 5.55 us  [shards(): lax.all_to_all(doubled.reshape(own_beams, columns, pair_feats.shape[3]),...]
    ppermute x1, waiting for transfers between devices: 0.01 us -> 4.36 us  [shards(): lax.ppermute(from_left[:cut], 'x', ahead)]
    ppermute x2, waiting for transfers between devices: 0.01 us -> 4.31 us  [place_ring(): from_left = lax.ppermute(source, axis, ahead)]
    all_to_all x1, starting transfers between devices: 8.5 us -> 12.4 us  [regroup(): return lax.all_to_all(blocks, BEAM, split_axis=1, concat_axis=1, tiled=True)]
  transfers between devices with their start and end apart: 17 -> 17, of which waited for: 8 -> 6; matrix products, arithmetic and copies ran while one was open for 21% -> 19% of each run, Pallas kernels for 0% -> 0%
where the time goes in v10:
time: 250 us; the launch traced here: 247 us
  starting transfers between devices  86.9 us (35%)
  blocking collectives  53.2 us (21%)
  waiting for transfers between devices  49.3 us (20%)
  local copies, waits for them, and re-layouts  29 us (12%)
  other arithmetic  14 us (6%)
  matrix products  13.6 us (5%)
    all_to_all x1, blocking collectives, shards(): spread = lax.all_to_all(partial.transpose(1, 0, 2), PAIR, 0, 0, tiled=True)  53.2 us
    all_to_all x1, waiting for transfers between devices, gather_rows(): lax.all_to_all(copies, axis, 0, 0, tiled=True)  19.1 us
    ppermute x2, waiting for transfers between devices, place_ring(): from_right = lax.ppermute(source, axis, behind)  13.1 us
    all_to_all x1, starting transfers between devices, regroup(): return lax.all_to_all(blocks, BEAM, split_axis=1, concat_axis=1, tiled=True)  12.4 us
    all_to_all x1, starting transfers between devices, shards(): lax.all_to_all(outgoing, BEAM, split_axis=0, concat_axis=0, tiled=True)  11.2 us
    all_to_all x1, starting transfers between devices, shards(): lax.all_to_all(doubled.reshape(own_beams, columns, pair_feats.shape[3]),...  10.5 us
    ppermute x2, starting transfers between devices, place_ring(): lax.ppermute(from_left[:cut], axis, ahead)  8.4 us
    dot_general x4, matrix products, shards(): jnp.einsum('jbd,dc->bjc', block.reshape(columns, own_beams, rows), piece,...  7.63 us
  transfers between devices with their start and end apart: 17, of which 6 were waited for; matrix products, arithmetic and copies ran while one was open for 19% of the time, Pallas kernels for 0%

profile of v10, /device:TPU:56, one launch (start us, length us, event | category | flops | bytes accessed | tf_op | source)
XLA Modules:
  0.0 246.7 jit_solution(15697179683547145635)
XLA Ops:
  0.0 1.1 reshape.232
  1.1 0.6 constant_dynamic-slice_fusion
  1.7 1.9 collective-permute-start
  3.7 1.2 broadcast_in_dim.53
  4.9 7.0 %all-to-all-start = ((bf16[4,512,320]{1,2,0:T(8,128)(2,1)}), bf16[4,512,320]{1,2,0:T(8,128)(2,1)S(1)}, u32[]{:S(2)}, u32[]{:S(2)}) async-start(bf16[4,512,320]{1,2,0:T(8,128)(2,1)} %broadcast_in_dim.53), calls=%async_computation | async-start | bytes 2621440 | tf_op jit(solution)/shard_map/all_to_all | solution.py:38
  11.9 3.1 %fusion = f32[256]{0:T(256)S(1)} fusion(bf16[256,8192]{1,0:T(8,128)(2,1)} %param.10), kind=kLoop, calls=%fused_computation.4 | loop fusion | flops 6291200 | bytes 4195328 | tf_op jit(solution)/shard_map/reduce_sum | solution.py:106
  15.0 0.5 broadcast.203
  15.5 0.7 reduce.4
  16.3 0.2 reduce_window_sum.22
  16.9 2.0 gather_fusion
  18.9 5.3 %fusion.2 = bf16[256,8192]{1,0:T(8,128)(2,1)} fusion(bf16[256,8192]{1,0:T(8,128)(2,1)} %param.10, f32[8192]{0:T(1024)S(1)} %convert_element_type.103, f32[256]{0:T(256)S(1)} %add_rsqrt_fusion), kind=kLoop, calls=%fused_computation.6 | loop fusion | flops 8388608 | bytes 8422400 | tf_op jit(solution)/shard_map/convert_element_type | solution.py:107
  24.2 19.1 %all-to-all-done = bf16[4,512,320]{1,2,0:T(8,128)(2,1)S(1)} async-done(((bf16[4,512,320]{1,2,0:T(8,128)(2,1)}), bf16[4,512,320]{1,2,0:T(8,128)(2,1)S(1)}, u32[]{:S(2)}, u32[]{:S(2)}) %all-to-all-start) | async-done | bytes 1310752 | tf_op jit(solution)/shard_map/all_to_all | solution.py:38
  43.4 11.2 %all-to-all-start.2 = ((bf16[32,2,2,8,1024]{4,3,2,1,0:T(8,128)(2,1)}), bf16[32,2,2,8,1024]{4,3,2,1,0:T(8,128)(2,1)}, u32[]{:S(2)}, u32[]{:S(2)}) async-start(bf16[32,2,2,8,1024]{4,3,2,1,0:T(8,128)(2,1)} %bitcast.27), calls=%async_computation.2 | async-start | bytes 4194304 | tf_op jit(solution)/shard_map/all_to_all | solution.py:146
  54.8 0.2 select_reduce_fusion
  55.3 1.2 copy.90
  56.6 3.4 %collective-permute-start.10 = (bf16[2048,320]{0,1:T(8,128)(2,1)}, bf16[2048,320]{0,1:T(8,128)(2,1)}, u32[]{:S(2)}, u32[]{:S(2)}) collective-permute-start(bf16[2048,320]{0,1:T(8,128)(2,1)} %bitcast.54), channel_id=1, source_target_pairs={{0,128},{128,256},{256,384},{384,0},{1,129},{129,257},{257,385},{3... | collective-permute-start | bytes 3932168 | tf_op jit(solution)/shard_map/ppermute | solution.py:116
  60.0 3.7 %collective-permute-start.9 = (bf16[2048,320]{0,1:T(8,128)(2,1)}, bf16[2048,320]{0,1:T(8,128)(2,1)}, u32[]{:S(2)}, u32[]{:S(2)}) collective-permute-start(bf16[2048,320]{0,1:T(8,128)(2,1)} %bitcast.54), channel_id=1, source_target_pairs={{0,384},{128,0},{256,128},{384,256},{1,385},{129,1},{257,129},{385... | collective-permute-start | bytes 3932168 | tf_op jit(solution)/shard_map/ppermute | solution.py:117
  63.9 2.8 %dynamic-slice_bitcast_fusion.2 = (bf16[32,8,2048]{2,1,0:T(8,128)(2,1)S(1)}, bf16[32,8,2048]{2,1,0:T(8,128)(2,1)S(1)}, bf16[32,8,2048]{2,1,0:T(8,128)(2,1)S(1)}, bf16[32,8,2048]{2,1,0:T(8,128)(2,1)S(1)}) fusion(bf16[256,8192]{1,0:T(8,128)(2,1)} %fusion.2, s32[]{:T(128)S(6)} %select_n.147, s32[]{:T(128)S(6)} %select_n.149, s32[]{:T(128)S(6)} %select_n.148, ...), kind=kLoop, calls=%fused_computation.43 | loop fusion | bytes 8388624 | tf_op jit(solution)/shard_map/reshape | solution.py:130
  66.6 3.4 %collective-permute-start.1 = (bf16[512,256]{1,0:T(8,128)(2,1)S(1)}, bf16[512,256]{1,0:T(8,128)(2,1)S(1)}, u32[]{:S(2)}, u32[]{:S(2)}) collective-permute-start(bf16[512,256]{1,0:T(8,128)(2,1)S(1)} %maximum_select_fusion), channel_id=1, source_target_pairs={{0,96},{32,0},{64,32},{96,64},{1,97},{33,1},{65,33},{97,65},{2,98}... | collective-permute-start | bytes 786440 | tf_op jit(solution)/shard_map/ppermute | solution.py:48
  70.0 4.6 %collective-permute-start.2 = (bf16[512,256]{1,0:T(8,128)(2,1)S(1)}, bf16[512,256]{1,0:T(8,128)(2,1)S(1)}, u32[]{:S(2)}, u32[]{:S(2)}) collective-permute-start(bf16[512,256]{1,0:T(8,128)(2,1)S(1)} %maximum_select_fusion), channel_id=1, source_target_pairs={{0,32},{32,64},{64,96},{96,0},{1,33},{33,65},{65,97},{97,1},{2,34}... | collective-permute-start | bytes 786440 | tf_op jit(solution)/shard_map/ppermute | solution.py:47
  74.6 2.2 fusion.13
  76.9 4.3 %collective-permute-done.2 = bf16[512,256]{1,0:T(8,128)(2,1)S(1)} collective-permute-done((bf16[512,256]{1,0:T(8,128)(2,1)S(1)}, bf16[512,256]{1,0:T(8,128)(2,1)S(1)}, u32[]{:S(2)}, u32[]{:S(2)}) %collective-permute-start.2) | collective-permute-done | bytes 262176 | tf_op jit(solution)/shard_map/ppermute | solution.py:47
  81.2 5.0 %collective-permute-start.3 = (bf16[256,256]{1,0:T(8,128)(2,1)S(1)}, bf16[256,256]{1,0:T(8,128)(2,1)S(1)}, u32[]{:S(2)}, u32[]{:S(2)}) collective-permute-start(bf16[256,256]{1,0:T(8,128)(2,1)S(1)} %slice.89), channel_id=1, source_target_pairs={{0,32},{32,64},{64,96},{96,0},{1,33},{33,65},{65,97},{97,1},{2,34}... | collective-permute-start | bytes 393224 | tf_op jit(solution)/shard_map/ppermute | solution.py:51
  86.2 13.1 %collective-permute-done.1 = bf16[512,256]{1,0:T(8,128)(2,1)S(1)} collective-permute-done((bf16[512,256]{1,0:T(8,128)(2,1)S(1)}, bf16[512,256]{1,0:T(8,128)(2,1)S(1)}, u32[]{:S(2)}, u32[]{:S(2)}) %collective-permute-start.1) | collective-permute-done | bytes 262176 | tf_op jit(solution)/shard_map/ppermute | solution.py:48
  99.3 3.6 %collective-permute-start.4 = (bf16[256,256]{1,0:T(8,128)(2,1)S(1)}, bf16[256,256]{1,0:T(8,128)(2,1)S(1)}, u32[]{:S(2)}, u32[]{:S(2)}) collective-permute-start(bf16[256,256]{1,0:T(8,128)(2,1)S(1)} %slice.90), channel_id=1, source_target_pairs={{0,96},{32,0},{64,32},{96,64},{1,97},{33,1},{65,33},{97,65},{2,98}... | collective-permute-start | bytes 393224 | tf_op jit(solution)/shard_map/ppermute | solution.py:51
  103.0 1.1 slice.94
  104.1 2.9 %collective-permute-start.11 = (bf16[1024,320]{0,1:T(8,128)(2,1)S(1)}, bf16[1024,320]{0,1:T(8,128)(2,1)S(1)}, u32[]{:S(2)}, u32[]{:S(2)}) collective-permute-start(bf16[1024,320]{0,1:T(8,128)(2,1)S(1)} %slice.94), channel_id=1, source_target_pairs={{0,128},{128,256},{256,384},{384,0},{1,129},{129,257},{257,385},{3... | collective-permute-start | bytes 1966088 | tf_op jit(solution)/shard_map/ppermute | solution.py:120
  107.0 1.1 slice.95
  108.1 4.2 %collective-permute-start.12 = (bf16[1024,320]{0,1:T(8,128)(2,1)S(1)}, bf16[1024,320]{0,1:T(8,128)(2,1)S(1)}, u32[]{:S(2)}, u32[]{:S(2)}) collective-permute-start(bf16[1024,320]{0,1:T(8,128)(2,1)S(1)} %slice.95), channel_id=1, source_target_pairs={{0,384},{128,0},{256,128},{384,256},{1,385},{129,1},{257,129},{385... | collective-permute-start | bytes 1966088 | tf_op jit(solution)/shard_map/ppermute | solution.py:120
  112.4 2.9 %collective-permute-start.5 = (bf16[4,512,256]{2,1,0:T(8,128)(2,1)S(1)}, bf16[4,512,256]{2,1,0:T(8,128)(2,1)}, u32[]{:S(2)}, u32[]{:S(2)}) collective-permute-start(bf16[4,512,256]{2,1,0:T(8,128)(2,1)S(1)} %bitcast_dynamic-update-slice_fusion.3), channel_id=1, source_target_pairs={{0,384},{128,0},{256,128},{384,256},{1,385},{129,1},{257,129},{385... | collective-permute-start | bytes 3145736 | tf_op jit(solution)/shard_map/ppermute | solution.py:48
  115.3 2.9 %collective-permute-start.6 = (bf16[4,512,256]{2,1,0:T(8,128)(2,1)S(1)}, bf16[4,512,256]{2,1,0:T(8,128)(2,1)S(1)}, u32[]{:S(2)}, u32[]{:S(2)}) collective-permute-start(bf16[4,512,256]{2,1,0:T(8,128)(2,1)S(1)} %bitcast_dynamic-update-slice_fusion.3), channel_id=1, source_target_pairs={{0,128},{128,256},{256,384},{384,0},{1,129},{129,257},{257,385},{3... | collective-permute-start | bytes 3145736 | tf_op jit(solution)/shard_map/ppermute | solution.py:47
  118.3 2.2 fusion.9
  120.5 4.4 %collective-permute-done.11 = bf16[1024,320]{0,1:T(8,128)(2,1)S(1)} collective-permute-done((bf16[1024,320]{0,1:T(8,128)(2,1)S(1)}, bf16[1024,320]{0,1:T(8,128)(2,1)S(1)}, u32[]{:S(2)}, u32[]{:S(2)}) %collective-permute-start.11) | collective-permute-done | bytes 655392 | tf_op jit(solution)/shard_map/ppermute | solution.py:120
  124.9 2.8 %collective-permute-done.12 = bf16[1024,320]{0,1:T(8,128)(2,1)S(1)} collective-permute-done((bf16[1024,320]{0,1:T(8,128)(2,1)S(1)}, bf16[1024,320]{0,1:T(8,128)(2,1)S(1)}, u32[]{:S(2)}, u32[]{:S(2)}) %collective-permute-start.12) | collective-permute-done | bytes 655392 | tf_op jit(solution)/shard_map/ppermute | solution.py:120
  127.7 0.9 fusion.6
  128.6 2.3 fusion.29
  130.9 0.8 copy.67
  131.6 12.4 %all-to-all-start.1 = ((bf16[8,32,320]{2,0,1:T(8,128)(2,1)}), bf16[8,32,320]{2,0,1:T(8,128)(2,1)S(1)}, u32[]{:S(2)}, u32[]{:S(2)}) async-start(bf16[8,32,320]{2,0,1:T(8,128)(2,1)} %copy.67), calls=%async_computation.1 | async-start | bytes 393216 | tf_op jit(solution)/shard_map/all_to_all | solution.py:33
  144.1 2.4 broadcast_in_dim.51
  146.4 1.0 bitcast_dynamic-update-slice_fusion.2
  147.5 0.8 slice.91
  148.3 3.4 %collective-permute-start.7 = (bf16[2,512,256]{2,1,0:T(8,128)(2,1)}, bf16[2,512,256]{2,1,0:T(8,128)(2,1)}, u32[]{:S(2)}, u32[]{:S(2)}) collective-permute-start(bf16[2,512,256]{2,1,0:T(8,128)(2,1)} %slice.91), channel_id=1, source_target_pairs={{0,128},{128,256},{256,384},{384,0},{1,129},{129,257},{257,385},{3... | collective-permute-start | bytes 1572872 | tf_op jit(solution)/shard_map/ppermute | solution.py:51
  151.7 1.9 slice.92
  153.6 3.9 %collective-permute-start.8 = (bf16[2,512,256]{2,1,0:T(8,128)(2,1)}, bf16[2,512,256]{2,1,0:T(8,128)(2,1)}, u32[]{:S(2)}, u32[]{:S(2)}) collective-permute-start(bf16[2,512,256]{2,1,0:T(8,128)(2,1)} %slice.92), channel_id=1, source_target_pairs={{0,384},{128,0},{256,128},{384,256},{1,385},{129,1},{257,129},{385... | collective-permute-start | bytes 1572872 | tf_op jit(solution)/shard_map/ppermute | solution.py:51
  157.5 2.2 gather_fusion.1
  159.8 0.3 copy.91
  160.0 0.9 fusion.67
  160.9 0.2 reshape.239
  161.6 0.3 fusion.52
  161.9 0.5 fusion.70
  162.4 0.3 fusion.42
  162.8 0.3 fusion.28
  163.3 0.7 broadcast_in_dim.106
  164.0 10.5 %all-to-all-start.3 = ((bf16[8,32,512]{2,0,1:T(8,128)(2,1)}), bf16[8,32,512]{2,0,1:T(8,128)(2,1)S(1)}, u32[]{:S(2)}, u32[]{:S(2)}) async-start(bf16[8,32,512]{2,0,1:T(8,128)(2,1)} %bitcast.41), calls=%async_computation.3 | async-start | bytes 524288 | tf_op jit(solution)/shard_map/all_to_all | solution.py:168
  174.5 2.3 bitcast_dynamic-update-slice_fusion.1
  176.8 2.2 fusion.32
  179.1 1.1 bitcast_dynamic-update-slice_fusion
  180.2 5.5 %all-to-all-done.3 = bf16[8,32,512]{2,0,1:T(8,128)(2,1)S(1)} async-done(((bf16[8,32,512]{2,0,1:T(8,128)(2,1)}), bf16[8,32,512]{2,0,1:T(8,128)(2,1)S(1)}, u32[]{:S(2)}, u32[]{:S(2)}) %all-to-all-start.3) | async-done | bytes 262176 | tf_op jit(solution)/shard_map/all_to_all | solution.py:168
  185.7 2.3 fusion.5
  188.0 2.5 %fusion.3 = bf16[32,8,16,256]{3,0,1,2:T(8,128)(2,1)S(1)} fusion(bf16[16,256,8,32]{1,3,2,0:T(8,128)(2,1)S(1)} %fusion.5, bf16[16,512,256]{2,1,0:T(8,128)(2,1)} %bitcast.10, bf16[8,32,256]{2,0,1:T(8,128)(2,1)S(1)} %get-tuple-element.31), kind=kOutput, calls=%fused_computation.8 | convolution fusion | flops 542113792 | bytes 6422528 | tf_op jit(solution)/shard_map/bjh,phc->jbpc/dot_general | solution.py:174
  190.6 1.2 copy.78
  191.8 0.7 copy.79
  192.5 53.2 %all_to_all.25 = bf16[16,256,256]{2,1,0:T(8,128)(2,1)S(1)} all-to-all(bf16[16,256,256]{2,1,0:T(8,128)(2,1)S(1)} %copy.79), channel_id=1, replica_groups=mesh['x'=4,'yh'=4,'yl'=2,'z'=8,'c'=2] {'yl','z'}, dimensions={0} | all-to-all | bytes 4194304 | tf_op jit(solution)/shard_map/all_to_all | solution.py:182
  245.7 1.0 reduce_sum.55
  (68 shorter events, 2.0 us)
Async XLA Ops:
  0.0 16.9 %copy-start = (bf16[32,2,8,1024]{3,2,1,0:T(8,128)(2,1)S(1)}, bf16[32,2,8,1024]{3,2,1,0:T(8,128)(2,1)}, u32[]{:S(2)}) copy-start(bf16[32,2,8,1024]{3,2,1,0:T(8,128)(2,1)} %param.14) | copy-start | bytes 3145732
  0.0 3.7 %copy-start.2 = (bf16[512,320]{0,1:T(8,128)(2,1)S(1)}, bf16[512,320]{0,1:T(8,128)(2,1)}, u32[]{:S(2)}) copy-start(bf16[512,320]{0,1:T(8,128)(2,1)} %param.12) | copy-start | bytes 983044
  1.7 10.1 %copy-start.3 = (bf16[8192]{0:T(1024)(128)(2,1)S(1)}, bf16[8192]{0:T(1024)(128)(2,1)}, u32[]{:S(2)}) copy-start(bf16[8192]{0:T(1024)(128)(2,1)} %param.11) | copy-start | bytes 49156
  1.7 53.5 %collective-permute-start = (bf16[256,256]{1,0:T(8,128)(2,1)S(1)}, bf16[256,256]{1,0:T(8,128)(2,1)S(1)}, u32[]{:S(2)}, u32[]{:S(2)}) collective-permute-start(bf16[256,256]{1,0:T(8,128)(2,1)S(1)} %fusion.46), channel_id=1, source_target_pairs={{0,1},{1,0},{2,3},{3,2},{4,5},{5,4},{6,7},{7,6},{8,9},{9,8},{10,11... | collective-permute-start | bytes 393224 | tf_op jit(solution)/shard_map/ppermute | solution.py:103
  4.9 38.5 %all-to-all-start = ((bf16[4,512,320]{1,2,0:T(8,128)(2,1)}), bf16[4,512,320]{1,2,0:T(8,128)(2,1)S(1)}, u32[]{:S(2)}, u32[]{:S(2)}) async-start(bf16[4,512,320]{1,2,0:T(8,128)(2,1)} %broadcast_in_dim.53), calls=%async_computation | async-start | bytes 2621440 | tf_op jit(solution)/shard_map/all_to_all | solution.py:38
  11.9 3.7 %copy-start.5 = (s32[1024,1]{0,1:T(1,128)S(1)}, s32[1024,1]{0,1:T(1,128)}, u32[]{:S(2)}) copy-start(s32[1024,1]{0,1:T(1,128)} %param.16) | copy-start | bytes 12292
  11.9 4.6 %copy-start.4 = (s32[1024]{0:T(1024)S(1)}, s32[1024]{0:T(1024)}, u32[]{:S(2)}) copy-start(s32[1024]{0:T(1024)} %param.17) | copy-start | bytes 12292
  43.4 11.4 %copy-start.6 = (s32[256]{0:T(256)S(1)}, s32[256]{0:T(256)}, u32[]{:S(2)}) copy-start(s32[256]{0:T(256)} %param.15) | copy-start | bytes 3076
  43.4 88.3 %all-to-all-start.2 = ((bf16[32,2,2,8,1024]{4,3,2,1,0:T(8,128)(2,1)}), bf16[32,2,2,8,1024]{4,3,2,1,0:T(8,128)(2,1)}, u32[]{:S(2)}, u32[]{:S(2)}) async-start(bf16[32,2,2,8,1024]{4,3,2,1,0:T(8,128)(2,1)} %bitcast.27), calls=%async_computation.2 | async-start | bytes 4194304 | tf_op jit(solution)/shard_map/all_to_all | solution.py:146
  56.6 46.4 %collective-permute-start.10 = (bf16[2048,320]{0,1:T(8,128)(2,1)}, bf16[2048,320]{0,1:T(8,128)(2,1)}, u32[]{:S(2)}, u32[]{:S(2)}) collective-permute-start(bf16[2048,320]{0,1:T(8,128)(2,1)} %bitcast.54), channel_id=1, source_target_pairs={{0,128},{128,256},{256,384},{384,0},{1,129},{129,257},{257,385},{3... | collective-permute-start | bytes 3932168 | tf_op jit(solution)/shard_map/ppermute | solution.py:116
  60.0 47.0 %collective-permute-start.9 = (bf16[2048,320]{0,1:T(8,128)(2,1)}, bf16[2048,320]{0,1:T(8,128)(2,1)}, u32[]{:S(2)}, u32[]{:S(2)}) collective-permute-start(bf16[2048,320]{0,1:T(8,128)(2,1)} %bitcast.54), channel_id=1, source_target_pairs={{0,384},{128,0},{256,128},{384,256},{1,385},{129,1},{257,129},{385... | collective-permute-start | bytes 3932168 | tf_op jit(solution)/shard_map/ppermute | solution.py:117
  66.6 32.7 %collective-permute-start.1 = (bf16[512,256]{1,0:T(8,128)(2,1)S(1)}, bf16[512,256]{1,0:T(8,128)(2,1)S(1)}, u32[]{:S(2)}, u32[]{:S(2)}) collective-permute-start(bf16[512,256]{1,0:T(8,128)(2,1)S(1)} %maximum_select_fusion), channel_id=1, source_target_pairs={{0,96},{32,0},{64,32},{96,64},{1,97},{33,1},{65,33},{97,65},{2,98}... | collective-permute-start | bytes 786440 | tf_op jit(solution)/shard_map/ppermute | solution.py:48
  70.0 11.2 %collective-permute-start.2 = (bf16[512,256]{1,0:T(8,128)(2,1)S(1)}, bf16[512,256]{1,0:T(8,128)(2,1)S(1)}, u32[]{:S(2)}, u32[]{:S(2)}) collective-permute-start(bf16[512,256]{1,0:T(8,128)(2,1)S(1)} %maximum_select_fusion), channel_id=1, source_target_pairs={{0,32},{32,64},{64,96},{96,0},{1,33},{33,65},{65,97},{97,1},{2,34}... | collective-permute-start | bytes 786440 | tf_op jit(solution)/shard_map/ppermute | solution.py:47
  81.2 31.1 %collective-permute-start.3 = (bf16[256,256]{1,0:T(8,128)(2,1)S(1)}, bf16[256,256]{1,0:T(8,128)(2,1)S(1)}, u32[]{:S(2)}, u32[]{:S(2)}) collective-permute-start(bf16[256,256]{1,0:T(8,128)(2,1)S(1)} %slice.89), channel_id=1, source_target_pairs={{0,32},{32,64},{64,96},{96,0},{1,33},{33,65},{65,97},{97,1},{2,34}... | collective-permute-start | bytes 393224 | tf_op jit(solution)/shard_map/ppermute | solution.py:51
  99.3 13.0 %collective-permute-start.4 = (bf16[256,256]{1,0:T(8,128)(2,1)S(1)}, bf16[256,256]{1,0:T(8,128)(2,1)S(1)}, u32[]{:S(2)}, u32[]{:S(2)}) collective-permute-start(bf16[256,256]{1,0:T(8,128)(2,1)S(1)} %slice.90), channel_id=1, source_target_pairs={{0,96},{32,0},{64,32},{96,64},{1,97},{33,1},{65,33},{97,65},{2,98}... | collective-permute-start | bytes 393224 | tf_op jit(solution)/shard_map/ppermute | solution.py:51
  104.1 20.8 %collective-permute-start.11 = (bf16[1024,320]{0,1:T(8,128)(2,1)S(1)}, bf16[1024,320]{0,1:T(8,128)(2,1)S(1)}, u32[]{:S(2)}, u32[]{:S(2)}) collective-permute-start(bf16[1024,320]{0,1:T(8,128)(2,1)S(1)} %slice.94), channel_id=1, source_target_pairs={{0,128},{128,256},{256,384},{384,0},{1,129},{129,257},{257,385},{3... | collective-permute-start | bytes 1966088 | tf_op jit(solution)/shard_map/ppermute | solution.py:120
  108.1 19.6 %collective-permute-start.12 = (bf16[1024,320]{0,1:T(8,128)(2,1)S(1)}, bf16[1024,320]{0,1:T(8,128)(2,1)S(1)}, u32[]{:S(2)}, u32[]{:S(2)}) collective-permute-start(bf16[1024,320]{0,1:T(8,128)(2,1)S(1)} %slice.95), channel_id=1, source_target_pairs={{0,384},{128,0},{256,128},{384,256},{1,385},{129,1},{257,129},{385... | collective-permute-start | bytes 1966088 | tf_op jit(solution)/shard_map/ppermute | solution.py:120
  112.4 39.3 %collective-permute-start.5 = (bf16[4,512,256]{2,1,0:T(8,128)(2,1)S(1)}, bf16[4,512,256]{2,1,0:T(8,128)(2,1)}, u32[]{:S(2)}, u32[]{:S(2)}) collective-permute-start(bf16[4,512,256]{2,1,0:T(8,128)(2,1)S(1)} %bitcast_dynamic-update-slice_fusion.3), channel_id=1, source_target_pairs={{0,384},{128,0},{256,128},{384,256},{1,385},{129,1},{257,129},{385... | collective-permute-start | bytes 3145736 | tf_op jit(solution)/shard_map/ppermute | solution.py:48
  115.3 32.1 %collective-permute-start.6 = (bf16[4,512,256]{2,1,0:T(8,128)(2,1)S(1)}, bf16[4,512,256]{2,1,0:T(8,128)(2,1)S(1)}, u32[]{:S(2)}, u32[]{:S(2)}) collective-permute-start(bf16[4,512,256]{2,1,0:T(8,128)(2,1)S(1)} %bitcast_dynamic-update-slice_fusion.3), channel_id=1, source_target_pairs={{0,128},{128,256},{256,384},{384,0},{1,129},{129,257},{257,385},{3... | collective-permute-start | bytes 3145736 | tf_op jit(solution)/shard_map/ppermute | solution.py:47
  131.6 29.3 %all-to-all-start.1 = ((bf16[8,32,320]{2,0,1:T(8,128)(2,1)}), bf16[8,32,320]{2,0,1:T(8,128)(2,1)S(1)}, u32[]{:S(2)}, u32[]{:S(2)}) async-start(bf16[8,32,320]{2,0,1:T(8,128)(2,1)} %copy.67), calls=%async_computation.1 | async-start | bytes 393216 | tf_op jit(solution)/shard_map/all_to_all | solution.py:33
  148.3 28.6 %collective-permute-start.7 = (bf16[2,512,256]{2,1,0:T(8,128)(2,1)}, bf16[2,512,256]{2,1,0:T(8,128)(2,1)}, u32[]{:S(2)}, u32[]{:S(2)}) collective-permute-start(bf16[2,512,256]{2,1,0:T(8,128)(2,1)} %slice.91), channel_id=1, source_target_pairs={{0,128},{128,256},{256,384},{384,0},{1,129},{129,257},{257,385},{3... | collective-permute-start | bytes 1572872 | tf_op jit(solution)/shard_map/ppermute | solution.py:51
  153.6 23.2 %collective-permute-start.8 = (bf16[2,512,256]{2,1,0:T(8,128)(2,1)}, bf16[2,512,256]{2,1,0:T(8,128)(2,1)}, u32[]{:S(2)}, u32[]{:S(2)}) collective-permute-start(bf16[2,512,256]{2,1,0:T(8,128)(2,1)} %slice.92), channel_id=1, source_target_pairs={{0,384},{128,0},{256,128},{384,256},{1,385},{129,1},{257,129},{385... | collective-permute-start | bytes 1572872 | tf_op jit(solution)/shard_map/ppermute | solution.py:51
  161.2 1.6 copy-start.1
  164.0 21.7 %all-to-all-start.3 = ((bf16[8,32,512]{2,0,1:T(8,128)(2,1)}), bf16[8,32,512]{2,0,1:T(8,128)(2,1)S(1)}, u32[]{:S(2)}, u32[]{:S(2)}) async-start(bf16[8,32,512]{2,0,1:T(8,128)(2,1)} %bitcast.41), calls=%async_computation.3 | async-start | bytes 524288 | tf_op jit(solution)/shard_map/all_to_all | solution.py:168

commit v11 on v6

--- a/solution.py
+++ b/solution.py
@@ -141,17 +141,16 @@
     fresh_key = rotary_embed(key_cols, positions).astype(jnp.bfloat16)
     attn = attend(queries, fresh_key, value_new, keys, values, positions)
     pairs = columns // cores
-    pair_feats = attn.reshape(own_beams, pairs, 1, cores * attn.shape[1] // columns)
-    doubled = jnp.broadcast_to(pair_feats, (own_beams, pairs, cores, pair_feats.shape[3]))
-    head_rows = lax.all_to_all(
-        doubled.reshape(own_beams, columns, pair_feats.shape[3]), BEAM, 1, 1, tiled=True
-    )
     block = attn.shape[1] // columns
+    own_rows = regroup(attn.reshape(own_beams, columns, block))
+    sib_rows = lax.ppermute(own_rows, "c", [(0, 1), (1, 0)])
+    first = jnp.where(core == 0, own_rows, sib_rows)
+    second = jnp.where(core == 0, sib_rows, own_rows)
     partial = None
     for half in range(cores):
         term = jnp.einsum(
             "bjh,hpc->jbpc",
-            head_rows[:, :, half * block : (half + 1) * block],
+            (first, second)[half],
             w_pair[half * block : (half + 1) * block],
             preferred_element_type=jnp.float32,
         ).astype(jnp.bfloat16).astype(jnp.float32)

time: 248 us -> 250 us (level)
    all_to_all x1, blocking collectives: 20.7 us -> 14.9 us  [regroup(): return lax.all_to_all(blocks, BEAM, split_axis=1, concat_axis=1, tiled=True)]
    all_to_all x1, blocking collectives: 56.4 us -> 61 us  [shards(): spread = lax.all_to_all(partial.transpose(1, 0, 2), PAIR, 0, 0, tiled=True)]
  transfers between devices with their start and end apart: 9 -> 10, of which waited for: 5 -> 6; matrix products, arithmetic and copies ran while one was open for 16% -> 16% of each run, Pallas kernels for 0% -> 0%
where the time goes in v11:
time: 250 us; the launch traced here: 248 us
  blocking collectives  75.9 us (30%)
  starting transfers between devices  54.2 us (22%)
  waiting for transfers between devices  53.4 us (21%)
  local copies, waits for them, and re-layouts  25.6 us (10%)
  between operations  13.9 us (6%)
  matrix products  12.8 us (5%)
  other arithmetic  12.4 us (5%)
    all_to_all x1, blocking collectives, shards(): spread = lax.all_to_all(partial.transpose(1, 0, 2), PAIR, 0, 0, tiled=True)  61 us
    all_to_all x1, waiting for transfers between devices, gather_rows(): lax.all_to_all(copies, axis, 0, 0, tiled=True)  23.9 us
    all_to_all x1, waiting for transfers between devices, regroup(): return lax.all_to_all(blocks, BEAM, split_axis=1, concat_axis=1, tiled=True)  15.5 us
    all_to_all x1, starting transfers between devices, regroup(): return lax.all_to_all(blocks, BEAM, split_axis=1, concat_axis=1, tiled=True)  14.9 us
    all_to_all x1, blocking collectives, regroup(): return lax.all_to_all(blocks, BEAM, split_axis=1, concat_axis=1, tiled=True)  14.9 us
    all_to_all x1, starting transfers between devices, shards(): lax.all_to_all(outgoing, BEAM, split_axis=0, concat_axis=0, tiled=True)  13.9 us
    dot_general x4, matrix products, shards(): jnp.einsum('jbd,dc->bjc', block.reshape(columns, own_beams, rows), piece,...  10.1 us
    all_to_all x1, waiting for transfers between devices, shards(): lax.all_to_all(outgoing, BEAM, split_axis=0, concat_axis=0, tiled=True)  7.22 us
  transfers between devices with their start and end apart: 10, of which 6 were waited for; matrix products, arithmetic and copies ran while one was open for 16% of the time, Pallas kernels for 0%

profile of v11, /device:TPU:56, one launch (start us, length us, event | category | flops | bytes accessed | tf_op | source)
XLA Modules:
  0.0 248.2 jit_solution(17463476157364112956)
XLA Ops:
  6.5 2.3 broadcast_in_dim.27
  8.8 7.1 %all-to-all-start = ((bf16[4,512,320]{1,2,0:T(8,128)(2,1)}), bf16[4,512,320]{1,2,0:T(8,128)(2,1)S(1)}, u32[]{:S(2)}, u32[]{:S(2)}) async-start(bf16[4,512,320]{1,2,0:T(8,128)(2,1)} %broadcast_in_dim.27), calls=%async_computation | async-start | bytes 2621440 | tf_op jit(solution)/shard_map/all_to_all | solution.py:38
  15.9 0.1 copy.71
  16.1 1.9 collective-permute-start
  18.0 0.5 broadcast.199
  18.6 0.7 reduce.4
  19.3 0.2 reduce_window_sum.22
  19.6 0.1 multiply_reduce_fusion
  19.7 0.1 copy.84
  19.8 0.1 reshape.230
  19.9 23.9 %all-to-all-done = bf16[4,512,320]{1,2,0:T(8,128)(2,1)S(1)} async-done(((bf16[4,512,320]{1,2,0:T(8,128)(2,1)}), bf16[4,512,320]{1,2,0:T(8,128)(2,1)S(1)}, u32[]{:S(2)}, u32[]{:S(2)}) %all-to-all-start) | async-done | bytes 1310752 | tf_op jit(solution)/shard_map/all_to_all | solution.py:38
  43.8 1.3 copy.106
  45.1 3.4 %collective-permute-start.1 = (bf16[2048,320]{0,1:T(8,128)(2,1)}, bf16[2048,320]{0,1:T(8,128)(2,1)}, u32[]{:S(2)}, u32[]{:S(2)}) collective-permute-start(bf16[2048,320]{0,1:T(8,128)(2,1)} %bitcast.51), channel_id=1, source_target_pairs={{0,128},{128,256},{256,384},{384,0},{1,129},{129,257},{257,385},{3... | collective-permute-start | bytes 3932168 | tf_op jit(solution)/shard_map/ppermute | solution.py:92
  48.5 3.7 %collective-permute-start.2 = (bf16[2048,320]{0,1:T(8,128)(2,1)}, bf16[2048,320]{0,1:T(8,128)(2,1)}, u32[]{:S(2)}, u32[]{:S(2)}) collective-permute-start(bf16[2048,320]{0,1:T(8,128)(2,1)} %bitcast.51), channel_id=1, source_target_pairs={{0,384},{128,0},{256,128},{384,256},{1,385},{129,1},{257,129},{385... | collective-permute-start | bytes 3932168 | tf_op jit(solution)/shard_map/ppermute | solution.py:93
  52.2 2.0 gather_fusion
  54.2 13.9 %all-to-all-start.2 = ((bf16[32,2,2,8,1024]{4,3,2,1,0:T(8,128)(2,1)}), bf16[32,2,2,8,1024]{4,3,2,1,0:T(8,128)(2,1)}, u32[]{:S(2)}, u32[]{:S(2)}) async-start(bf16[32,2,2,8,1024]{4,3,2,1,0:T(8,128)(2,1)} %bitcast.127), calls=%async_computation.2 | async-start | bytes 4194304 | tf_op jit(solution)/shard_map/all_to_all | solution.py:124
  68.2 0.1 fusion.45
  68.3 3.1 %fusion = f32[256]{0:T(256)S(1)} fusion(bf16[256,8192]{1,0:T(8,128)(2,1)} %param.10), kind=kLoop, calls=%fused_computation.4 | loop fusion | flops 6291200 | bytes 4195328 | tf_op jit(solution)/shard_map/reduce_sum | solution.py:84
  71.4 0.1 fusion.55
  71.5 0.8 maximum_select_fusion
  72.4 0.1 iota_compare_fusion.2
  72.6 0.2 select_reduce_fusion
  72.8 0.1 multiply_cosine_fusion
  72.9 3.6 %fusion.2 = bf16[256,8192]{1,0:T(8,128)(2,1)S(1)} fusion(bf16[256,8192]{1,0:T(8,128)(2,1)} %param.10, f32[8192]{0:T(1024)S(1)} %convert_element_type.97, f32[256]{0:T(256)S(1)} %add_rsqrt_fusion), kind=kLoop, calls=%fused_computation.6 | loop fusion | flops 8388608 | bytes 8422400 | tf_op jit(solution)/shard_map/convert_element_type | solution.py:85
  76.5 1.9 dynamic-slice_bitcast_fusion.2
  78.4 0.7 copy-done.1
  79.1 2.0 slice.40
  81.1 3.2 %collective-permute-start.3 = (bf16[1024,320]{0,1:T(8,128)(2,1)}, bf16[1024,320]{0,1:T(8,128)(2,1)}, u32[]{:S(2)}, u32[]{:S(2)}) collective-permute-start(bf16[1024,320]{0,1:T(8,128)(2,1)} %slice.40), channel_id=1, source_target_pairs={{0,128},{128,256},{256,384},{384,0},{1,129},{129,257},{257,385},{3... | collective-permute-start | bytes 1966088 | tf_op jit(solution)/shard_map/ppermute | solution.py:98
  84.3 2.0 slice.41
  86.3 3.8 %collective-permute-start.4 = (bf16[1024,320]{0,1:T(8,128)(2,1)}, bf16[1024,320]{0,1:T(8,128)(2,1)}, u32[]{:S(2)}, u32[]{:S(2)}) collective-permute-start(bf16[1024,320]{0,1:T(8,128)(2,1)} %slice.41), channel_id=1, source_target_pairs={{0,384},{128,0},{256,128},{384,256},{1,385},{129,1},{257,129},{385... | collective-permute-start | bytes 1966088 | tf_op jit(solution)/shard_map/ppermute | solution.py:98
  90.1 2.1 copy.74
  92.2 3.0 %reshape.314 = bf16[2048,320,1]{0,1,2:T(8,128)(2,1)S(1)} reshape(bf16[4,512,320]{1,0,2:T(4,128)(2,1)} %copy.74) | data formatting | bytes 2621440 | tf_op jit(solution)/shard_map/reshape | solution.py:38
  95.3 2.6 %fusion.7 = f32[320,32,8]{0,1,2:T(8,128)S(1)} fusion(bf16[2048,320]{0,1:T(8,128)(2,1)} %collective-permute-done.1, bf16[32,8,2048]{2,1,0:T(8,128)(2,1)} %get-tuple-element.29), kind=kOutput, calls=%fused_computation.13 | convolution fusion | flops 335544320 | bytes 2686976 | tf_op jit(solution)/shard_map/jbd,dc->bjc/dot_general | solution.py:106
  97.9 2.2 fusion.9
  100.1 1.2 collective-permute-done.3
  101.3 4.5 %collective-permute-done.4 = bf16[1024,320]{0,1:T(8,128)(2,1)} collective-permute-done((bf16[1024,320]{0,1:T(8,128)(2,1)}, bf16[1024,320]{0,1:T(8,128)(2,1)}, u32[]{:S(2)}, u32[]{:S(2)}) %collective-permute-start.4) | collective-permute-done | bytes 655392 | tf_op jit(solution)/shard_map/ppermute | solution.py:98
  105.8 2.2 fusion.4
  108.0 3.1 %fusion.24 = bf16[8,32,320]{2,0,1:T(8,128)(2,1)} fusion(f32[320,32,8]{0,1,2:T(8,128)S(1)} %fusion.4, f32[320,32,8]{0,1,2:T(8,128)S(1)} %fusion.7, bf16[2048,320,1]{0,1,2:T(8,128)(2,1)S(1)} %reshape.314, bf16[256,8192]{1,0:T(8,128)(2,1)} %copy-done.1, s32[]{:T(128)S(6)} %select_n.96, f32[320,32,8]{0,1,2:T(8,128)S(1)} %fusion.9), kind=kOutput, calls=%fused_computation.37 | convolution fusion | flops 335872000 | bytes 3506180 | tf_op jit(solution)/shard_map/jbd,dc->bjc/dot_general | solution.py:106
  111.1 7.2 %all-to-all-done.2 = bf16[32,2,2,8,1024]{4,3,2,1,0:T(8,128)(2,1)} async-done(((bf16[32,2,2,8,1024]{4,3,2,1,0:T(8,128)(2,1)}), bf16[32,2,2,8,1024]{4,3,2,1,0:T(8,128)(2,1)}, u32[]{:S(2)}, u32[]{:S(2)}) %all-to-all-start.2) | async-done | bytes 2097184 | tf_op jit(solution)/shard_map/all_to_all | solution.py:124
  118.4 14.9 %all-to-all-start.1 = ((bf16[8,32,320]{2,0,1:T(8,128)(2,1)}), bf16[8,32,320]{2,0,1:T(8,128)(2,1)S(1)}, u32[]{:S(2)}, u32[]{:S(2)}) async-start(bf16[8,32,320]{2,0,1:T(8,128)(2,1)} %fusion.24), calls=%async_computation.1 | async-start | bytes 393216 | tf_op jit(solution)/shard_map/all_to_all | solution.py:33
  133.3 2.2 gather_fusion.1
  135.5 0.3 copy.107
  135.8 0.1 fusion.57
  135.9 15.5 %all-to-all-done.1 = bf16[8,32,320]{2,0,1:T(8,128)(2,1)S(1)} async-done(((bf16[8,32,320]{2,0,1:T(8,128)(2,1)}), bf16[8,32,320]{2,0,1:T(8,128)(2,1)S(1)}, u32[]{:S(2)}, u32[]{:S(2)}) %all-to-all-start.1) | async-done | bytes 163872 | tf_op jit(solution)/shard_map/all_to_all | solution.py:33
  151.4 0.2 reshape.228
  151.6 0.1 subtract_convert_fusion.1
  151.7 0.1 maximum_bitcast_fusion.2
  151.8 0.1 fusion.58
  151.9 0.1 fusion.28
  152.1 0.3 fusion.40
  152.3 0.5 fusion.59
  152.9 0.3 fusion.27
  153.2 0.3 fusion.14
  153.6 0.1 copy.88
  153.7 14.9 %all_to_all.25 = bf16[8,32,256]{2,0,1:T(8,128)(2,1)S(1)} all-to-all(bf16[8,32,256]{2,0,1:T(8,128)(2,1)S(1)} %copy.88), channel_id=1, replica_groups=mesh['x'=4,'yh'=4,'yl'=2,'z'=8,'c'=2] {'yl','z','c'}, dimensions={1} | all-to-all | bytes 262144 | tf_op jit(solution)/shard_map/all_to_all | solution.py:33
  168.5 2.2 collective-permute-start.5
  170.7 1.0 collective-permute-done.5
  171.8 2.5 %fusion.56 = (bf16[256,4096]{0,1:T(8,128)(2,1)S(1)}, bf16[256,4096]{0,1:T(8,128)(2,1)S(1)}) fusion(bf16[512,4096]{0,1:T(8,128)(2,1)} %all-gather.3.cloned.1.call-done), kind=kLoop, calls=%fused_computation.103 | loop fusion | bytes 8388608 | tf_op jit(solution)/shard_map/slice | solution.py:154
  174.3 0.7 fusion.32
  175.1 0.7 fusion.3
  175.8 1.2 copy.93
  177.0 0.7 copy.94
  177.7 61.0 %all_to_all.26 = bf16[16,256,256]{2,1,0:T(8,128)(2,1)} all-to-all(bf16[16,256,256]{2,1,0:T(8,128)(2,1)S(1)} %copy.94), channel_id=1, replica_groups=mesh['x'=4,'yh'=4,'yl'=2,'z'=8,'c'=2] {'yl','z'}, dimensions={0} | all-to-all | bytes 4194304 | tf_op jit(solution)/shard_map/all_to_all | solution.py:159
  238.7 2.6 %reduce_sum.55 = bf16[256,256]{1,0:T(8,128)(2,1)} reduce(bf16[16,256,256]{2,1,0:T(8,128)(2,1)} %all_to_all.26, bf16[]{:T(256)} %constant.113.clone.1), dimensions={0}, to_apply=%region_7.9 | reduce | flops 983040 | bytes 2228226 | tf_op jit(solution)/shard_map/reduce_sum | solution.py:160
  (43 shorter events, 0.6 us)
Async XLA Ops:
  6.5 45.7 %copy-start = (bf16[32,2,8,1024]{3,2,1,0:T(8,128)(2,1)S(1)}, bf16[32,2,8,1024]{3,2,1,0:T(8,128)(2,1)}, u32[]{:S(2)}) copy-start(bf16[32,2,8,1024]{3,2,1,0:T(8,128)(2,1)} %param.14) | copy-start | bytes 3145732
  6.5 9.4 %copy-start.3 = (bf16[256,512]{1,0:T(8,128)(2,1)S(1)}, bf16[256,512]{1,0:T(8,128)(2,1)}, u32[]{:S(2)}) copy-start(bf16[256,512]{1,0:T(8,128)(2,1)} %param.13) | copy-start | bytes 786436
  8.8 9.8 %copy-start.6 = (s32[1024,1]{0,1:T(1,128)S(1)}, s32[1024,1]{0,1:T(1,128)}, u32[]{:S(2)}) copy-start(s32[1024,1]{0,1:T(1,128)} %param.16) | copy-start | bytes 12292
  8.8 10.7 %copy-start.5 = (s32[1024]{0:T(1024)S(1)}, s32[1024]{0:T(1024)}, u32[]{:S(2)}) copy-start(s32[1024]{0:T(1024)} %param.17) | copy-start | bytes 12292
  8.8 35.0 %all-to-all-start = ((bf16[4,512,320]{1,2,0:T(8,128)(2,1)}), bf16[4,512,320]{1,2,0:T(8,128)(2,1)S(1)}, u32[]{:S(2)}, u32[]{:S(2)}) async-start(bf16[4,512,320]{1,2,0:T(8,128)(2,1)} %broadcast_in_dim.27), calls=%async_computation | async-start | bytes 2621440 | tf_op jit(solution)/shard_map/all_to_all | solution.py:38
  16.1 55.4 %collective-permute-start = (bf16[256,256]{0,1:T(8,128)(2,1)S(1)}, bf16[256,256]{0,1:T(8,128)(2,1)S(1)}, u32[]{:S(2)}, u32[]{:S(2)}) collective-permute-start(bf16[256,256]{0,1:T(8,128)(2,1)S(1)} %get-tuple-element.39), channel_id=1, source_target_pairs={{0,1},{1,0},{2,3},{3,2},{4,5},{5,4},{6,7},{7,6},{8,9},{9,8},{10,11... | collective-permute-start | bytes 393224 | tf_op jit(solution)/shard_map/ppermute | solution.py:81
  45.1 27.3 %collective-permute-start.1 = (bf16[2048,320]{0,1:T(8,128)(2,1)}, bf16[2048,320]{0,1:T(8,128)(2,1)}, u32[]{:S(2)}, u32[]{:S(2)}) collective-permute-start(bf16[2048,320]{0,1:T(8,128)(2,1)} %bitcast.51), channel_id=1, source_target_pairs={{0,128},{128,256},{256,384},{384,0},{1,129},{129,257},{257,385},{3... | collective-permute-start | bytes 3932168 | tf_op jit(solution)/shard_map/ppermute | solution.py:92
  48.5 23.9 %collective-permute-start.2 = (bf16[2048,320]{0,1:T(8,128)(2,1)}, bf16[2048,320]{0,1:T(8,128)(2,1)}, u32[]{:S(2)}, u32[]{:S(2)}) collective-permute-start(bf16[2048,320]{0,1:T(8,128)(2,1)} %bitcast.51), channel_id=1, source_target_pairs={{0,384},{128,0},{256,128},{384,256},{1,385},{129,1},{257,129},{385... | collective-permute-start | bytes 3932168 | tf_op jit(solution)/shard_map/ppermute | solution.py:93
  54.2 64.1 %all-to-all-start.2 = ((bf16[32,2,2,8,1024]{4,3,2,1,0:T(8,128)(2,1)}), bf16[32,2,2,8,1024]{4,3,2,1,0:T(8,128)(2,1)}, u32[]{:S(2)}, u32[]{:S(2)}) async-start(bf16[32,2,2,8,1024]{4,3,2,1,0:T(8,128)(2,1)} %bitcast.127), calls=%async_computation.2 | async-start | bytes 4194304 | tf_op jit(solution)/shard_map/all_to_all | solution.py:124
  68.1 103.7 %all-gather.3.cloned.1.call-start = ((), (), s32[]{:S(2)}) async-start(), calls=%async_computation.5 | async-start | bytes 4456448 | tf_op jit(solution)/shard_map/all_gather | solution.py:95
  68.3 3.2 %copy-start.7 = (s32[256]{0:T(256)S(1)}, s32[256]{0:T(256)}, u32[]{:S(2)}) copy-start(s32[256]{0:T(256)} %param.15) | copy-start | bytes 3076
  68.3 4.2 %copy-start.4 = (bf16[8192]{0:T(1024)(128)(2,1)S(1)}, bf16[8192]{0:T(1024)(128)(2,1)}, u32[]{:S(2)}) copy-start(bf16[8192]{0:T(1024)(128)(2,1)} %param.11) | copy-start | bytes 49156
  76.5 2.6 %copy-start.1 = (bf16[256,8192]{1,0:T(8,128)(2,1)}, bf16[256,8192]{1,0:T(8,128)(2,1)S(1)}, u32[]{:S(2)}) copy-start(bf16[256,8192]{1,0:T(8,128)(2,1)S(1)} %fusion.2) | copy-start | bytes 12582916
  81.1 20.2 %collective-permute-start.3 = (bf16[1024,320]{0,1:T(8,128)(2,1)}, bf16[1024,320]{0,1:T(8,128)(2,1)}, u32[]{:S(2)}, u32[]{:S(2)}) collective-permute-start(bf16[1024,320]{0,1:T(8,128)(2,1)} %slice.40), channel_id=1, source_target_pairs={{0,128},{128,256},{256,384},{384,0},{1,129},{129,257},{257,385},{3... | collective-permute-start | bytes 1966088 | tf_op jit(solution)/shard_map/ppermute | solution.py:98
  86.3 19.5 %collective-permute-start.4 = (bf16[1024,320]{0,1:T(8,128)(2,1)}, bf16[1024,320]{0,1:T(8,128)(2,1)}, u32[]{:S(2)}, u32[]{:S(2)}) collective-permute-start(bf16[1024,320]{0,1:T(8,128)(2,1)} %slice.41), channel_id=1, source_target_pairs={{0,384},{128,0},{256,128},{384,256},{1,385},{129,1},{257,129},{385... | collective-permute-start | bytes 1966088 | tf_op jit(solution)/shard_map/ppermute | solution.py:98
  95.3 2.6 %copy-start.2 = (bf16[32,8,2048]{2,1,0:T(8,128)(2,1)S(1)}, bf16[32,8,2048]{2,1,0:T(8,128)(2,1)}, u32[]{:S(2)}) copy-start(bf16[32,8,2048]{2,1,0:T(8,128)(2,1)} %get-tuple-element.27) | copy-start | bytes 3145732
  118.4 33.0 %all-to-all-start.1 = ((bf16[8,32,320]{2,0,1:T(8,128)(2,1)}), bf16[8,32,320]{2,0,1:T(8,128)(2,1)S(1)}, u32[]{:S(2)}, u32[]{:S(2)}) async-start(bf16[8,32,320]{2,0,1:T(8,128)(2,1)} %fusion.24), calls=%async_computation.1 | async-start | bytes 393216 | tf_op jit(solution)/shard_map/all_to_all | solution.py:33
  168.5 3.2 %collective-permute-start.5 = (bf16[8,32,256]{2,0,1:T(8,128)(2,1)S(1)}, bf16[8,32,256]{2,0,1:T(8,128)(2,1)S(1)}, u32[]{:S(2)}, u32[]{:S(2)}) collective-permute-start(bf16[8,32,256]{2,0,1:T(8,128)(2,1)S(1)} %all_to_all.25), channel_id=1, source_target_pairs={{0,1},{1,0},{2,3},{3,2},{4,5},{5,4},{6,7},{7,6},{8,9},{9,8},{10,11... | collective-permute-start | bytes 393224 | tf_op jit(solution)/shard_map/ppermute | solution.py:146
Sparse Core Ops, SparseCore 0:
  72.5 92.8 all-gather.2

commit v12 on v6

--- a/solution.py
+++ b/solution.py
@@ -150,14 +150,14 @@
     partial = None
     for half in range(cores):
         term = jnp.einsum(
-            "bjh,hpc->jbpc",
+            "bjh,hpc->pjbc",
             head_rows[:, :, half * block : (half + 1) * block],
             w_pair[half * block : (half + 1) * block],
             preferred_element_type=jnp.float32,
         ).astype(jnp.bfloat16).astype(jnp.float32)
         partial = term if partial is None else partial + term
-    partial = partial.astype(jnp.bfloat16).reshape(grouped_row_block, pairs, block)
-    spread = lax.all_to_all(partial.transpose(1, 0, 2), PAIR, 0, 0, tiled=True)
+    partial = partial.astype(jnp.bfloat16).reshape(pairs, grouped_row_block, block)
+    spread = lax.all_to_all(partial, PAIR, 0, 0, tiled=True)
     return jnp.sum(spread.astype(jnp.float32), axis=0).astype(jnp.bfloat16)
 
 

time: 248 us -> 248 us (level)
  no operation moved by 1% of the time
where the time goes in v12:
time: 248 us; the launch traced here: 246 us
  blocking collectives  77.1 us (31%)
  waiting for transfers between devices  52.4 us (21%)
  starting transfers between devices  52 us (21%)
  local copies, waits for them, and re-layouts  25.2 us (10%)
  between operations  13.9 us (6%)
  matrix products  12.8 us (5%)
  other arithmetic  12.4 us (5%)
    all_to_all x1, blocking collectives, shards(): spread = lax.all_to_all(partial, PAIR, 0, 0, tiled=True)  56.4 us
    all_to_all x1, waiting for transfers between devices, gather_rows(): lax.all_to_all(copies, axis, 0, 0, tiled=True)  23.9 us
    all_to_all x1, blocking collectives, shards(): lax.all_to_all(doubled.reshape(own_beams, columns, pair_feats.shape[3]),...  20.7 us
    all_to_all x1, waiting for transfers between devices, regroup(): return lax.all_to_all(blocks, BEAM, split_axis=1, concat_axis=1, tiled=True)  15.5 us
    all_to_all x1, starting transfers between devices, regroup(): return lax.all_to_all(blocks, BEAM, split_axis=1, concat_axis=1, tiled=True)  15 us
    all_to_all x1, starting transfers between devices, shards(): lax.all_to_all(outgoing, BEAM, split_axis=0, concat_axis=0, tiled=True)  13.9 us
    dot_general x4, matrix products, shards(): jnp.einsum('jbd,dc->bjc', block.reshape(columns, own_beams, rows), piece,...  10.1 us
    all_to_all x1, waiting for transfers between devices, shards(): lax.all_to_all(outgoing, BEAM, split_axis=0, concat_axis=0, tiled=True)  7.18 us
  transfers between devices with their start and end apart: 9, of which 5 were waited for; matrix products, arithmetic and copies ran while one was open for 16% of the time, Pallas kernels for 0%

profile of v12, /device:TPU:56, one launch (start us, length us, event | category | flops | bytes accessed | tf_op | source)
XLA Modules:
  0.0 245.7 jit_solution(15796158393036346080)
XLA Ops:
  6.5 2.2 broadcast_in_dim.29
  8.8 7.1 %all-to-all-start = ((bf16[4,512,320]{1,2,0:T(8,128)(2,1)}), bf16[4,512,320]{1,2,0:T(8,128)(2,1)S(1)}, u32[]{:S(2)}, u32[]{:S(2)}) async-start(bf16[4,512,320]{1,2,0:T(8,128)(2,1)} %broadcast_in_dim.29), calls=%async_computation | async-start | bytes 2621440 | tf_op jit(solution)/shard_map/all_to_all | solution.py:38
  15.9 0.1 copy.70
  16.1 1.9 collective-permute-start
  18.0 0.5 broadcast.199
  18.5 0.7 reduce.4
  19.2 0.1 reshape.236
  19.3 0.2 reduce_window_sum.22
  19.5 0.1 mul.217
  19.6 0.1 multiply_reduce_fusion
  19.7 0.1 copy.83
  19.8 0.1 reshape.237
  19.9 23.9 %all-to-all-done = bf16[4,512,320]{1,2,0:T(8,128)(2,1)S(1)} async-done(((bf16[4,512,320]{1,2,0:T(8,128)(2,1)}), bf16[4,512,320]{1,2,0:T(8,128)(2,1)S(1)}, u32[]{:S(2)}, u32[]{:S(2)}) %all-to-all-start) | async-done | bytes 1310752 | tf_op jit(solution)/shard_map/all_to_all | solution.py:38
  43.8 1.3 copy.106
  45.1 3.4 %collective-permute-start.1 = (bf16[2048,320]{0,1:T(8,128)(2,1)}, bf16[2048,320]{0,1:T(8,128)(2,1)}, u32[]{:S(2)}, u32[]{:S(2)}) collective-permute-start(bf16[2048,320]{0,1:T(8,128)(2,1)} %bitcast.50), channel_id=1, source_target_pairs={{0,128},{128,256},{256,384},{384,0},{1,129},{129,257},{257,385},{3... | collective-permute-start | bytes 3932168 | tf_op jit(solution)/shard_map/ppermute | solution.py:92
  48.5 3.7 %collective-permute-start.2 = (bf16[2048,320]{0,1:T(8,128)(2,1)}, bf16[2048,320]{0,1:T(8,128)(2,1)}, u32[]{:S(2)}, u32[]{:S(2)}) collective-permute-start(bf16[2048,320]{0,1:T(8,128)(2,1)} %bitcast.50), channel_id=1, source_target_pairs={{0,384},{128,0},{256,128},{384,256},{1,385},{129,1},{257,129},{385... | collective-permute-start | bytes 3932168 | tf_op jit(solution)/shard_map/ppermute | solution.py:93
  52.2 2.0 gather_fusion
  54.2 13.9 %all-to-all-start.2 = ((bf16[32,2,2,8,1024]{4,3,2,1,0:T(8,128)(2,1)}), bf16[32,2,2,8,1024]{4,3,2,1,0:T(8,128)(2,1)}, u32[]{:S(2)}, u32[]{:S(2)}) async-start(bf16[32,2,2,8,1024]{4,3,2,1,0:T(8,128)(2,1)} %bitcast.128), calls=%async_computation.2 | async-start | bytes 4194304 | tf_op jit(solution)/shard_map/all_to_all | solution.py:124
  68.2 0.1 fusion.41
  68.2 3.1 %fusion = f32[256]{0:T(256)S(1)} fusion(bf16[256,8192]{1,0:T(8,128)(2,1)} %param.10), kind=kLoop, calls=%fused_computation.4 | loop fusion | flops 6291200 | bytes 4195328 | tf_op jit(solution)/shard_map/reduce_sum | solution.py:84
  71.4 0.1 fusion.51
  71.5 0.8 maximum_select_fusion
  72.4 0.1 iota_compare_fusion.2
  72.6 0.2 select_reduce_fusion
  72.8 0.1 multiply_cosine_fusion
  72.9 3.6 %fusion.2 = bf16[256,8192]{1,0:T(8,128)(2,1)S(1)} fusion(bf16[256,8192]{1,0:T(8,128)(2,1)} %param.10, f32[8192]{0:T(1024)S(1)} %convert_element_type.100, f32[256]{0:T(256)S(1)} %add_rsqrt_fusion), kind=kLoop, calls=%fused_computation.6 | loop fusion | flops 8388608 | bytes 8422400 | tf_op jit(solution)/shard_map/convert_element_type | solution.py:85
  76.5 1.9 dynamic-slice_bitcast_fusion.2
  78.4 0.7 copy-done.1
  79.1 2.0 slice.46
  81.1 3.3 %collective-permute-start.3 = (bf16[1024,320]{0,1:T(8,128)(2,1)}, bf16[1024,320]{0,1:T(8,128)(2,1)}, u32[]{:S(2)}, u32[]{:S(2)}) collective-permute-start(bf16[1024,320]{0,1:T(8,128)(2,1)} %slice.46), channel_id=1, source_target_pairs={{0,128},{128,256},{256,384},{384,0},{1,129},{129,257},{257,385},{3... | collective-permute-start | bytes 1966088 | tf_op jit(solution)/shard_map/ppermute | solution.py:98
  84.3 2.0 slice.47
  86.3 3.8 %collective-permute-start.4 = (bf16[1024,320]{0,1:T(8,128)(2,1)}, bf16[1024,320]{0,1:T(8,128)(2,1)}, u32[]{:S(2)}, u32[]{:S(2)}) collective-permute-start(bf16[1024,320]{0,1:T(8,128)(2,1)} %slice.47), channel_id=1, source_target_pairs={{0,384},{128,0},{256,128},{384,256},{1,385},{129,1},{257,129},{385... | collective-permute-start | bytes 1966088 | tf_op jit(solution)/shard_map/ppermute | solution.py:98
  90.1 2.1 copy.73
  92.2 3.0 %reshape.322 = bf16[2048,320,1]{0,1,2:T(8,128)(2,1)S(1)} reshape(bf16[4,512,320]{1,0,2:T(4,128)(2,1)} %copy.73) | data formatting | bytes 2621440 | tf_op jit(solution)/shard_map/reshape | solution.py:38
  95.3 2.6 %fusion.7 = f32[320,32,8]{0,1,2:T(8,128)S(1)} fusion(bf16[2048,320]{0,1:T(8,128)(2,1)} %collective-permute-done.1, bf16[32,8,2048]{2,1,0:T(8,128)(2,1)} %get-tuple-element.29), kind=kOutput, calls=%fused_computation.14 | convolution fusion | flops 335544320 | bytes 2686976 | tf_op jit(solution)/shard_map/jbd,dc->bjc/dot_general | solution.py:106
  97.9 2.2 fusion.9
  100.1 1.2 collective-permute-done.3
  101.3 4.5 %collective-permute-done.4 = bf16[1024,320]{0,1:T(8,128)(2,1)} collective-permute-done((bf16[1024,320]{0,1:T(8,128)(2,1)}, bf16[1024,320]{0,1:T(8,128)(2,1)}, u32[]{:S(2)}, u32[]{:S(2)}) %collective-permute-start.4) | collective-permute-done | bytes 655392 | tf_op jit(solution)/shard_map/ppermute | solution.py:98
  105.8 2.2 fusion.4
  108.0 3.1 %fusion.24 = bf16[8,32,320]{2,0,1:T(8,128)(2,1)} fusion(f32[320,32,8]{0,1,2:T(8,128)S(1)} %fusion.4, f32[320,32,8]{0,1,2:T(8,128)S(1)} %fusion.7, bf16[2048,320,1]{0,1,2:T(8,128)(2,1)S(1)} %reshape.322, bf16[256,8192]{1,0:T(8,128)(2,1)} %copy-done.1, s32[]{:T(128)S(6)} %select_n.83, f32[320,32,8]{0,1,2:T(8,128)S(1)} %fusion.9), kind=kOutput, calls=%fused_computation.38 | convolution fusion | flops 335872000 | bytes 3506180 | tf_op jit(solution)/shard_map/jbd,dc->bjc/dot_general | solution.py:106
  111.1 7.2 %all-to-all-done.2 = bf16[32,2,2,8,1024]{4,3,2,1,0:T(8,128)(2,1)} async-done(((bf16[32,2,2,8,1024]{4,3,2,1,0:T(8,128)(2,1)}), bf16[32,2,2,8,1024]{4,3,2,1,0:T(8,128)(2,1)}, u32[]{:S(2)}, u32[]{:S(2)}) %all-to-all-start.2) | async-done | bytes 2097184 | tf_op jit(solution)/shard_map/all_to_all | solution.py:124
  118.3 15.0 %all-to-all-start.1 = ((bf16[8,32,320]{2,0,1:T(8,128)(2,1)}), bf16[8,32,320]{2,0,1:T(8,128)(2,1)S(1)}, u32[]{:S(2)}, u32[]{:S(2)}) async-start(bf16[8,32,320]{2,0,1:T(8,128)(2,1)} %fusion.24), calls=%async_computation.1 | async-start | bytes 393216 | tf_op jit(solution)/shard_map/all_to_all | solution.py:33
  133.3 2.2 gather_fusion.1
  135.5 0.3 copy.107
  135.8 0.1 fusion.53
  135.9 15.5 %all-to-all-done.1 = bf16[8,32,320]{2,0,1:T(8,128)(2,1)S(1)} async-done(((bf16[8,32,320]{2,0,1:T(8,128)(2,1)}), bf16[8,32,320]{2,0,1:T(8,128)(2,1)S(1)}, u32[]{:S(2)}, u32[]{:S(2)}) %all-to-all-start.1) | async-done | bytes 163872 | tf_op jit(solution)/shard_map/all_to_all | solution.py:33
  151.4 0.2 reshape.235
  151.6 0.1 subtract_convert_fusion.1
  151.7 0.1 maximum_bitcast_fusion.2
  151.8 0.1 fusion.55
  151.9 0.1 fusion.28
  152.1 0.3 fusion.36
  152.3 0.5 fusion.56
  152.9 0.3 fusion.27
  153.2 0.3 fusion.14
  153.5 0.1 convert_element_type.116
  153.6 0.1 copy.87
  153.7 20.7 %all_to_all.25 = bf16[8,32,512]{2,0,1:T(8,128)(2,1)S(1)} all-to-all(bf16[8,32,512]{2,0,1:T(8,128)(2,1)S(1)} %bitcast.135), channel_id=1, replica_groups=mesh['x'=4,'yh'=4,'yl'=2,'z'=8,'c'=2] {'yl','z','c'}, dimensions={1} | all-to-all | bytes 524288 | tf_op jit(solution)/shard_map/all_to_all | solution.py:146
  174.5 2.5 %fusion.52 = (bf16[256,4096]{0,1:T(8,128)(2,1)S(1)}, bf16[256,4096]{0,1:T(8,128)(2,1)S(1)}) fusion(bf16[512,4096]{0,1:T(8,128)(2,1)} %all-gather.3.cloned.1.call-done), kind=kLoop, calls=%fused_computation.100 | loop fusion | bytes 8388608 | tf_op jit(solution)/shard_map/slice | solution.py:155
  177.0 0.7 fusion.31
  177.7 0.7 fusion.3
  178.5 1.4 copy.148
  179.9 56.4 %all_to_all.26 = bf16[16,256,256]{2,1,0:T(8,128)(2,1)} all-to-all(bf16[16,256,256]{2,1,0:T(8,128)(2,1)S(1)} %bitcast.130), channel_id=1, replica_groups=mesh['x'=4,'yh'=4,'yl'=2,'z'=8,'c'=2] {'yl','z'}, dimensions={0} | all-to-all | bytes 4194304 | tf_op jit(solution)/shard_map/all_to_all | solution.py:160
  236.3 2.6 %reduce_sum.55 = bf16[256,256]{1,0:T(8,128)(2,1)} reduce(bf16[16,256,256]{2,1,0:T(8,128)(2,1)} %all_to_all.26, bf16[]{:T(256)} %constant.113.clone.1), dimensions={0}, to_apply=%region_7.9 | reduce | flops 983040 | bytes 2228226 | tf_op jit(solution)/shard_map/reduce_sum | solution.py:161
  (41 shorter events, 0.4 us)
Async XLA Ops:
  6.5 45.6 %copy-start = (bf16[32,2,8,1024]{3,2,1,0:T(8,128)(2,1)S(1)}, bf16[32,2,8,1024]{3,2,1,0:T(8,128)(2,1)}, u32[]{:S(2)}) copy-start(bf16[32,2,8,1024]{3,2,1,0:T(8,128)(2,1)} %param.14) | copy-start | bytes 3145732
  6.5 9.4 %copy-start.3 = (bf16[256,512]{1,0:T(8,128)(2,1)S(1)}, bf16[256,512]{1,0:T(8,128)(2,1)}, u32[]{:S(2)}) copy-start(bf16[256,512]{1,0:T(8,128)(2,1)} %param.13) | copy-start | bytes 786436
  8.8 9.8 %copy-start.6 = (s32[1024,1]{0,1:T(1,128)S(1)}, s32[1024,1]{0,1:T(1,128)}, u32[]{:S(2)}) copy-start(s32[1024,1]{0,1:T(1,128)} %param.16) | copy-start | bytes 12292
  8.8 10.7 %copy-start.5 = (s32[1024]{0:T(1024)S(1)}, s32[1024]{0:T(1024)}, u32[]{:S(2)}) copy-start(s32[1024]{0:T(1024)} %param.17) | copy-start | bytes 12292
  8.8 35.0 %all-to-all-start = ((bf16[4,512,320]{1,2,0:T(8,128)(2,1)}), bf16[4,512,320]{1,2,0:T(8,128)(2,1)S(1)}, u32[]{:S(2)}, u32[]{:S(2)}) async-start(bf16[4,512,320]{1,2,0:T(8,128)(2,1)} %broadcast_in_dim.29), calls=%async_computation | async-start | bytes 2621440 | tf_op jit(solution)/shard_map/all_to_all | solution.py:38
  16.1 55.4 %collective-permute-start = (bf16[256,256]{0,1:T(8,128)(2,1)S(1)}, bf16[256,256]{0,1:T(8,128)(2,1)S(1)}, u32[]{:S(2)}, u32[]{:S(2)}) collective-permute-start(bf16[256,256]{0,1:T(8,128)(2,1)S(1)} %get-tuple-element.39), channel_id=1, source_target_pairs={{0,1},{1,0},{2,3},{3,2},{4,5},{5,4},{6,7},{7,6},{8,9},{9,8},{10,11... | collective-permute-start | bytes 393224 | tf_op jit(solution)/shard_map/ppermute | solution.py:81
  45.1 27.3 %collective-permute-start.1 = (bf16[2048,320]{0,1:T(8,128)(2,1)}, bf16[2048,320]{0,1:T(8,128)(2,1)}, u32[]{:S(2)}, u32[]{:S(2)}) collective-permute-start(bf16[2048,320]{0,1:T(8,128)(2,1)} %bitcast.50), channel_id=1, source_target_pairs={{0,128},{128,256},{256,384},{384,0},{1,129},{129,257},{257,385},{3... | collective-permute-start | bytes 3932168 | tf_op jit(solution)/shard_map/ppermute | solution.py:92
  48.5 23.9 %collective-permute-start.2 = (bf16[2048,320]{0,1:T(8,128)(2,1)}, bf16[2048,320]{0,1:T(8,128)(2,1)}, u32[]{:S(2)}, u32[]{:S(2)}) collective-permute-start(bf16[2048,320]{0,1:T(8,128)(2,1)} %bitcast.50), channel_id=1, source_target_pairs={{0,384},{128,0},{256,128},{384,256},{1,385},{129,1},{257,129},{385... | collective-permute-start | bytes 3932168 | tf_op jit(solution)/shard_map/ppermute | solution.py:93
  54.2 64.1 %all-to-all-start.2 = ((bf16[32,2,2,8,1024]{4,3,2,1,0:T(8,128)(2,1)}), bf16[32,2,2,8,1024]{4,3,2,1,0:T(8,128)(2,1)}, u32[]{:S(2)}, u32[]{:S(2)}) async-start(bf16[32,2,2,8,1024]{4,3,2,1,0:T(8,128)(2,1)} %bitcast.128), calls=%async_computation.2 | async-start | bytes 4194304 | tf_op jit(solution)/shard_map/all_to_all | solution.py:124
  68.1 106.4 %all-gather.3.cloned.1.call-start = ((), (), s32[]{:S(2)}) async-start(), calls=%async_computation.5 | async-start | bytes 4456448 | tf_op jit(solution)/shard_map/all_gather | solution.py:95
  68.2 3.2 %copy-start.7 = (s32[256]{0:T(256)S(1)}, s32[256]{0:T(256)}, u32[]{:S(2)}) copy-start(s32[256]{0:T(256)} %param.15) | copy-start | bytes 3076
  68.2 4.2 %copy-start.4 = (bf16[8192]{0:T(1024)(128)(2,1)S(1)}, bf16[8192]{0:T(1024)(128)(2,1)}, u32[]{:S(2)}) copy-start(bf16[8192]{0:T(1024)(128)(2,1)} %param.11) | copy-start | bytes 49156
  76.5 2.6 %copy-start.1 = (bf16[256,8192]{1,0:T(8,128)(2,1)}, bf16[256,8192]{1,0:T(8,128)(2,1)S(1)}, u32[]{:S(2)}) copy-start(bf16[256,8192]{1,0:T(8,128)(2,1)S(1)} %fusion.2) | copy-start | bytes 12582916
  81.1 20.2 %collective-permute-start.3 = (bf16[1024,320]{0,1:T(8,128)(2,1)}, bf16[1024,320]{0,1:T(8,128)(2,1)}, u32[]{:S(2)}, u32[]{:S(2)}) collective-permute-start(bf16[1024,320]{0,1:T(8,128)(2,1)} %slice.46), channel_id=1, source_target_pairs={{0,128},{128,256},{256,384},{384,0},{1,129},{129,257},{257,385},{3... | collective-permute-start | bytes 1966088 | tf_op jit(solution)/shard_map/ppermute | solution.py:98
  86.3 19.5 %collective-permute-start.4 = (bf16[1024,320]{0,1:T(8,128)(2,1)}, bf16[1024,320]{0,1:T(8,128)(2,1)}, u32[]{:S(2)}, u32[]{:S(2)}) collective-permute-start(bf16[1024,320]{0,1:T(8,128)(2,1)} %slice.47), channel_id=1, source_target_pairs={{0,384},{128,0},{256,128},{384,256},{1,385},{129,1},{257,129},{385... | collective-permute-start | bytes 1966088 | tf_op jit(solution)/shard_map/ppermute | solution.py:98
  95.3 2.6 %copy-start.2 = (bf16[32,8,2048]{2,1,0:T(8,128)(2,1)S(1)}, bf16[32,8,2048]{2,1,0:T(8,128)(2,1)}, u32[]{:S(2)}) copy-start(bf16[32,8,2048]{2,1,0:T(8,128)(2,1)} %get-tuple-element.27) | copy-start | bytes 3145732
  118.3 33.0 %all-to-all-start.1 = ((bf16[8,32,320]{2,0,1:T(8,128)(2,1)}), bf16[8,32,320]{2,0,1:T(8,128)(2,1)S(1)}, u32[]{:S(2)}, u32[]{:S(2)}) async-start(bf16[8,32,320]{2,0,1:T(8,128)(2,1)} %fusion.24), calls=%async_computation.1 | async-start | bytes 393216 | tf_op jit(solution)/shard_map/all_to_all | solution.py:33
Sparse Core Ops, SparseCore 0:
  72.5 93.3 all-gather.2

commit v13 on v12

--- a/solution.py
+++ b/solution.py
@@ -147,15 +147,13 @@
         doubled.reshape(own_beams, columns, pair_feats.shape[3]), BEAM, 1, 1, tiled=True
     )
     block = attn.shape[1] // columns
-    partial = None
-    for half in range(cores):
-        term = jnp.einsum(
-            "bjh,hpc->pjbc",
-            head_rows[:, :, half * block : (half + 1) * block],
-            w_pair[half * block : (half + 1) * block],
-            preferred_element_type=jnp.float32,
-        ).astype(jnp.bfloat16).astype(jnp.float32)
-        partial = term if partial is None else partial + term
+    halves_out = jnp.einsum(
+        "bjkh,khpc->kpjbc",
+        head_rows.reshape(own_beams, columns, cores, block),
+        w_pair.reshape(cores, block, pairs, block),
+        preferred_element_type=jnp.float32,
+    )
+    partial = jnp.sum(halves_out.astype(jnp.bfloat16).astype(jnp.float32), axis=0)
     partial = partial.astype(jnp.bfloat16).reshape(pairs, grouped_row_block, block)
     spread = lax.all_to_all(partial, PAIR, 0, 0, tiled=True)
     return jnp.sum(spread.astype(jnp.float32), axis=0).astype(jnp.bfloat16)

time: 248 us -> 254 us (1.024)
  local copies, waits for them, and re-layouts: 25.2 us -> 29.8 us
    reshape x0 -> x2, local copies, waits for them, and re-layouts: none -> 7.02 us  [the longest x1 6.96 us: shards(): w_pair.reshape(cores, block, pairs, block)]
where the time goes in v13:
time: 254 us; the launch traced here: 252 us
  blocking collectives  76.4 us (30%)
  waiting for transfers between devices  52.3 us (21%)
  starting transfers between devices  52.1 us (21%)
  local copies, waits for them, and re-layouts  29.8 us (12%)
  matrix products  15 us (6%)
  between operations  13.9 us (5%)
  other arithmetic  12.4 us (5%)
    all_to_all x1, blocking collectives, shards(): spread = lax.all_to_all(partial, PAIR, 0, 0, tiled=True)  55.4 us
    all_to_all x1, waiting for transfers between devices, gather_rows(): lax.all_to_all(copies, axis, 0, 0, tiled=True)  23.9 us
    all_to_all x1, blocking collectives, shards(): lax.all_to_all(doubled.reshape(own_beams, columns, pair_feats.shape[3]),...  21.1 us
    all_to_all x1, waiting for transfers between devices, regroup(): return lax.all_to_all(blocks, BEAM, split_axis=1, concat_axis=1, tiled=True)  15.5 us
    all_to_all x1, starting transfers between devices, regroup(): return lax.all_to_all(blocks, BEAM, split_axis=1, concat_axis=1, tiled=True)  14.9 us
    all_to_all x1, starting transfers between devices, shards(): lax.all_to_all(outgoing, BEAM, split_axis=0, concat_axis=0, tiled=True)  14 us
    dot_general x4, matrix products, shards(): jnp.einsum('jbd,dc->bjc', block.reshape(columns, own_beams, rows), piece,...  10.2 us
    all_to_all x1, waiting for transfers between devices, shards(): lax.all_to_all(outgoing, BEAM, split_axis=0, concat_axis=0, tiled=True)  7.13 us
  transfers between devices with their start and end apart: 9, of which 5 were waited for; matrix products, arithmetic and copies ran while one was open for 16% of the time, Pallas kernels for 0%

profile of v13, /device:TPU:56, one launch (start us, length us, event | category | flops | bytes accessed | tf_op | source)
XLA Modules:
  0.0 251.8 jit_solution(12075042042625968868)
XLA Ops:
  6.5 2.2 broadcast_in_dim.29
  8.8 7.1 %all-to-all-start = ((bf16[4,512,320]{1,2,0:T(8,128)(2,1)}), bf16[4,512,320]{1,2,0:T(8,128)(2,1)S(1)}, u32[]{:S(2)}, u32[]{:S(2)}) async-start(bf16[4,512,320]{1,2,0:T(8,128)(2,1)} %broadcast_in_dim.29), calls=%async_computation | async-start | bytes 2621440 | tf_op jit(solution)/shard_map/all_to_all | solution.py:38
  15.9 0.1 copy.67
  16.1 1.9 collective-permute-start
  18.0 0.5 broadcast.199
  18.5 0.7 reduce.6
  19.2 0.1 reshape.243
  19.3 0.2 reduce_window_sum.22
  19.5 0.1 mul.217
  19.5 0.1 multiply_reduce_fusion
  19.7 0.1 copy.81
  19.8 0.1 reshape.244
  19.9 23.9 %all-to-all-done = bf16[4,512,320]{1,2,0:T(8,128)(2,1)S(1)} async-done(((bf16[4,512,320]{1,2,0:T(8,128)(2,1)}), bf16[4,512,320]{1,2,0:T(8,128)(2,1)S(1)}, u32[]{:S(2)}, u32[]{:S(2)}) %all-to-all-start) | async-done | bytes 1310752 | tf_op jit(solution)/shard_map/all_to_all | solution.py:38
  43.8 1.2 copy.105
  45.1 3.4 %collective-permute-start.1 = (bf16[2048,320]{0,1:T(8,128)(2,1)}, bf16[2048,320]{0,1:T(8,128)(2,1)}, u32[]{:S(2)}, u32[]{:S(2)}) collective-permute-start(bf16[2048,320]{0,1:T(8,128)(2,1)} %bitcast.40), channel_id=1, source_target_pairs={{0,128},{128,256},{256,384},{384,0},{1,129},{129,257},{257,385},{3... | collective-permute-start | bytes 3932168 | tf_op jit(solution)/shard_map/ppermute | solution.py:92
  48.5 3.7 %collective-permute-start.2 = (bf16[2048,320]{0,1:T(8,128)(2,1)}, bf16[2048,320]{0,1:T(8,128)(2,1)}, u32[]{:S(2)}, u32[]{:S(2)}) collective-permute-start(bf16[2048,320]{0,1:T(8,128)(2,1)} %bitcast.40), channel_id=1, source_target_pairs={{0,384},{128,0},{256,128},{384,256},{1,385},{129,1},{257,129},{385... | collective-permute-start | bytes 3932168 | tf_op jit(solution)/shard_map/ppermute | solution.py:93
  52.2 2.0 gather_fusion
  54.1 14.0 %all-to-all-start.2 = ((bf16[32,2,2,8,1024]{4,3,2,1,0:T(8,128)(2,1)}), bf16[32,2,2,8,1024]{4,3,2,1,0:T(8,128)(2,1)}, u32[]{:S(2)}, u32[]{:S(2)}) async-start(bf16[32,2,2,8,1024]{4,3,2,1,0:T(8,128)(2,1)} %bitcast.115), calls=%async_computation.2 | async-start | bytes 4194304 | tf_op jit(solution)/shard_map/all_to_all | solution.py:124
  68.3 0.1 fusion.54
  68.4 3.1 %fusion = f32[256]{0:T(256)S(1)} fusion(bf16[256,8192]{1,0:T(8,128)(2,1)} %param.10), kind=kLoop, calls=%fused_computation.4 | loop fusion | flops 6291200 | bytes 4195328 | tf_op jit(solution)/shard_map/reduce_sum | solution.py:84
  71.5 0.1 iota_compare_fusion.2
  71.6 0.8 maximum_select_fusion
  72.4 0.1 fusion.44
  72.6 0.2 select_reduce_fusion
  72.8 0.1 multiply_cosine_fusion
  72.9 3.6 %fusion.2 = bf16[256,8192]{1,0:T(8,128)(2,1)S(1)} fusion(bf16[256,8192]{1,0:T(8,128)(2,1)} %param.10, f32[8192]{0:T(1024)S(1)} %convert_element_type.84, f32[256]{0:T(256)S(1)} %add_rsqrt_fusion), kind=kLoop, calls=%fused_computation.6 | loop fusion | flops 8388608 | bytes 8422400 | tf_op jit(solution)/shard_map/convert_element_type | solution.py:85
  76.6 1.9 dynamic-slice_bitcast_fusion.2
  78.4 0.8 copy-done.1
  79.2 2.0 slice.33
  81.2 3.2 %collective-permute-start.3 = (bf16[1024,320]{0,1:T(8,128)(2,1)}, bf16[1024,320]{0,1:T(8,128)(2,1)}, u32[]{:S(2)}, u32[]{:S(2)}) collective-permute-start(bf16[1024,320]{0,1:T(8,128)(2,1)} %slice.33), channel_id=1, source_target_pairs={{0,128},{128,256},{256,384},{384,0},{1,129},{129,257},{257,385},{3... | collective-permute-start | bytes 1966088 | tf_op jit(solution)/shard_map/ppermute | solution.py:98
  84.4 2.0 slice.34
  86.4 3.9 %collective-permute-start.4 = (bf16[1024,320]{0,1:T(8,128)(2,1)}, bf16[1024,320]{0,1:T(8,128)(2,1)}, u32[]{:S(2)}, u32[]{:S(2)}) collective-permute-start(bf16[1024,320]{0,1:T(8,128)(2,1)} %slice.34), channel_id=1, source_target_pairs={{0,384},{128,0},{256,128},{384,256},{1,385},{129,1},{257,129},{385... | collective-permute-start | bytes 1966088 | tf_op jit(solution)/shard_map/ppermute | solution.py:98
  90.3 2.1 copy.70
  92.4 3.0 %reshape.329 = bf16[2048,320,1]{0,1,2:T(8,128)(2,1)S(1)} reshape(bf16[4,512,320]{1,0,2:T(4,128)(2,1)} %copy.70) | data formatting | bytes 2621440 | tf_op jit(solution)/shard_map/reshape | solution.py:38
  95.4 2.6 %fusion.10 = f32[320,32,8]{0,1,2:T(8,128)S(1)} fusion(bf16[2048,320]{0,1:T(8,128)(2,1)} %collective-permute-done.1, bf16[32,8,2048]{2,1,0:T(8,128)(2,1)} %get-tuple-element.27), kind=kOutput, calls=%fused_computation.15 | convolution fusion | flops 335544320 | bytes 2686976 | tf_op jit(solution)/shard_map/jbd,dc->bjc/dot_general | solution.py:106
  98.0 2.2 fusion.12
  100.3 1.2 collective-permute-done.3
  101.4 4.5 %collective-permute-done.4 = bf16[1024,320]{0,1:T(8,128)(2,1)} collective-permute-done((bf16[1024,320]{0,1:T(8,128)(2,1)}, bf16[1024,320]{0,1:T(8,128)(2,1)}, u32[]{:S(2)}, u32[]{:S(2)}) %collective-permute-start.4) | collective-permute-done | bytes 655392 | tf_op jit(solution)/shard_map/ppermute | solution.py:98
  106.0 2.2 fusion.7
  108.1 3.1 %fusion.27 = bf16[8,32,320]{2,0,1:T(8,128)(2,1)} fusion(f32[320,32,8]{0,1,2:T(8,128)S(1)} %fusion.7, f32[320,32,8]{0,1,2:T(8,128)S(1)} %fusion.10, bf16[2048,320,1]{0,1,2:T(8,128)(2,1)S(1)} %reshape.329, bf16[256,8192]{1,0:T(8,128)(2,1)} %copy-done.1, s32[]{:T(128)S(6)} %select_n.83, f32[320,32,8]{0,1,2:T(8,128)S(1)} %fusion.12), kind=kOutput, calls=%fused_computation.39 | convolution fusion | flops 335872000 | bytes 3506180 | tf_op jit(solution)/shard_map/jbd,dc->bjc/dot_general | solution.py:106
  111.3 7.1 %all-to-all-done.2 = bf16[32,2,2,8,1024]{4,3,2,1,0:T(8,128)(2,1)} async-done(((bf16[32,2,2,8,1024]{4,3,2,1,0:T(8,128)(2,1)}), bf16[32,2,2,8,1024]{4,3,2,1,0:T(8,128)(2,1)}, u32[]{:S(2)}, u32[]{:S(2)}) %all-to-all-start.2) | async-done | bytes 2097184 | tf_op jit(solution)/shard_map/all_to_all | solution.py:124
  118.4 14.9 %all-to-all-start.1 = ((bf16[8,32,320]{2,0,1:T(8,128)(2,1)}), bf16[8,32,320]{2,0,1:T(8,128)(2,1)S(1)}, u32[]{:S(2)}, u32[]{:S(2)}) async-start(bf16[8,32,320]{2,0,1:T(8,128)(2,1)} %fusion.27), calls=%async_computation.1 | async-start | bytes 393216 | tf_op jit(solution)/shard_map/all_to_all | solution.py:33
  133.4 2.2 gather_fusion.1
  135.6 0.3 copy.106
  135.9 0.1 fusion.55
  135.9 15.5 %all-to-all-done.1 = bf16[8,32,320]{2,0,1:T(8,128)(2,1)S(1)} async-done(((bf16[8,32,320]{2,0,1:T(8,128)(2,1)}), bf16[8,32,320]{2,0,1:T(8,128)(2,1)S(1)}, u32[]{:S(2)}, u32[]{:S(2)}) %all-to-all-start.1) | async-done | bytes 163872 | tf_op jit(solution)/shard_map/all_to_all | solution.py:33
  151.4 0.2 reshape.242
  151.7 0.1 subtract_convert_fusion.1
  151.7 0.1 maximum_bitcast_fusion.2
  151.8 0.1 fusion.56
  152.0 0.1 fusion.32
  152.1 0.3 fusion.39
  152.4 0.5 fusion.57
  152.9 0.3 fusion.31
  153.2 0.3 fusion.17
  153.6 0.1 convert_element_type.100
  153.7 0.1 copy.85
  153.8 21.1 %all_to_all.25 = bf16[8,32,512]{2,0,1:T(8,128)(2,1)S(1)} all-to-all(bf16[8,32,512]{2,0,1:T(8,128)(2,1)S(1)} %bitcast.122), channel_id=1, replica_groups=mesh['x'=4,'yh'=4,'yl'=2,'z'=8,'c'=2] {'yl','z','c'}, dimensions={1} | all-to-all | bytes 524288 | tf_op jit(solution)/shard_map/all_to_all | solution.py:146
  174.8 0.1 reshape.339
  174.9 7.0 %reshape.337 = bf16[2,256,16,256]{1,0,3,2:T(2,128)(2,1)} reshape(bf16[512,4096]{0,1:T(8,128)(2,1)} %all-gather.3.cloned.1.call-done) | data formatting | bytes 8388608 | tf_op jit(solution)/shard_map/reshape | solution.py:153
  181.9 3.7 %convert_reduce_fusion = bf16[16,256,8,32]{1,3,2,0:T(8,128)(2,1)S(1)} fusion(bf16[2,256,16,256,1]{1,0,3,2,4:T(2,128)(2,1)} %bitcast.118, bf16[8,32,2,256,1]{3,2,0,1,4:T(2,128)(2,1)S(1)} %bitcast.123), kind=kOutput, calls=%fused_computation.9 | convolution fusion | flops 1076887552 | bytes 6553600 | tf_op jit(solution)/shard_map/bjkh,khpc->kpjbc/dot_general | solution.py:150
  185.6 1.4 copy.149
  187.1 55.4 %all_to_all.26 = bf16[16,256,256]{2,1,0:T(8,128)(2,1)} all-to-all(bf16[16,256,256]{2,1,0:T(8,128)(2,1)S(1)} %bitcast.116), channel_id=1, replica_groups=mesh['x'=4,'yh'=4,'yl'=2,'z'=8,'c'=2] {'yl','z'}, dimensions={0} | all-to-all | bytes 4194304 | tf_op jit(solution)/shard_map/all_to_all | solution.py:158
  242.4 2.6 %reduce_sum.71 = bf16[256,256]{1,0:T(8,128)(2,1)} reduce(bf16[16,256,256]{2,1,0:T(8,128)(2,1)} %all_to_all.26, bf16[]{:T(256)} %constant.114.clone.1), dimensions={0}, to_apply=%region_8.10 | reduce | flops 983040 | bytes 2228226 | tf_op jit(solution)/shard_map/reduce_sum | solution.py:159
  (40 shorter events, 0.4 us)
Async XLA Ops:
  6.5 45.6 %copy-start = (bf16[32,2,8,1024]{3,2,1,0:T(8,128)(2,1)S(1)}, bf16[32,2,8,1024]{3,2,1,0:T(8,128)(2,1)}, u32[]{:S(2)}) copy-start(bf16[32,2,8,1024]{3,2,1,0:T(8,128)(2,1)} %param.14) | copy-start | bytes 3145732
  6.5 9.3 %copy-start.3 = (bf16[256,512]{1,0:T(8,128)(2,1)S(1)}, bf16[256,512]{1,0:T(8,128)(2,1)}, u32[]{:S(2)}) copy-start(bf16[256,512]{1,0:T(8,128)(2,1)} %param.13) | copy-start | bytes 786436
  8.8 9.8 %copy-start.6 = (s32[1024,1]{0,1:T(1,128)S(1)}, s32[1024,1]{0,1:T(1,128)}, u32[]{:S(2)}) copy-start(s32[1024,1]{0,1:T(1,128)} %param.16) | copy-start | bytes 12292
  8.8 10.7 %copy-start.5 = (s32[1024]{0:T(1024)S(1)}, s32[1024]{0:T(1024)}, u32[]{:S(2)}) copy-start(s32[1024]{0:T(1024)} %param.17) | copy-start | bytes 12292
  8.8 35.0 %all-to-all-start = ((bf16[4,512,320]{1,2,0:T(8,128)(2,1)}), bf16[4,512,320]{1,2,0:T(8,128)(2,1)S(1)}, u32[]{:S(2)}, u32[]{:S(2)}) async-start(bf16[4,512,320]{1,2,0:T(8,128)(2,1)} %broadcast_in_dim.29), calls=%async_computation | async-start | bytes 2621440 | tf_op jit(solution)/shard_map/all_to_all | solution.py:38
  16.1 55.5 %collective-permute-start = (bf16[256,256]{0,1:T(8,128)(2,1)S(1)}, bf16[256,256]{0,1:T(8,128)(2,1)S(1)}, u32[]{:S(2)}, u32[]{:S(2)}) collective-permute-start(bf16[256,256]{0,1:T(8,128)(2,1)S(1)} %get-tuple-element.35), channel_id=1, source_target_pairs={{0,1},{1,0},{2,3},{3,2},{4,5},{5,4},{6,7},{7,6},{8,9},{9,8},{10,11... | collective-permute-start | bytes 393224 | tf_op jit(solution)/shard_map/ppermute | solution.py:81
  45.1 27.3 %collective-permute-start.1 = (bf16[2048,320]{0,1:T(8,128)(2,1)}, bf16[2048,320]{0,1:T(8,128)(2,1)}, u32[]{:S(2)}, u32[]{:S(2)}) collective-permute-start(bf16[2048,320]{0,1:T(8,128)(2,1)} %bitcast.40), channel_id=1, source_target_pairs={{0,128},{128,256},{256,384},{384,0},{1,129},{129,257},{257,385},{3... | collective-permute-start | bytes 3932168 | tf_op jit(solution)/shard_map/ppermute | solution.py:92
  48.5 23.9 %collective-permute-start.2 = (bf16[2048,320]{0,1:T(8,128)(2,1)}, bf16[2048,320]{0,1:T(8,128)(2,1)}, u32[]{:S(2)}, u32[]{:S(2)}) collective-permute-start(bf16[2048,320]{0,1:T(8,128)(2,1)} %bitcast.40), channel_id=1, source_target_pairs={{0,384},{128,0},{256,128},{384,256},{1,385},{129,1},{257,129},{385... | collective-permute-start | bytes 3932168 | tf_op jit(solution)/shard_map/ppermute | solution.py:93
  54.1 14.1 %copy-start.7 = (s32[256]{0:T(256)S(1)}, s32[256]{0:T(256)}, u32[]{:S(2)}) copy-start(s32[256]{0:T(256)} %param.15) | copy-start | bytes 3076
  54.1 64.3 %all-to-all-start.2 = ((bf16[32,2,2,8,1024]{4,3,2,1,0:T(8,128)(2,1)}), bf16[32,2,2,8,1024]{4,3,2,1,0:T(8,128)(2,1)}, u32[]{:S(2)}, u32[]{:S(2)}) async-start(bf16[32,2,2,8,1024]{4,3,2,1,0:T(8,128)(2,1)} %bitcast.115), calls=%async_computation.2 | async-start | bytes 4194304 | tf_op jit(solution)/shard_map/all_to_all | solution.py:124
  68.2 106.7 %all-gather.3.cloned.1.call-start = ((), (), s32[]{:S(2)}) async-start(), calls=%async_computation.5 | async-start | bytes 4456448 | tf_op jit(solution)/shard_map/all_gather | solution.py:95
  68.3 4.2 %copy-start.4 = (bf16[8192]{0:T(1024)(128)(2,1)S(1)}, bf16[8192]{0:T(1024)(128)(2,1)}, u32[]{:S(2)}) copy-start(bf16[8192]{0:T(1024)(128)(2,1)} %param.11) | copy-start | bytes 49156
  76.6 2.7 %copy-start.1 = (bf16[256,8192]{1,0:T(8,128)(2,1)}, bf16[256,8192]{1,0:T(8,128)(2,1)S(1)}, u32[]{:S(2)}) copy-start(bf16[256,8192]{1,0:T(8,128)(2,1)S(1)} %fusion.2) | copy-start | bytes 12582916
  81.2 20.2 %collective-permute-start.3 = (bf16[1024,320]{0,1:T(8,128)(2,1)}, bf16[1024,320]{0,1:T(8,128)(2,1)}, u32[]{:S(2)}, u32[]{:S(2)}) collective-permute-start(bf16[1024,320]{0,1:T(8,128)(2,1)} %slice.33), channel_id=1, source_target_pairs={{0,128},{128,256},{256,384},{384,0},{1,129},{129,257},{257,385},{3... | collective-permute-start | bytes 1966088 | tf_op jit(solution)/shard_map/ppermute | solution.py:98
  86.4 19.6 %collective-permute-start.4 = (bf16[1024,320]{0,1:T(8,128)(2,1)}, bf16[1024,320]{0,1:T(8,128)(2,1)}, u32[]{:S(2)}, u32[]{:S(2)}) collective-permute-start(bf16[1024,320]{0,1:T(8,128)(2,1)} %slice.34), channel_id=1, source_target_pairs={{0,384},{128,0},{256,128},{384,256},{1,385},{129,1},{257,129},{385... | collective-permute-start | bytes 1966088 | tf_op jit(solution)/shard_map/ppermute | solution.py:98
  95.4 2.6 %copy-start.2 = (bf16[32,8,2048]{2,1,0:T(8,128)(2,1)S(1)}, bf16[32,8,2048]{2,1,0:T(8,128)(2,1)}, u32[]{:S(2)}) copy-start(bf16[32,8,2048]{2,1,0:T(8,128)(2,1)} %get-tuple-element.25) | copy-start | bytes 3145732
  118.4 33.0 %all-to-all-start.1 = ((bf16[8,32,320]{2,0,1:T(8,128)(2,1)}), bf16[8,32,320]{2,0,1:T(8,128)(2,1)S(1)}, u32[]{:S(2)}, u32[]{:S(2)}) async-start(bf16[8,32,320]{2,0,1:T(8,128)(2,1)} %fusion.27), calls=%async_computation.1 | async-start | bytes 393216 | tf_op jit(solution)/shard_map/all_to_all | solution.py:33
Sparse Core Ops, SparseCore 0:
  72.5 92.5 all-gather.2

commit v14 on v6

--- a/solution.py
+++ b/solution.py
@@ -158,7 +158,11 @@
         partial = term if partial is None else partial + term
     partial = partial.astype(jnp.bfloat16).reshape(grouped_row_block, pairs, block)
     spread = lax.all_to_all(partial.transpose(1, 0, 2), PAIR, 0, 0, tiled=True)
-    return jnp.sum(spread.astype(jnp.float32), axis=0).astype(jnp.bfloat16)
+    total = spread.astype(jnp.float32)
+    while total.shape[0] > 1:
+        count = total.shape[0] // 2
+        total = total[:count] + total[count:]
+    return total[0].astype(jnp.bfloat16)
 
 
 def solution(mesh):

time: 248 us -> 246 us (level)
    reduce_sum x1 -> x0, other arithmetic: 2.57 us -> none  [shards(): return jnp.sum(spread.astype(jnp.float32), axis=0).astype(jnp.bfloat16)]
where the time goes in v14:
time: 246 us; the launch traced here: 244 us
  blocking collectives  75.7 us (31%)
  waiting for transfers between devices  52.4 us (21%)
  starting transfers between devices  52 us (21%)
  local copies, waits for them, and re-layouts  25.7 us (10%)
  between operations  13.9 us (6%)
  matrix products  12.8 us (5%)
  other arithmetic  11.4 us (5%)
    all_to_all x1, blocking collectives, shards(): spread = lax.all_to_all(partial.transpose(1, 0, 2), PAIR, 0, 0, tiled=True)  55 us
    all_to_all x1, waiting for transfers between devices, gather_rows(): lax.all_to_all(copies, axis, 0, 0, tiled=True)  23.9 us
    all_to_all x1, blocking collectives, shards(): lax.all_to_all(doubled.reshape(own_beams, columns, pair_feats.shape[3]),...  20.7 us
    all_to_all x1, waiting for transfers between devices, regroup(): return lax.all_to_all(blocks, BEAM, split_axis=1, concat_axis=1, tiled=True)  15.5 us
    all_to_all x1, starting transfers between devices, regroup(): return lax.all_to_all(blocks, BEAM, split_axis=1, concat_axis=1, tiled=True)  14.9 us
    all_to_all x1, starting transfers between devices, shards(): lax.all_to_all(outgoing, BEAM, split_axis=0, concat_axis=0, tiled=True)  13.9 us
    dot_general x4, matrix products, shards(): jnp.einsum('jbd,dc->bjc', block.reshape(columns, own_beams, rows), piece,...  10.1 us
    all_to_all x1, waiting for transfers between devices, shards(): lax.all_to_all(outgoing, BEAM, split_axis=0, concat_axis=0, tiled=True)  7.21 us
  transfers between devices with their start and end apart: 9, of which 5 were waited for; matrix products, arithmetic and copies ran while one was open for 16% of the time, Pallas kernels for 0%

profile of v14, /device:TPU:56, one launch (start us, length us, event | category | flops | bytes accessed | tf_op | source)
XLA Modules:
  0.0 243.9 jit_solution(11373319049798341922)
XLA Ops:
  6.5 2.3 broadcast_in_dim.29
  8.8 7.1 %all-to-all-start = ((bf16[4,512,320]{1,2,0:T(8,128)(2,1)}), bf16[4,512,320]{1,2,0:T(8,128)(2,1)S(1)}, u32[]{:S(2)}, u32[]{:S(2)}) async-start(bf16[4,512,320]{1,2,0:T(8,128)(2,1)} %broadcast_in_dim.29), calls=%async_computation | async-start | bytes 2621440 | tf_op jit(solution)/shard_map/all_to_all | solution.py:38
  15.9 0.1 copy.71
  16.1 1.9 collective-permute-start
  18.0 0.5 broadcast.199
  18.6 0.7 reduce.3
  19.3 0.2 reduce_window_sum.22
  19.6 0.1 multiply_reduce_fusion
  19.7 0.1 copy.84
  19.8 0.1 reshape.238
  19.9 23.9 %all-to-all-done = bf16[4,512,320]{1,2,0:T(8,128)(2,1)S(1)} async-done(((bf16[4,512,320]{1,2,0:T(8,128)(2,1)}), bf16[4,512,320]{1,2,0:T(8,128)(2,1)S(1)}, u32[]{:S(2)}, u32[]{:S(2)}) %all-to-all-start) | async-done | bytes 1310752 | tf_op jit(solution)/shard_map/all_to_all | solution.py:38
  43.9 1.3 copy.108
  45.1 3.4 %collective-permute-start.1 = (bf16[2048,320]{0,1:T(8,128)(2,1)}, bf16[2048,320]{0,1:T(8,128)(2,1)}, u32[]{:S(2)}, u32[]{:S(2)}) collective-permute-start(bf16[2048,320]{0,1:T(8,128)(2,1)} %bitcast.53), channel_id=1, source_target_pairs={{0,128},{128,256},{256,384},{384,0},{1,129},{129,257},{257,385},{3... | collective-permute-start | bytes 3932168 | tf_op jit(solution)/shard_map/ppermute | solution.py:92
  48.5 3.7 %collective-permute-start.2 = (bf16[2048,320]{0,1:T(8,128)(2,1)}, bf16[2048,320]{0,1:T(8,128)(2,1)}, u32[]{:S(2)}, u32[]{:S(2)}) collective-permute-start(bf16[2048,320]{0,1:T(8,128)(2,1)} %bitcast.53), channel_id=1, source_target_pairs={{0,384},{128,0},{256,128},{384,256},{1,385},{129,1},{257,129},{385... | collective-permute-start | bytes 3932168 | tf_op jit(solution)/shard_map/ppermute | solution.py:93
  52.2 2.0 gather_fusion
  54.2 13.9 %all-to-all-start.2 = ((bf16[32,2,2,8,1024]{4,3,2,1,0:T(8,128)(2,1)}), bf16[32,2,2,8,1024]{4,3,2,1,0:T(8,128)(2,1)}, u32[]{:S(2)}, u32[]{:S(2)}) async-start(bf16[32,2,2,8,1024]{4,3,2,1,0:T(8,128)(2,1)} %bitcast.130), calls=%async_computation.2 | async-start | bytes 4194304 | tf_op jit(solution)/shard_map/all_to_all | solution.py:124
  68.3 3.1 %fusion = f32[256]{0:T(256)S(1)} fusion(bf16[256,8192]{1,0:T(8,128)(2,1)} %param.10), kind=kLoop, calls=%fused_computation.4 | loop fusion | flops 6291200 | bytes 4195328 | tf_op jit(solution)/shard_map/reduce_sum | solution.py:84
  71.4 0.1 fusion.53
  71.5 0.8 maximum_select_fusion
  72.4 0.1 iota_compare_fusion.2
  72.6 0.2 select_reduce_fusion
  72.8 0.1 multiply_cosine_fusion
  72.9 3.6 %fusion.2 = bf16[256,8192]{1,0:T(8,128)(2,1)S(1)} fusion(bf16[256,8192]{1,0:T(8,128)(2,1)} %param.10, f32[8192]{0:T(1024)S(1)} %convert_element_type.107, f32[256]{0:T(256)S(1)} %add_rsqrt_fusion), kind=kLoop, calls=%fused_computation.6 | loop fusion | flops 8388608 | bytes 8422400 | tf_op jit(solution)/shard_map/convert_element_type | solution.py:85
  76.5 1.9 dynamic-slice_bitcast_fusion.2
  78.4 0.7 copy-done.1
  79.1 2.0 slice.70
  81.1 3.3 %collective-permute-start.3 = (bf16[1024,320]{0,1:T(8,128)(2,1)}, bf16[1024,320]{0,1:T(8,128)(2,1)}, u32[]{:S(2)}, u32[]{:S(2)}) collective-permute-start(bf16[1024,320]{0,1:T(8,128)(2,1)} %slice.70), channel_id=1, source_target_pairs={{0,128},{128,256},{256,384},{384,0},{1,129},{129,257},{257,385},{3... | collective-permute-start | bytes 1966088 | tf_op jit(solution)/shard_map/ppermute | solution.py:98
  84.4 2.0 slice.71
  86.3 3.8 %collective-permute-start.4 = (bf16[1024,320]{0,1:T(8,128)(2,1)}, bf16[1024,320]{0,1:T(8,128)(2,1)}, u32[]{:S(2)}, u32[]{:S(2)}) collective-permute-start(bf16[1024,320]{0,1:T(8,128)(2,1)} %slice.71), channel_id=1, source_target_pairs={{0,384},{128,0},{256,128},{384,256},{1,385},{129,1},{257,129},{385... | collective-permute-start | bytes 1966088 | tf_op jit(solution)/shard_map/ppermute | solution.py:98
  90.1 2.1 copy.74
  92.2 3.0 %reshape.323 = bf16[2048,320,1]{0,1,2:T(8,128)(2,1)S(1)} reshape(bf16[4,512,320]{1,0,2:T(4,128)(2,1)} %copy.74) | data formatting | bytes 2621440 | tf_op jit(solution)/shard_map/reshape | solution.py:38
  95.3 2.6 %fusion.7 = f32[320,32,8]{0,1,2:T(8,128)S(1)} fusion(bf16[2048,320]{0,1:T(8,128)(2,1)} %collective-permute-done.1, bf16[32,8,2048]{2,1,0:T(8,128)(2,1)} %get-tuple-element.29), kind=kOutput, calls=%fused_computation.14 | convolution fusion | flops 335544320 | bytes 2686976 | tf_op jit(solution)/shard_map/jbd,dc->bjc/dot_general | solution.py:106
  97.9 2.2 fusion.9
  100.1 1.1 collective-permute-done.3
  101.3 4.5 %collective-permute-done.4 = bf16[1024,320]{0,1:T(8,128)(2,1)} collective-permute-done((bf16[1024,320]{0,1:T(8,128)(2,1)}, bf16[1024,320]{0,1:T(8,128)(2,1)}, u32[]{:S(2)}, u32[]{:S(2)}) %collective-permute-start.4) | collective-permute-done | bytes 655392 | tf_op jit(solution)/shard_map/ppermute | solution.py:98
  105.8 2.2 fusion.4
  108.0 3.1 %fusion.24 = bf16[8,32,320]{2,0,1:T(8,128)(2,1)} fusion(f32[320,32,8]{0,1,2:T(8,128)S(1)} %fusion.4, f32[320,32,8]{0,1,2:T(8,128)S(1)} %fusion.7, bf16[2048,320,1]{0,1,2:T(8,128)(2,1)S(1)} %reshape.323, bf16[256,8192]{1,0:T(8,128)(2,1)} %copy-done.1, s32[]{:T(128)S(6)} %select_n.83, f32[320,32,8]{0,1,2:T(8,128)S(1)} %fusion.9), kind=kOutput, calls=%fused_computation.40 | convolution fusion | flops 335872000 | bytes 3506180 | tf_op jit(solution)/shard_map/jbd,dc->bjc/dot_general | solution.py:106
  111.2 7.2 %all-to-all-done.2 = bf16[32,2,2,8,1024]{4,3,2,1,0:T(8,128)(2,1)} async-done(((bf16[32,2,2,8,1024]{4,3,2,1,0:T(8,128)(2,1)}), bf16[32,2,2,8,1024]{4,3,2,1,0:T(8,128)(2,1)}, u32[]{:S(2)}, u32[]{:S(2)}) %all-to-all-start.2) | async-done | bytes 2097184 | tf_op jit(solution)/shard_map/all_to_all | solution.py:124
  118.4 14.9 %all-to-all-start.1 = ((bf16[8,32,320]{2,0,1:T(8,128)(2,1)}), bf16[8,32,320]{2,0,1:T(8,128)(2,1)S(1)}, u32[]{:S(2)}, u32[]{:S(2)}) async-start(bf16[8,32,320]{2,0,1:T(8,128)(2,1)} %fusion.24), calls=%async_computation.1 | async-start | bytes 393216 | tf_op jit(solution)/shard_map/all_to_all | solution.py:33
  133.3 2.2 gather_fusion.1
  135.5 0.3 copy.109
  135.9 15.5 %all-to-all-done.1 = bf16[8,32,320]{2,0,1:T(8,128)(2,1)S(1)} async-done(((bf16[8,32,320]{2,0,1:T(8,128)(2,1)}), bf16[8,32,320]{2,0,1:T(8,128)(2,1)S(1)}, u32[]{:S(2)}, u32[]{:S(2)}) %all-to-all-start.1) | async-done | bytes 163872 | tf_op jit(solution)/shard_map/all_to_all | solution.py:33
  151.4 0.2 reshape.236
  151.6 0.1 subtract_convert_fusion.1
  151.7 0.1 maximum_bitcast_fusion.2
  151.8 0.1 fusion.57
  152.0 0.1 fusion.29
  152.1 0.3 fusion.38
  152.4 0.5 fusion.58
  152.9 0.3 fusion.28
  153.2 0.3 fusion.14
  153.5 0.1 convert_element_type.123
  153.6 0.1 copy.88
  153.8 20.7 %all_to_all.25 = bf16[8,32,512]{2,0,1:T(8,128)(2,1)S(1)} all-to-all(bf16[8,32,512]{2,0,1:T(8,128)(2,1)S(1)} %bitcast.137), channel_id=1, replica_groups=mesh['x'=4,'yh'=4,'yl'=2,'z'=8,'c'=2] {'yl','z','c'}, dimensions={1} | all-to-all | bytes 524288 | tf_op jit(solution)/shard_map/all_to_all | solution.py:146
  174.5 2.5 %fusion.54 = (bf16[256,4096]{0,1:T(8,128)(2,1)S(1)}, bf16[256,4096]{0,1:T(8,128)(2,1)S(1)}) fusion(bf16[512,4096]{0,1:T(8,128)(2,1)} %all-gather.3.cloned.1.call-done), kind=kLoop, calls=%fused_computation.105 | loop fusion | bytes 8388608 | tf_op jit(solution)/shard_map/slice | solution.py:155
  177.0 0.7 fusion.33
  177.8 0.7 fusion.3
  178.5 1.2 copy.93
  179.7 0.7 copy.94
  180.4 55.0 %all_to_all.26 = bf16[16,256,256]{2,1,0:T(8,128)(2,1)S(1)} all-to-all(bf16[16,256,256]{2,1,0:T(8,128)(2,1)S(1)} %copy.94), channel_id=1, replica_groups=mesh['x'=4,'yh'=4,'yl'=2,'z'=8,'c'=2] {'yl','z'}, dimensions={0} | all-to-all | bytes 4194304 | tf_op jit(solution)/shard_map/all_to_all | solution.py:160
  235.5 0.4 convert_element_type.130
  235.9 0.3 slice_add_fusion
  236.2 0.1 slice_add_fusion.1
  236.4 0.7 fusion.31
  (46 shorter events, 0.8 us)
Async XLA Ops:
  6.5 45.7 %copy-start = (bf16[32,2,8,1024]{3,2,1,0:T(8,128)(2,1)S(1)}, bf16[32,2,8,1024]{3,2,1,0:T(8,128)(2,1)}, u32[]{:S(2)}) copy-start(bf16[32,2,8,1024]{3,2,1,0:T(8,128)(2,1)} %param.14) | copy-start | bytes 3145732
  6.5 9.4 %copy-start.3 = (bf16[256,512]{1,0:T(8,128)(2,1)S(1)}, bf16[256,512]{1,0:T(8,128)(2,1)}, u32[]{:S(2)}) copy-start(bf16[256,512]{1,0:T(8,128)(2,1)} %param.13) | copy-start | bytes 786436
  8.8 9.8 %copy-start.6 = (s32[1024,1]{0,1:T(1,128)S(1)}, s32[1024,1]{0,1:T(1,128)}, u32[]{:S(2)}) copy-start(s32[1024,1]{0,1:T(1,128)} %param.16) | copy-start | bytes 12292
  8.8 10.7 %copy-start.5 = (s32[1024]{0:T(1024)S(1)}, s32[1024]{0:T(1024)}, u32[]{:S(2)}) copy-start(s32[1024]{0:T(1024)} %param.17) | copy-start | bytes 12292
  8.8 35.0 %all-to-all-start = ((bf16[4,512,320]{1,2,0:T(8,128)(2,1)}), bf16[4,512,320]{1,2,0:T(8,128)(2,1)S(1)}, u32[]{:S(2)}, u32[]{:S(2)}) async-start(bf16[4,512,320]{1,2,0:T(8,128)(2,1)} %broadcast_in_dim.29), calls=%async_computation | async-start | bytes 2621440 | tf_op jit(solution)/shard_map/all_to_all | solution.py:38
  16.1 55.4 %collective-permute-start = (bf16[256,256]{0,1:T(8,128)(2,1)S(1)}, bf16[256,256]{0,1:T(8,128)(2,1)S(1)}, u32[]{:S(2)}, u32[]{:S(2)}) collective-permute-start(bf16[256,256]{0,1:T(8,128)(2,1)S(1)} %get-tuple-element.39), channel_id=1, source_target_pairs={{0,1},{1,0},{2,3},{3,2},{4,5},{5,4},{6,7},{7,6},{8,9},{9,8},{10,11... | collective-permute-start | bytes 393224 | tf_op jit(solution)/shard_map/ppermute | solution.py:81
  45.1 27.2 %collective-permute-start.1 = (bf16[2048,320]{0,1:T(8,128)(2,1)}, bf16[2048,320]{0,1:T(8,128)(2,1)}, u32[]{:S(2)}, u32[]{:S(2)}) collective-permute-start(bf16[2048,320]{0,1:T(8,128)(2,1)} %bitcast.53), channel_id=1, source_target_pairs={{0,128},{128,256},{256,384},{384,0},{1,129},{129,257},{257,385},{3... | collective-permute-start | bytes 3932168 | tf_op jit(solution)/shard_map/ppermute | solution.py:92
  48.5 23.8 %collective-permute-start.2 = (bf16[2048,320]{0,1:T(8,128)(2,1)}, bf16[2048,320]{0,1:T(8,128)(2,1)}, u32[]{:S(2)}, u32[]{:S(2)}) collective-permute-start(bf16[2048,320]{0,1:T(8,128)(2,1)} %bitcast.53), channel_id=1, source_target_pairs={{0,384},{128,0},{256,128},{384,256},{1,385},{129,1},{257,129},{385... | collective-permute-start | bytes 3932168 | tf_op jit(solution)/shard_map/ppermute | solution.py:93
  54.2 64.1 %all-to-all-start.2 = ((bf16[32,2,2,8,1024]{4,3,2,1,0:T(8,128)(2,1)}), bf16[32,2,2,8,1024]{4,3,2,1,0:T(8,128)(2,1)}, u32[]{:S(2)}, u32[]{:S(2)}) async-start(bf16[32,2,2,8,1024]{4,3,2,1,0:T(8,128)(2,1)} %bitcast.130), calls=%async_computation.2 | async-start | bytes 4194304 | tf_op jit(solution)/shard_map/all_to_all | solution.py:124
  68.1 106.4 %all-gather.3.cloned.1.call-start = ((), (), s32[]{:S(2)}) async-start(), calls=%async_computation.5 | async-start | bytes 4456448 | tf_op jit(solution)/shard_map/all_gather | solution.py:95
  68.3 3.2 %copy-start.7 = (s32[256]{0:T(256)S(1)}, s32[256]{0:T(256)}, u32[]{:S(2)}) copy-start(s32[256]{0:T(256)} %param.15) | copy-start | bytes 3076
  68.3 4.2 %copy-start.4 = (bf16[8192]{0:T(1024)(128)(2,1)S(1)}, bf16[8192]{0:T(1024)(128)(2,1)}, u32[]{:S(2)}) copy-start(bf16[8192]{0:T(1024)(128)(2,1)} %param.11) | copy-start | bytes 49156
  76.5 2.6 %copy-start.1 = (bf16[256,8192]{1,0:T(8,128)(2,1)}, bf16[256,8192]{1,0:T(8,128)(2,1)S(1)}, u32[]{:S(2)}) copy-start(bf16[256,8192]{1,0:T(8,128)(2,1)S(1)} %fusion.2) | copy-start | bytes 12582916
  81.1 20.2 %collective-permute-start.3 = (bf16[1024,320]{0,1:T(8,128)(2,1)}, bf16[1024,320]{0,1:T(8,128)(2,1)}, u32[]{:S(2)}, u32[]{:S(2)}) collective-permute-start(bf16[1024,320]{0,1:T(8,128)(2,1)} %slice.70), channel_id=1, source_target_pairs={{0,128},{128,256},{256,384},{384,0},{1,129},{129,257},{257,385},{3... | collective-permute-start | bytes 1966088 | tf_op jit(solution)/shard_map/ppermute | solution.py:98
  86.3 19.5 %collective-permute-start.4 = (bf16[1024,320]{0,1:T(8,128)(2,1)}, bf16[1024,320]{0,1:T(8,128)(2,1)}, u32[]{:S(2)}, u32[]{:S(2)}) collective-permute-start(bf16[1024,320]{0,1:T(8,128)(2,1)} %slice.71), channel_id=1, source_target_pairs={{0,384},{128,0},{256,128},{384,256},{1,385},{129,1},{257,129},{385... | collective-permute-start | bytes 1966088 | tf_op jit(solution)/shard_map/ppermute | solution.py:98
  95.3 2.6 %copy-start.2 = (bf16[32,8,2048]{2,1,0:T(8,128)(2,1)S(1)}, bf16[32,8,2048]{2,1,0:T(8,128)(2,1)}, u32[]{:S(2)}) copy-start(bf16[32,8,2048]{2,1,0:T(8,128)(2,1)} %get-tuple-element.27) | copy-start | bytes 3145732
  118.4 33.0 %all-to-all-start.1 = ((bf16[8,32,320]{2,0,1:T(8,128)(2,1)}), bf16[8,32,320]{2,0,1:T(8,128)(2,1)S(1)}, u32[]{:S(2)}, u32[]{:S(2)}) async-start(bf16[8,32,320]{2,0,1:T(8,128)(2,1)} %fusion.24), calls=%async_computation.1 | async-start | bytes 393216 | tf_op jit(solution)/shard_map/all_to_all | solution.py:33
Sparse Core Ops, SparseCore 0:
  72.5 92.8 all-gather.2
